TPU v7x, 256 devices: a whole 4x4x8 slice. The times are simulated.
256 devices in a mesh: pair: 32 (over z, x_lo, core), grp: 8 (over y, x_hi).
Axes of the slice: x: 4 (x_hi: 2, x_lo: 2; x = x_hi * 2 + x_lo), y: 4, z: 8, core: 2. Of those that a mesh axis runs over, the one named last changes fastest.
Arguments:
- amplitudes: float32 [8, 224, 2048], P('grp', 'pair'), may hold values from -6 to 6
- integrals: float32 [2048, 65536], P('grp', 'pair'), may hold values from -0.375 to 0.375
- owner_blocks: int32 [16], replicated, may hold values from 0 to 15, each once
- occ_pairs: int32 [8, 2, 224], P('grp'), may hold values from 0 to 63, as said below
- vir_pairs: int32 [2, 65536], replicated, may hold values from 0 to 511, as said below
- occ_energy: float32 [64], replicated, may hold values from -1.5 to -0.5
- vir_energy: float32 [512], replicated, may hold values from 0.2 to 1.5
Outputs:
- ladder: float32 [8, 224, 65536], P('grp', 'pair')
Inputs may be any that keep to these rules, and one draw needn't show every extreme that they name: `occ_pairs`: each column is a pair i<j; no pair occurs twice. `vir_pairs`: each column is a pair a<b; no pair occurs twice. `owner_blocks`: a permutation.
All inputs are finite; a program needn't handle non-finite values.
Results may differ from a plain program's by a relative error of at most 0.000071.
Values sent between devices are 32-bit elements; how exact they have to be, the bound alone decides.
No kernel may reach another device: no remote copies, remote signals or barrier semaphores. Data moves between devices by JAX's collectives and lax.ppermute only.
A program may use at most 64 MiB of HBM per device.

v0:
```python
import jax
import jax.numpy as jnp
from jax import lax
from jax.sharding import PartitionSpec as P


def pair_energies(energy, pairs):
    return jnp.take(energy, pairs[0]) + jnp.take(energy, pairs[1])


def on_device(amplitudes, integrals, owner_blocks, occ_pairs, vir_pairs, occ_energy, vir_energy):
    block = integrals.shape[0]
    columns = integrals.shape[1]
    groups = lax.axis_size("grp")
    nblocks = owner_blocks.shape[0]
    sub_width = block * groups // nblocks
    group_rows = lax.all_gather(amplitudes, "pair", axis=1, tiled=True)[0]
    piece = lax.all_gather(integrals, "grp", axis=0, tiled=True)
    count = piece.shape[0]
    rows = jnp.arange(count, dtype=jnp.int32)
    owner = jnp.take(owner_blocks, rows // sub_width)
    picked = owner * sub_width + rows % sub_width
    chosen = jnp.take(group_rows, picked, axis=1)
    work = jnp.dot(
        chosen, piece, precision=lax.Precision.HIGHEST, preferred_element_type=jnp.float32
    )
    occ_sum = pair_energies(occ_energy, occ_pairs[0])
    vir_local = lax.dynamic_slice_in_dim(vir_pairs, lax.axis_index("pair") * columns, columns, 1)
    vir_sum = pair_energies(vir_energy, vir_local)
    payload = work / (occ_sum[:, None] - vir_sum[None, :])
    return lax.all_to_all(payload[None], "pair", split_axis=1, concat_axis=2, tiled=True)


def solution(mesh):
    return jax.shard_map(
        on_device,
        mesh=mesh,
        in_specs=(
            P("grp", "pair", None),
            P("grp", "pair"),
            P(),
            P("grp", None, None),
            P(),
            P(),
            P(),
        ),
        out_specs=P("grp", "pair", None),
        check_vma=False,
    )
```

profile of v0, /device:TPU:1, one launch (start us, length us, event | category | flops | bytes accessed | tf_op | source)
XLA Modules:
  0.0 351.4 jit_solution(17929817763536348124)
XLA Ops:
  6.5 0.0 copy-start
  6.5 0.0 all-gather.3.cloned.1.call-start
  6.5 0.7 all-gather.3.cloned.1.call-update
  7.3 0.0 all-gather.5.cloned.1.call-start
  7.3 0.7 all-gather.5.cloned.1.call-update
  8.0 0.9 constant_dynamic-slice_fusion
  8.9 0.0 copy-done
  8.9 13.2 %gather_fusion.3 = f32[2048]{0:T(1024)S(1)} fusion(f32[512]{0:T(512)S(1)} %copy-done, s32[2048]{0:T(1024)S(1)} %fusion.16), kind=kCustom, calls=%fused_computation.1.clone | custom fusion | bytes 24576 | tf_op jit(solution)/shard_map/jit(_take)/gather | solution.py:8
  22.1 0.0 copy-start.3
  22.1 0.0 copy-start.1
  22.1 13.2 %gather_fusion.4 = f32[2048]{0:T(1024)S(1)} fusion(f32[512]{0:T(512)S(1)} %copy-done, s32[2048]{0:T(1024)S(1)} %fusion.17), kind=kCustom, calls=%fused_computation.3.clone | custom fusion | bytes 24576 | tf_op jit(solution)/shard_map/jit(_take)/gather | solution.py:8
  35.3 0.0 copy-done.3
  35.4 0.0 copy-start.2
  35.4 0.0 copy-done.1
  35.4 1.9 gather_fusion.1
  37.3 1.9 gather_fusion.2
  39.6 0.0 copy-done.2
  39.6 0.7 fusion.21
  40.3 4.4 %compare_select_fusion.2 = s32[2048,1]{0,1:T(1,128)S(1)} fusion(s32[]{:T(128)} %bitcast.9, s32[]{:T(128)} %bitcast.10, s32[]{:T(128)} %bitcast.11, s32[]{:T(128)} %bitcast.12, s32[]{:T(128)} %bitcast.13, s32[]{:T(128)} %bitcast.15, s32[]{:T(128)} %bitcast.14), kind=kLoop, calls=%fused_computation.21 | loop fusion | flops 47104 | bytes 8220 | tf_op jit(solution)/shard_map/jit(_take)/gather | solution.py:21
  44.8 5.7 %compare_and_fusion = (pred[2048]{0:T(1024)(128)(4,1)S(1)}, s32[2048]{0:T(1024)S(1)}) fusion(pred[2048]{0:T(1024)(128)(4,1)S(1)} %compare_reduce_fusion, pred[2048]{0:T(1024)(128)(4,1)S(1)} %compare_reduce_fusion.1, pred[2048]{0:T(1024)(128)(4,1)S(1)} %compare_reduce_fusion.2, pred[2048]{0:T(1024)(128)(4,1)S(1)} %compare_reduce_fusion.3, ...), kind=kLoop, calls=%fused_computation.55 | loop fusion | flops 73728 | bytes 36900 | tf_op jit(solution)/shard_map/jit(_take)/and | solution.py:23
  50.5 27.1 %all-gather.3.cloned.1.call-done = f32[1,224,2048]{2,0,1:T(1,128)} async-done(((f32[1,7,2048]{2,0,1:T(1,128)}), f32[1,224,2048]{2,0,1:T(1,128)}) %all-gather.3.cloned.1.call-update) | async-done | bytes 1835024 | tf_op jit(solution)/shard_map/all_gather | solution.py:17
  77.6 4.1 %copy.13 = f32[1,224,2048]{1,2,0:T(8,128)S(1)} copy(f32[1,224,2048]{2,0,1:T(1,128)} %all-gather.3.cloned.1.call-done) | data formatting | bytes 3670016 | tf_op jit(solution)/shard_map/all_gather | solution.py:17
  81.6 8.6 %gather_fusion = f32[2048,224]{1,0:T(8,128)} fusion(f32[224,2048]{0,1:T(8,128)S(1)} %bitcast.32, s32[2048]{0:T(1024)S(1)} %broadcast_clamp_fusion), kind=kCustom, calls=%fused_computation.4 | custom fusion | bytes 3678208 | tf_op jit(solution)/shard_map/jit(_take)/gather | solution.py:23
  90.2 175.9 %all-gather.5.cloned.1.call-done = f32[2048,2048]{1,0:T(8,128)} async-done(((f32[256,2048]{1,0:T(8,128)}), f32[2048,2048]{1,0:T(8,128)}) %all-gather.5.cloned.1.call-update) | async-done | bytes 16777232 | tf_op jit(solution)/shard_map/all_gather | solution.py:18
  266.1 20.5 %fusion = f32[1,224,2048]{2,1,0:T(8,128)S(1)} fusion(f32[2048,2048]{1,0:T(8,128)} %all-gather.5.cloned.1.call-done, f32[2048,224]{1,0:T(8,128)} %gather_fusion, pred[2048]{0:T(1024)(128)(4,1)S(1)} %get-tuple-element.6, f32[2048]{0:T(1024)S(1)} %select_add_fusion, f32[224]{0:T(256)S(1)} %fusion.18), kind=kOutput, calls=%fused_computation.6 | convolution fusion | flops 11275665408 | bytes 20458368 | tf_op jit(solution)/shard_map/dot_general | solution.py:24
  286.6 1.9 copy.14
  288.5 53.5 %all_to_all.18 = f32[1,224,2048]{2,0,1:T(1,128)S(1)} all-to-all(f32[1,224,2048]{2,0,1:T(1,128)S(1)} %copy.14), channel_id=1, replica_groups=mesh['pair'=32,'grp'=8] {'pair'}, dimensions={1} | all-to-all | bytes 3670016 | tf_op jit(solution)/shard_map/all_to_all | solution.py:31
  342.0 2.6 copy.16
  (20 shorter events, 0.5 us)
Async XLA Ops:
  6.5 2.4 copy-start
  6.5 71.0 %all-gather.3.cloned.1.call-start = ((), (), s32[]{:S(2)}) async-start(), calls=%async_computation.1 | async-start | bytes 1892352 | tf_op jit(solution)/shard_map/all_gather | solution.py:17
  7.3 258.8 %all-gather.5.cloned.1.call-start = ((), (), s32[]{:S(2)}) async-start(), calls=%async_computation.2 | async-start | bytes 18874368 | tf_op jit(solution)/shard_map/all_gather | solution.py:18
  22.1 13.2 %copy-start.3 = (s32[1,2,224]{2,1,0:T(2,128)S(1)}, s32[1,2,224]{2,1,0:T(2,128)}, u32[]{:S(2)}) copy-start(s32[1,2,224]{2,1,0:T(2,128)} %param.14) | copy-start | bytes 5380
  22.1 13.3 %copy-start.1 = (f32[64]{0:T(128)S(1)}, f32[64]{0:T(128)}, u32[]{:S(2)}) copy-start(f32[64]{0:T(128)} %param.16) | copy-start | bytes 772
  35.4 4.2 %copy-start.2 = (s32[16]{0:T(128)S(1)}, s32[16]{0:T(128)}, u32[]{:S(2)}) copy-start(s32[16]{0:T(128)} %param.13) | copy-start | bytes 196
Sparse Core Ops, SparseCore 0:
  9.2 68.3 all-gather.2
  80.2 185.8 all-gather.4
where the time goes:
time: 352 us; the launch traced here: 351 us
  waiting for transfers between devices  204 us (58%)
  blocking collectives  53.5 us (15%)
  local copies, waits for them, and re-layouts  48.8 us (14%)
  matrix products  20.5 us (6%)
  between operations  13.6 us (4%)
  other arithmetic  10.5 us (3%)
    all_gather x1, waiting for transfers between devices, on_device(): piece = lax.all_gather(integrals, 'grp', axis=0, tiled=True)  176 us
    all_to_all x1, blocking collectives, on_device(): lax.all_to_all(payload[None], 'pair', split_axis=1, concat_axis=2, tiled=...  53.5 us
    gather x4, local copies, waits for them, and re-layouts, pair_energies(): return jnp.take(energy, pairs[0]) + jnp.take(energy, pairs[1])  30.1 us
    all_gather x1, waiting for transfers between devices, on_device(): group_rows = lax.all_gather(amplitudes, 'pair', axis=1, tiled=True)[0]  27.1 us
    dot_general x1, matrix products, on_device(): jnp.dot(chosen, piece, precision=lax.Precision.HIGHEST, preferred_element...  20.5 us
    gather x1, local copies, waits for them, and re-layouts, on_device(): chosen = jnp.take(group_rows, picked, axis=1)  8.56 us
  transfers between devices with their start and end apart: 2, of which 2 were waited for; matrix products, arithmetic and copies ran while one was open for 16% of the time, Pallas kernels for 0%

commit v1 on v0

v1 whole, which is shorter than its diff:
```python
import jax
import jax.numpy as jnp
import numpy as np
from jax import lax
from jax.sharding import Mesh, PartitionSpec as P

N_CHUNK = 4


def pair_energies(energy, pairs):
    return jnp.take(energy, pairs[0]) + jnp.take(energy, pairs[1])


def on_device(amplitudes, integrals, owner_blocks, occ_pairs, vir_pairs, occ_energy, vir_energy):
    rows_l = amplitudes.shape[1]
    width = amplitudes.shape[2]
    block = integrals.shape[0]
    columns = integrals.shape[1]
    nblocks = owner_blocks.shape[0]
    sub = width // nblocks
    per_block = block // sub
    ny = lax.axis_size("gy")
    nx = lax.axis_size("gx")
    npair = lax.axis_size("pair")
    gx = lax.axis_index("gx")
    p = lax.axis_index("pair")

    def half_blocks(x):
        m = jnp.arange(ny * per_block, dtype=jnp.int32)
        b = ((m // per_block) * nx + x) * per_block + m % per_block
        return jnp.take(owner_blocks, b)

    tau = amplitudes[0].reshape(rows_l, nblocks, sub)

    def select(x):
        return jnp.take(tau, half_blocks(x), axis=1).reshape(rows_l, -1)

    mine = select(gx)
    other = select(1 - gx)
    swap = [(0, 1), (1, 0)]
    got = lax.ppermute(other, "gx", swap)
    both = jnp.where(gx == 0, jnp.stack([mine, got]), jnp.stack([got, mine]))
    spread = jnp.broadcast_to(both[None], (npair,) + both.shape)
    t_all = lax.all_to_all(spread, "pair", 0, 0, tiled=True)
    lhs = t_all.reshape(npair * nx * rows_l, -1)

    occ_sum = pair_energies(occ_energy, occ_pairs[0]).reshape(npair, rows_l)
    vir_local = lax.dynamic_slice_in_dim(vir_pairs, p * columns, columns, 1)
    vir_sum = pair_energies(vir_energy, vir_local)

    w = columns // N_CHUNK
    outs = []
    for c in range(N_CHUNK):
        piece = lax.all_gather(integrals[:, c * w:(c + 1) * w], "gy", axis=0, tiled=True)
        part = jnp.dot(lhs, piece, precision=lax.Precision.HIGHEST, preferred_element_type=jnp.float32)
        part = part.reshape(npair, nx, rows_l, w)
        keep = lax.dynamic_index_in_dim(part, gx, 1, keepdims=False)
        send = lax.dynamic_index_in_dim(part, 1 - gx, 1, keepdims=False)
        work = keep + lax.ppermute(send, "gx", swap)
        payload = work / (occ_sum[:, :, None] - vir_sum[None, None, c * w:(c + 1) * w])
        outs.append(lax.all_to_all(payload, "pair", 0, 0, tiled=True))
    res = jnp.stack(outs, axis=2)
    res = jnp.transpose(res, (1, 0, 2, 3)).reshape(1, rows_l, npair * columns)
    return res


def solution(mesh):
    devs = np.asarray(mesh.devices)
    npair, ngrp = devs.shape
    nx = 2
    sub_mesh = Mesh(devs.reshape(npair, ngrp // nx, nx), ("pair", "gy", "gx"))
    g = ("gy", "gx")
    return jax.shard_map(
        on_device,
        mesh=sub_mesh,
        in_specs=(
            P(g, "pair", None),
            P(g, "pair"),
            P(),
            P(g, None, None),
            P(),
            P(),
            P(),
        ),
        out_specs=P(g, "pair", None),
        check_vma=False,
    )
```

time: 352 us -> 310 us (0.88)
  waiting for transfers between devices: 204 us -> 156 us
  starting transfers between devices: 0.04 us -> 40.9 us
  blocking collectives: 53.5 us -> 20.6 us
  other arithmetic: 10.5 us -> 3.5 us
  local copies, waits for them, and re-layouts: 48.8 us -> 53.5 us
    all_gather x2 -> x4, waiting for transfers between devices: 203 us -> 67.1 us  [on_device(): lax.all_gather(integrals[:, c * w:(c + 1) * w], 'gy', axis=0, tiled=True)]
    all_to_all x0 -> x4, waiting for transfers between devices: none -> 76.9 us  [the longest x3 48.1 us: on_device(): outs.append(lax.all_to_all(payload, 'pair', 0, 0, tiled=True))]
    all_to_all x1, blocking collectives: 53.5 us -> 20.6 us  [on_device(): outs.append(lax.all_to_all(payload, 'pair', 0, 0, tiled=True))]
    all_to_all x0 -> x4, starting transfers between devices: none -> 31.2 us  [the longest x3 19.5 us: on_device(): outs.append(lax.all_to_all(payload, 'pair', 0, 0, tiled=True))]
    ppermute x0 -> x5, waiting for transfers between devices: none -> 9.94 us  [the longest x4 9.94 us: on_device(): work = keep + lax.ppermute(send, 'gx', swap)]
    ppermute x0 -> x5, starting transfers between devices: none -> 9.56 us  [the longest x4 5.94 us: on_device(): work = keep + lax.ppermute(send, 'gx', swap)]
    gather x2 -> x4, local copies, waits for them, and re-layouts: 9.29 us -> 2.39 us  [the longest x2 1.28 us: half_blocks(): return jnp.take(owner_blocks, b)]
    and x1 -> x2, other arithmetic: 5.65 us -> 0.04 us  [select(): return jnp.take(tau, half_blocks(x), axis=1).reshape(rows_l, -1)]
  transfers between devices with their start and end apart: 2 -> 13, of which waited for: 2 -> 10; matrix products, arithmetic and copies ran while one was open for 16% -> 18% of each run, Pallas kernels for 0% -> 0%
where the time goes in v1:
time: 310 us; the launch traced here: 309 us
  waiting for transfers between devices  156 us (50%)
  local copies, waits for them, and re-layouts  53.5 us (17%)
  starting transfers between devices  40.9 us (13%)
  matrix products  21 us (7%)
  blocking collectives  20.6 us (7%)
  between operations  13.5 us (4%)
  other arithmetic  3.5 us (1%)
    all_gather x4, waiting for transfers between devices, on_device(): lax.all_gather(integrals[:, c * w:(c + 1) * w], 'gy', axis=0, tiled=True)  67.1 us
    all_to_all x3, waiting for transfers between devices, on_device(): outs.append(lax.all_to_all(payload, 'pair', 0, 0, tiled=True))  48.1 us
    gather x4, local copies, waits for them, and re-layouts, pair_energies(): return jnp.take(energy, pairs[0]) + jnp.take(energy, pairs[1])  30.3 us
    all_to_all x1, waiting for transfers between devices, on_device(): t_all = lax.all_to_all(spread, 'pair', 0, 0, tiled=True)  28.8 us
    dot_general x4, matrix products, on_device(): jnp.dot(lhs, piece, precision=lax.Precision.HIGHEST, preferred_element_ty...  21 us
    all_to_all x1, blocking collectives, on_device(): outs.append(lax.all_to_all(payload, 'pair', 0, 0, tiled=True))  20.6 us
    all_to_all x3, starting transfers between devices, on_device(): outs.append(lax.all_to_all(payload, 'pair', 0, 0, tiled=True))  19.5 us
    all_to_all x1, starting transfers between devices, on_device(): t_all = lax.all_to_all(spread, 'pair', 0, 0, tiled=True)  11.7 us
  transfers between devices with their start and end apart: 13, of which 10 were waited for; matrix products, arithmetic and copies ran while one was open for 18% of the time, Pallas kernels for 0%

profile of v1, /device:TPU:1, one launch (start us, length us, event | category | flops | bytes accessed | tf_op | source)
XLA Modules:
  0.0 308.9 jit_solution(17155572473532148239)
XLA Ops:
  6.5 3.0 fusion.20
  12.4 3.6 %collective-permute-start = (f32[7,1024]{1,0:T(8,128)S(1)}, f32[7,1024]{1,0:T(8,128)S(1)}, u32[]{:S(2)}, u32[]{:S(2)}) collective-permute-start(f32[7,1024]{1,0:T(8,128)S(1)} %select_bitcast_fusion), channel_id=1, source_target_pairs={{0,1},{1,0},{2,3},{3,2},{4,5},{5,4},{6,7},{7,6},{8,9},{9,8},{10,11... | collective-permute-start | bytes 86024 | tf_op jit(solution)/shard_map/ppermute | solution.py:41
  17.5 1.7 broadcast_in_dim.34
  19.2 11.7 %all-to-all-start = ((f32[32,2,7,1024]{3,1,2,0:T(2,128)}), f32[32,2,7,1024]{3,1,2,0:T(2,128)S(1)}, u32[]{:S(2)}, u32[]{:S(2)}) async-start(f32[32,2,7,1024]{3,1,2,0:T(2,128)} %broadcast_in_dim.34), calls=%async_computation | async-start | bytes 3670016 | tf_op jit(solution)/shard_map/all_to_all | solution.py:44
  31.5 1.9 gather_fusion.5
  33.4 2.0 gather_fusion.4
  36.4 10.3 %all-gather.9.cloned.1.call-done = f32[1024,512]{1,0:T(8,128)} async-done(((f32[256,512]{1,0:T(8,128)}), f32[1024,512]{1,0:T(8,128)}) %all-gather.9.cloned.1.call-update) | async-done | bytes 2097168 | tf_op jit(solution)/shard_map/all_gather | solution.py:54
  46.7 28.8 %all-to-all-done = f32[32,2,7,1024]{3,1,2,0:T(2,128)S(1)} async-done(((f32[32,2,7,1024]{3,1,2,0:T(2,128)}), f32[32,2,7,1024]{3,1,2,0:T(2,128)S(1)}, u32[]{:S(2)}, u32[]{:S(2)}) %all-to-all-start) | async-done | bytes 1835040 | tf_op jit(solution)/shard_map/all_to_all | solution.py:44
  75.5 5.2 %fusion.2 = f32[32,2,7,512]{3,0,2,1:T(8,128)S(1)} fusion(f32[1024,512]{1,0:T(8,128)} %all-gather.9.cloned.1.call-done, f32[32,2,7,1024]{3,1,2,0:T(2,128)S(1)} %all-to-all-done), kind=kOutput, calls=%fused_computation.11 | convolution fusion | flops 2818572288 | bytes 4849664 | tf_op jit(solution)/shard_map/dot_general | solution.py:55
  81.9 5.2 %fusion = f32[32,2,7,512]{3,0,2,1:T(8,128)S(1)} fusion(f32[1024,512]{1,0:T(8,128)} %all-gather.11.cloned.1.call-done, f32[32,2,7,1024]{3,1,2,0:T(2,128)S(1)} %all-to-all-done), kind=kOutput, calls=%fused_computation.9 | convolution fusion | flops 2818572288 | bytes 4849664 | tf_op jit(solution)/shard_map/dot_general | solution.py:55
  88.9 28.2 %all-gather.7.cloned.1.call-done = f32[1024,512]{1,0:T(8,128)} async-done(((f32[256,512]{1,0:T(8,128)}), f32[1024,512]{1,0:T(8,128)}) %all-gather.7.cloned.1.call-update) | async-done | bytes 2097168 | tf_op jit(solution)/shard_map/all_gather | solution.py:54
  117.1 5.2 %fusion.4 = f32[32,2,7,512]{3,0,2,1:T(8,128)S(1)} fusion(f32[1024,512]{1,0:T(8,128)} %all-gather.7.cloned.1.call-done, f32[32,2,7,1024]{3,1,2,0:T(2,128)S(1)} %all-to-all-done), kind=kOutput, calls=%fused_computation.13 | convolution fusion | flops 2818572288 | bytes 4849664 | tf_op jit(solution)/shard_map/dot_general | solution.py:55
  124.0 28.1 %all-gather.5.cloned.1.call-done = f32[1024,512]{1,0:T(8,128)} async-done(((f32[256,512]{1,0:T(8,128)}), f32[1024,512]{1,0:T(8,128)}) %all-gather.5.cloned.1.call-update) | async-done | bytes 2097168 | tf_op jit(solution)/shard_map/all_gather | solution.py:54
  152.2 5.4 %fusion.6 = f32[32,2,7,512]{3,0,2,1:T(8,128)S(1)} fusion(f32[1024,512]{1,0:T(8,128)} %all-gather.5.cloned.1.call-done, f32[32,2,7,1024]{3,1,2,0:T(2,128)S(1)} %all-to-all-done), kind=kOutput, calls=%fused_computation.15 | convolution fusion | flops 2818572288 | bytes 4849664 | tf_op jit(solution)/shard_map/dot_general | solution.py:55
  159.3 2.7 collective-permute-start.1
  162.3 2.7 collective-permute-start.4
  165.5 13.2 %gather_fusion.7 = f32[2048]{0:T(1024)S(1)} fusion(f32[512]{0:T(512)S(1)} %copy-done, s32[2048]{0:T(1024)S(1)} %fusion.17), kind=kCustom, calls=%fused_computation.7.clone | custom fusion | bytes 24576 | tf_op jit(solution)/shard_map/jit(_take)/gather | solution.py:11
  178.7 13.2 %gather_fusion.6 = f32[2048]{0:T(1024)S(1)} fusion(f32[512]{0:T(512)S(1)} %copy-done, s32[2048]{0:T(1024)S(1)} %fusion.16), kind=kCustom, calls=%fused_computation.3.clone | custom fusion | bytes 24576 | tf_op jit(solution)/shard_map/jit(_take)/gather | solution.py:11
  192.1 9.8 %collective-permute-done.3 = f32[32,7,512]{2,0,1:T(8,128)} collective-permute-done((f32[32,7,512]{2,0,1:T(8,128)}, f32[32,7,512]{2,0,1:T(8,128)}, u32[]{:S(2)}, u32[]{:S(2)}) %collective-permute-start.3) | collective-permute-done | bytes 458784 | tf_op jit(solution)/shard_map/ppermute | solution.py:59
  201.9 3.0 fusion.15
  204.9 1.1 copy.45
  206.0 9.8 %all-to-all-start.1 = ((f32[32,7,512]{2,1,0:T(8,128)}), f32[32,7,512]{2,1,0:T(8,128)S(1)}, u32[]{:S(2)}, u32[]{:S(2)}) async-start(f32[32,7,512]{2,1,0:T(8,128)} %copy.45), calls=%async_computation.1 | async-start | bytes 1048576 | tf_op jit(solution)/shard_map/all_to_all | solution.py:61
  215.7 1.1 copy.51
  216.8 15.5 %all-to-all-done.1 = f32[32,7,512]{2,1,0:T(8,128)S(1)} async-done(((f32[32,7,512]{2,1,0:T(8,128)}), f32[32,7,512]{2,1,0:T(8,128)S(1)}, u32[]{:S(2)}, u32[]{:S(2)}) %all-to-all-start.1) | async-done | bytes 458784 | tf_op jit(solution)/shard_map/all_to_all | solution.py:61
  232.3 4.9 %all-to-all-start.4 = ((f32[32,7,512]{2,1,0:T(8,128)}), f32[32,7,512]{2,1,0:T(8,128)S(1)}, u32[]{:S(2)}, u32[]{:S(2)}) async-start(f32[32,7,512]{2,1,0:T(8,128)} %copy.51), calls=%async_computation.4 | async-start | bytes 1048576 | tf_op jit(solution)/shard_map/all_to_all | solution.py:61
  237.2 1.1 copy.49
  238.3 15.9 %all-to-all-done.4 = f32[32,7,512]{2,1,0:T(8,128)S(1)} async-done(((f32[32,7,512]{2,1,0:T(8,128)}), f32[32,7,512]{2,1,0:T(8,128)S(1)}, u32[]{:S(2)}, u32[]{:S(2)}) %all-to-all-start.4) | async-done | bytes 458784 | tf_op jit(solution)/shard_map/all_to_all | solution.py:61
  254.2 4.9 %all-to-all-start.3 = ((f32[32,7,512]{2,1,0:T(8,128)}), f32[32,7,512]{2,1,0:T(8,128)S(1)}, u32[]{:S(2)}, u32[]{:S(2)}) async-start(f32[32,7,512]{2,1,0:T(8,128)} %copy.49), calls=%async_computation.3 | async-start | bytes 1048576 | tf_op jit(solution)/shard_map/all_to_all | solution.py:61
  259.3 16.7 %all-to-all-done.3 = f32[32,7,512]{2,1,0:T(8,128)S(1)} async-done(((f32[32,7,512]{2,1,0:T(8,128)}), f32[32,7,512]{2,1,0:T(8,128)S(1)}, u32[]{:S(2)}, u32[]{:S(2)}) %all-to-all-start.3) | async-done | bytes 458784 | tf_op jit(solution)/shard_map/all_to_all | solution.py:61
  276.1 20.6 %all_to_all.25 = f32[32,7,512]{2,1,0:T(8,128)S(1)} all-to-all(f32[32,7,512]{2,1,0:T(8,128)S(1)} %copy.47), channel_id=1, replica_groups=mesh['pair'=32,'gy'=4,'gx'=2] {'pair'}, dimensions={0} | all-to-all | bytes 917504 | tf_op jit(solution)/shard_map/all_to_all | solution.py:61
  297.0 1.2 copy.52
  298.2 4.2 %reshape.175 = f32[1,7,65536]{2,0,1:T(1,128)} reshape(f32[7,32,4,512]{3,2,1,0:T(4,128)S(1)} %copy.52) | data formatting | bytes 3670016 | tf_op jit(solution)/shard_map/reshape | solution.py:63
  (75 shorter events, 13.4 us)
Async XLA Ops:
  6.5 158.9 %copy-start = (f32[512]{0:T(512)S(1)}, f32[512]{0:T(512)}, u32[]{:S(2)}) copy-start(f32[512]{0:T(512)} %param.21) | copy-start | bytes 6148
  6.5 4.5 %copy-start.11 = (f32[1,7,2048]{2,0,1:T(1,128)S(1)}, f32[1,7,2048]{2,0,1:T(1,128)}, u32[]{:S(2)}) copy-start(f32[1,7,2048]{2,0,1:T(1,128)} %param.15) | copy-start | bytes 172036
  6.5 4.6 %copy-start.2 = (s32[16]{0:T(128)S(1)}, s32[16]{0:T(128)}, u32[]{:S(2)}) copy-start(s32[16]{0:T(128)} %param.17) | copy-start | bytes 196
  6.5 40.1 %all-gather.9.cloned.1.call-start = ((), (), s32[]{:S(2)}) async-start(), calls=%async_computation.7 | async-start | bytes 2621440 | tf_op jit(solution)/shard_map/all_gather | solution.py:54
  9.5 72.3 %all-gather.11.cloned.1.call-start = ((), (), s32[]{:S(2)}) async-start(), calls=%async_computation.8 | async-start | bytes 2621440 | tf_op jit(solution)/shard_map/all_gather | solution.py:54
  10.3 106.8 %all-gather.7.cloned.1.call-start = ((), (), s32[]{:S(2)}) async-start(), calls=%async_computation.6 | async-start | bytes 2621440 | tf_op jit(solution)/shard_map/all_gather | solution.py:54
  12.4 4.9 %collective-permute-start = (f32[7,1024]{1,0:T(8,128)S(1)}, f32[7,1024]{1,0:T(8,128)S(1)}, u32[]{:S(2)}, u32[]{:S(2)}) collective-permute-start(f32[7,1024]{1,0:T(8,128)S(1)} %select_bitcast_fusion), channel_id=1, source_target_pairs={{0,1},{1,0},{2,3},{3,2},{4,5},{5,4},{6,7},{7,6},{8,9},{9,8},{10,11... | collective-permute-start | bytes 86024 | tf_op jit(solution)/shard_map/ppermute | solution.py:41
  19.2 12.3 %copy-start.12 = (s32[1,2,224]{2,1,0:T(2,128)S(1)}, s32[1,2,224]{2,1,0:T(2,128)}, u32[]{:S(2)}) copy-start(s32[1,2,224]{2,1,0:T(2,128)} %param.18) | copy-start | bytes 5380
  19.2 12.3 %copy-start.1 = (f32[64]{0:T(128)S(1)}, f32[64]{0:T(128)}, u32[]{:S(2)}) copy-start(f32[64]{0:T(128)} %param.20) | copy-start | bytes 772
  19.2 56.3 %all-to-all-start = ((f32[32,2,7,1024]{3,1,2,0:T(2,128)}), f32[32,2,7,1024]{3,1,2,0:T(2,128)S(1)}, u32[]{:S(2)}, u32[]{:S(2)}) async-start(f32[32,2,7,1024]{3,1,2,0:T(2,128)} %broadcast_in_dim.34), calls=%async_computation | async-start | bytes 3670016 | tf_op jit(solution)/shard_map/all_to_all | solution.py:44
  30.9 121.3 %all-gather.5.cloned.1.call-start = ((), (), s32[]{:S(2)}) async-start(), calls=%async_computation.5 | async-start | bytes 2621440 | tf_op jit(solution)/shard_map/all_gather | solution.py:54
  87.1 1.0 copy-start.3
  122.3 0.9 copy-start.5
  157.6 0.9 copy-start.7
  159.3 32.6 %collective-permute-start.1 = (f32[32,7,512]{2,0,1:T(8,128)}, f32[32,7,512]{2,0,1:T(8,128)S(1)}, u32[]{:S(2)}, u32[]{:S(2)}) collective-permute-start(f32[32,7,512]{2,0,1:T(8,128)} %dynamic-slice_bitcast_fusion.3), channel_id=1, source_target_pairs={{0,1},{1,0},{2,3},{3,2},{4,5},{5,4},{6,7},{7,6},{8,9},{9,8},{10,11... | collective-permute-start | bytes 1376264 | tf_op jit(solution)/shard_map/ppermute | solution.py:59
  162.0 29.9 %collective-permute-start.2 = (f32[32,7,512]{2,0,1:T(8,128)}, f32[32,7,512]{2,0,1:T(8,128)}, u32[]{:S(2)}, u32[]{:S(2)}) collective-permute-start(f32[32,7,512]{2,0,1:T(8,128)} %dynamic-slice_bitcast_fusion.2), channel_id=1, source_target_pairs={{0,1},{1,0},{2,3},{3,2},{4,5},{5,4},{6,7},{7,6},{8,9},{9,8},{10,11... | collective-permute-start | bytes 1376264 | tf_op jit(solution)/shard_map/ppermute | solution.py:59
  162.3 29.7 %collective-permute-start.4 = (f32[32,7,512]{2,0,1:T(8,128)}, f32[32,7,512]{2,0,1:T(8,128)}, u32[]{:S(2)}, u32[]{:S(2)}) collective-permute-start(f32[32,7,512]{2,0,1:T(8,128)} %dynamic-slice_bitcast_fusion), channel_id=1, source_target_pairs={{0,1},{1,0},{2,3},{3,2},{4,5},{5,4},{6,7},{7,6},{8,9},{9,8},{10,11... | collective-permute-start | bytes 1376264 | tf_op jit(solution)/shard_map/ppermute | solution.py:59
  165.0 36.9 %collective-permute-start.3 = (f32[32,7,512]{2,0,1:T(8,128)}, f32[32,7,512]{2,0,1:T(8,128)}, u32[]{:S(2)}, u32[]{:S(2)}) collective-permute-start(f32[32,7,512]{2,0,1:T(8,128)} %dynamic-slice_bitcast_fusion.1), channel_id=1, source_target_pairs={{0,1},{1,0},{2,3},{3,2},{4,5},{5,4},{6,7},{7,6},{8,9},{9,8},{10,11... | collective-permute-start | bytes 1376264 | tf_op jit(solution)/shard_map/ppermute | solution.py:59
  178.7 23.2 %copy-start.4 = (f32[32,2,7,512]{3,0,2,1:T(8,128)S(1)}, f32[32,2,7,512]{3,0,2,1:T(8,128)}, u32[]{:S(2)}) copy-start(f32[32,2,7,512]{3,0,2,1:T(8,128)} %copy-done.3) | copy-start | bytes 2752516
  178.7 23.2 %copy-start.6 = (f32[32,2,7,512]{3,0,2,1:T(8,128)S(1)}, f32[32,2,7,512]{3,0,2,1:T(8,128)}, u32[]{:S(2)}) copy-start(f32[32,2,7,512]{3,0,2,1:T(8,128)} %copy-done.5) | copy-start | bytes 2752516
  191.9 10.0 %copy-start.10 = (f32[32,7,512]{2,0,1:T(8,128)}, f32[32,7,512]{2,0,1:T(8,128)S(1)}, u32[]{:S(2)}) copy-start(f32[32,7,512]{2,0,1:T(8,128)S(1)} %collective-permute-done.1) | copy-start | bytes 1376260
  204.9 10.9 %copy-start.9 = (f32[32,7,512]{2,0,1:T(8,128)S(1)}, f32[32,7,512]{2,0,1:T(8,128)}, u32[]{:S(2)}) copy-start(f32[32,7,512]{2,0,1:T(8,128)} %get-tuple-element.24) | copy-start | bytes 1376260
  204.9 32.3 %copy-start.8 = (f32[32,7,512]{2,0,1:T(8,128)S(1)}, f32[32,7,512]{2,0,1:T(8,128)}, u32[]{:S(2)}) copy-start(f32[32,7,512]{2,0,1:T(8,128)} %get-tuple-element.25) | copy-start | bytes 1376260
  206.0 26.3 %all-to-all-start.1 = ((f32[32,7,512]{2,1,0:T(8,128)}), f32[32,7,512]{2,1,0:T(8,128)S(1)}, u32[]{:S(2)}, u32[]{:S(2)}) async-start(f32[32,7,512]{2,1,0:T(8,128)} %copy.45), calls=%async_computation.1 | async-start | bytes 1048576 | tf_op jit(solution)/shard_map/all_to_all | solution.py:61
  232.3 21.9 %all-to-all-start.4 = ((f32[32,7,512]{2,1,0:T(8,128)}), f32[32,7,512]{2,1,0:T(8,128)S(1)}, u32[]{:S(2)}, u32[]{:S(2)}) async-start(f32[32,7,512]{2,1,0:T(8,128)} %copy.51), calls=%async_computation.4 | async-start | bytes 1048576 | tf_op jit(solution)/shard_map/all_to_all | solution.py:61
  254.2 21.9 %all-to-all-start.3 = ((f32[32,7,512]{2,1,0:T(8,128)}), f32[32,7,512]{2,1,0:T(8,128)S(1)}, u32[]{:S(2)}, u32[]{:S(2)}) async-start(f32[32,7,512]{2,1,0:T(8,128)} %copy.49), calls=%async_computation.3 | async-start | bytes 1048576 | tf_op jit(solution)/shard_map/all_to_all | solution.py:61
Sparse Core Ops, SparseCore 0:
  9.7 36.9 all-gather.8
  48.5 33.3 all-gather.10
  83.7 33.3 all-gather.6
  118.8 33.3 all-gather.4

commit v2 on v1

--- a/solution.py
+++ b/solution.py
@@ -7,8 +7,13 @@
 N_CHUNK = 4
 
 
+def lookup(energy, idx):
+    k = jnp.arange(energy.shape[0], dtype=idx.dtype)
+    return jnp.sum(jnp.where(idx[..., None] == k, energy, 0.0), axis=-1)
+
+
 def pair_energies(energy, pairs):
-    return jnp.take(energy, pairs[0]) + jnp.take(energy, pairs[1])
+    return lookup(energy, pairs[0]) + lookup(energy, pairs[1])
 
 
 def on_device(amplitudes, integrals, owner_blocks, occ_pairs, vir_pairs, occ_energy, vir_energy):
@@ -50,14 +55,19 @@
 
     w = columns // N_CHUNK
     outs = []
+    works = []
     for c in range(N_CHUNK):
         piece = lax.all_gather(integrals[:, c * w:(c + 1) * w], "gy", axis=0, tiled=True)
+        if c >= 1:
+            piece, works[c - 1] = lax.optimization_barrier((piece, works[c - 1]))
+        if c >= 2:
+            piece, outs[c - 2] = lax.optimization_barrier((piece, outs[c - 2]))
         part = jnp.dot(lhs, piece, precision=lax.Precision.HIGHEST, preferred_element_type=jnp.float32)
         part = part.reshape(npair, nx, rows_l, w)
         keep = lax.dynamic_index_in_dim(part, gx, 1, keepdims=False)
         send = lax.dynamic_index_in_dim(part, 1 - gx, 1, keepdims=False)
-        work = keep + lax.ppermute(send, "gx", swap)
-        payload = work / (occ_sum[:, :, None] - vir_sum[None, None, c * w:(c + 1) * w])
+        works.append(keep + lax.ppermute(send, "gx", swap))
+        payload = works[c] / (occ_sum[:, :, None] - vir_sum[None, None, c * w:(c + 1) * w])
         outs.append(lax.all_to_all(payload, "pair", 0, 0, tiled=True))
     res = jnp.stack(outs, axis=2)
     res = jnp.transpose(res, (1, 0, 2, 3)).reshape(1, rows_l, npair * columns)

time: 310 us -> 223 us (0.72)
  waiting for transfers between devices: 156 us -> 96 us
  local copies, waits for them, and re-layouts: 53.5 us -> 17.3 us
  starting transfers between devices: 40.9 us -> 46.2 us
  blocking collectives: 20.6 us -> 24.1 us
    all_gather x4, waiting for transfers between devices: 67.1 us -> 14.8 us  [on_device(): lax.all_gather(integrals[:, c * w:(c + 1) * w], 'gy', axis=0, tiled=True)]
    all_to_all x3, waiting for transfers between devices: 48.1 us -> 0.01 us  [on_device(): outs.append(lax.all_to_all(payload, 'pair', 0, 0, tiled=True))]
    ppermute x4, waiting for transfers between devices: 9.94 us -> 51.9 us  [on_device(): works.append(keep + lax.ppermute(send, 'gx', swap))]
    gather x4 -> x0, local copies, waits for them, and re-layouts: 30.3 us -> none  [pair_energies(): return jnp.take(energy, pairs[0]) + jnp.take(energy, pairs[1])]
    ppermute x4, starting transfers between devices: 5.94 us -> 9.72 us  [on_device(): works.append(keep + lax.ppermute(send, 'gx', swap))]
    all_to_all x1, blocking collectives: 20.6 us -> 24.1 us  [on_device(): outs.append(lax.all_to_all(payload, 'pair', 0, 0, tiled=True))]
  transfers between devices with their start and end apart: 13 -> 13, of which waited for: 10 -> 6; matrix products, arithmetic and copies ran while one was open for 18% -> 15% of each run, Pallas kernels for 0% -> 0%
where the time goes in v2:
time: 223 us; the launch traced here: 222 us
  waiting for transfers between devices  96 us (43%)
  starting transfers between devices  46.2 us (21%)
  blocking collectives  24.1 us (11%)
  matrix products  20.9 us (9%)
  local copies, waits for them, and re-layouts  17.3 us (8%)
  between operations  13.5 us (6%)
  other arithmetic  3.74 us (2%)
    ppermute x4, waiting for transfers between devices, on_device(): works.append(keep + lax.ppermute(send, 'gx', swap))  51.9 us
    all_to_all x1, waiting for transfers between devices, on_device(): t_all = lax.all_to_all(spread, 'pair', 0, 0, tiled=True)  28.1 us
    all_to_all x1, blocking collectives, on_device(): outs.append(lax.all_to_all(payload, 'pair', 0, 0, tiled=True))  24.1 us
    all_to_all x3, starting transfers between devices, on_device(): outs.append(lax.all_to_all(payload, 'pair', 0, 0, tiled=True))  21.1 us
    dot_general x4, matrix products, on_device(): jnp.dot(lhs, piece, precision=lax.Precision.HIGHEST, preferred_element_ty...  20.9 us
    all_gather x4, waiting for transfers between devices, on_device(): lax.all_gather(integrals[:, c * w:(c + 1) * w], 'gy', axis=0, tiled=True)  14.8 us
    all_to_all x1, starting transfers between devices, on_device(): t_all = lax.all_to_all(spread, 'pair', 0, 0, tiled=True)  11.7 us
    ppermute x4, starting transfers between devices, on_device(): works.append(keep + lax.ppermute(send, 'gx', swap))  9.72 us
  transfers between devices with their start and end apart: 13, of which 6 were waited for; matrix products, arithmetic and copies ran while one was open for 15% of the time, Pallas kernels for 0%

profile of v2, /device:TPU:1, one launch (start us, length us, event | category | flops | bytes accessed | tf_op | source)
XLA Modules:
  0.0 221.8 jit_solution(328396562895413701)
XLA Ops:
  6.5 3.0 %fusion.14 = (f32[256,512]{1,0:T(8,128)}, f32[256,512]{1,0:T(8,128)}, f32[256,512]{1,0:T(8,128)}, f32[256,512]{1,0:T(8,128)}) fusion(f32[256,2048]{1,0:T(8,128)} %param.12), kind=kLoop, calls=%fused_computation.59 | loop fusion | bytes 4194304 | tf_op jit(solution)/shard_map/slice | solution.py:60
  9.6 0.7 all-gather.7.cloned.1.call-update
  10.5 0.6 gather_fusion.2
  11.8 3.6 %collective-permute-start = (f32[7,1024]{1,0:T(8,128)S(1)}, f32[7,1024]{1,0:T(8,128)S(1)}, u32[]{:S(2)}, u32[]{:S(2)}) collective-permute-start(f32[7,1024]{1,0:T(8,128)S(1)} %select_bitcast_fusion), channel_id=1, source_target_pairs={{0,1},{1,0},{2,3},{3,2},{4,5},{5,4},{6,7},{7,6},{8,9},{9,8},{10,11... | collective-permute-start | bytes 86024 | tf_op jit(solution)/shard_map/ppermute | solution.py:46
  16.8 1.7 broadcast_in_dim.46
  18.5 11.7 %all-to-all-start = ((f32[32,2,7,1024]{3,1,2,0:T(2,128)}), f32[32,2,7,1024]{3,1,2,0:T(2,128)S(1)}, u32[]{:S(2)}, u32[]{:S(2)}) async-start(f32[32,2,7,1024]{3,1,2,0:T(2,128)} %broadcast_in_dim.46), calls=%async_computation | async-start | bytes 3670016 | tf_op jit(solution)/shard_map/all_to_all | solution.py:49
  31.1 0.9 constant_dynamic-slice_fusion
  32.0 14.7 %all-gather.9.cloned.1.call-done = f32[1024,512]{1,0:T(8,128)} async-done(((f32[256,512]{1,0:T(8,128)}), f32[1024,512]{1,0:T(8,128)}) %all-gather.9.cloned.1.call-update) | async-done | bytes 2097168 | tf_op jit(solution)/shard_map/all_gather | solution.py:60
  46.7 28.1 %all-to-all-done = f32[32,2,7,1024]{3,1,2,0:T(2,128)S(1)} async-done(((f32[32,2,7,1024]{3,1,2,0:T(2,128)}), f32[32,2,7,1024]{3,1,2,0:T(2,128)S(1)}, u32[]{:S(2)}, u32[]{:S(2)}) %all-to-all-start) | async-done | bytes 1835040 | tf_op jit(solution)/shard_map/all_to_all | solution.py:49
  74.8 5.2 %fusion.6 = f32[32,2,7,512]{3,0,2,1:T(8,128)S(1)} fusion(f32[1024,512]{1,0:T(8,128)} %all-gather.9.cloned.1.call-done, f32[32,2,7,1024]{3,1,2,0:T(2,128)S(1)} %all-to-all-done), kind=kOutput, calls=%fused_computation.15 | convolution fusion | flops 2818572288 | bytes 4849664 | tf_op jit(solution)/shard_map/dot_general | solution.py:65
  80.1 2.5 %collective-permute-start.1 = (f32[32,7,512]{2,0,1:T(8,128)S(1)}, f32[32,7,512]{2,0,1:T(8,128)}, u32[]{:S(2)}, u32[]{:S(2)}) collective-permute-start(f32[32,7,512]{2,0,1:T(8,128)S(1)} %dynamic-slice_bitcast_fusion.3), channel_id=1, source_target_pairs={{0,1},{1,0},{2,3},{3,2},{4,5},{5,4},{6,7},{7,6},{8,9},{9,8},{10,11... | collective-permute-start | bytes 1376264 | tf_op jit(solution)/shard_map/ppermute | solution.py:69
  82.6 1.6 select_reduce_fusion
  84.2 9.2 %collective-permute-done.1 = f32[32,7,512]{2,0,1:T(8,128)} collective-permute-done((f32[32,7,512]{2,0,1:T(8,128)S(1)}, f32[32,7,512]{2,0,1:T(8,128)}, u32[]{:S(2)}, u32[]{:S(2)}) %collective-permute-start.1) | collective-permute-done | bytes 458784 | tf_op jit(solution)/shard_map/ppermute | solution.py:69
  93.4 1.2 subtract_divide_fusion.2
  94.6 1.1 copy.60
  95.7 5.5 %all-to-all-start.1 = ((f32[32,7,512]{2,1,0:T(8,128)}), f32[32,7,512]{2,1,0:T(8,128)S(1)}, u32[]{:S(2)}, u32[]{:S(2)}) async-start(f32[32,7,512]{2,1,0:T(8,128)} %copy.60), calls=%async_computation.1 | async-start | bytes 1048576 | tf_op jit(solution)/shard_map/all_to_all | solution.py:71
  101.2 5.2 %fusion.4 = f32[32,2,7,512]{3,0,2,1:T(8,128)S(1)} fusion(f32[1024,512]{1,0:T(8,128)} %all-gather.7.cloned.1.call-done, f32[32,2,7,1024]{3,1,2,0:T(2,128)S(1)} %all-to-all-done), kind=kOutput, calls=%fused_computation.13 | convolution fusion | flops 2818572288 | bytes 4849664 | tf_op jit(solution)/shard_map/dot_general | solution.py:65
  106.4 2.7 %collective-permute-start.2 = (f32[32,7,512]{2,0,1:T(8,128)S(1)}, f32[32,7,512]{2,0,1:T(8,128)S(1)}, u32[]{:S(2)}, u32[]{:S(2)}) collective-permute-start(f32[32,7,512]{2,0,1:T(8,128)S(1)} %dynamic-slice_bitcast_fusion.2), channel_id=1, source_target_pairs={{0,1},{1,0},{2,3},{3,2},{4,5},{5,4},{6,7},{7,6},{8,9},{9,8},{10,11... | collective-permute-start | bytes 1376264 | tf_op jit(solution)/shard_map/ppermute | solution.py:69
  109.2 14.0 %collective-permute-done.2 = f32[32,7,512]{2,0,1:T(8,128)S(1)} collective-permute-done((f32[32,7,512]{2,0,1:T(8,128)S(1)}, f32[32,7,512]{2,0,1:T(8,128)S(1)}, u32[]{:S(2)}, u32[]{:S(2)}) %collective-permute-start.2) | collective-permute-done | bytes 458784 | tf_op jit(solution)/shard_map/ppermute | solution.py:69
  123.3 1.1 copy.62
  124.4 7.9 %all-to-all-start.2 = ((f32[32,7,512]{2,1,0:T(8,128)}), f32[32,7,512]{2,1,0:T(8,128)S(1)}, u32[]{:S(2)}, u32[]{:S(2)}) async-start(f32[32,7,512]{2,1,0:T(8,128)} %copy.62), calls=%async_computation.2 | async-start | bytes 1048576 | tf_op jit(solution)/shard_map/all_to_all | solution.py:71
  132.3 5.3 %fusion.2 = f32[32,2,7,512]{3,0,2,1:T(8,128)S(1)} fusion(f32[1024,512]{1,0:T(8,128)} %all-gather.5.cloned.1.call-done, f32[32,2,7,1024]{3,1,2,0:T(2,128)S(1)} %all-to-all-done), kind=kOutput, calls=%fused_computation.11 | convolution fusion | flops 2818572288 | bytes 4849664 | tf_op jit(solution)/shard_map/dot_general | solution.py:65
  137.6 2.3 %collective-permute-start.3 = (f32[32,7,512]{2,0,1:T(8,128)S(1)}, f32[32,7,512]{2,0,1:T(8,128)S(1)}, u32[]{:S(2)}, u32[]{:S(2)}) collective-permute-start(f32[32,7,512]{2,0,1:T(8,128)S(1)} %dynamic-slice_bitcast_fusion.1), channel_id=1, source_target_pairs={{0,1},{1,0},{2,3},{3,2},{4,5},{5,4},{6,7},{7,6},{8,9},{9,8},{10,11... | collective-permute-start | bytes 1376264 | tf_op jit(solution)/shard_map/ppermute | solution.py:69
  139.9 14.3 %collective-permute-done.3 = f32[32,7,512]{2,0,1:T(8,128)S(1)} collective-permute-done((f32[32,7,512]{2,0,1:T(8,128)S(1)}, f32[32,7,512]{2,0,1:T(8,128)S(1)}, u32[]{:S(2)}, u32[]{:S(2)}) %collective-permute-start.3) | collective-permute-done | bytes 458784 | tf_op jit(solution)/shard_map/ppermute | solution.py:69
  154.4 1.1 copy.63
  155.5 7.7 %all-to-all-start.3 = ((f32[32,7,512]{2,1,0:T(8,128)}), f32[32,7,512]{2,1,0:T(8,128)S(1)}, u32[]{:S(2)}, u32[]{:S(2)}) async-start(f32[32,7,512]{2,1,0:T(8,128)} %copy.63), calls=%async_computation.3 | async-start | bytes 1048576 | tf_op jit(solution)/shard_map/all_to_all | solution.py:71
  163.2 5.2 %fusion = f32[32,2,7,512]{3,0,2,1:T(8,128)S(1)} fusion(f32[1024,512]{1,0:T(8,128)} %all-gather.11.cloned.1.call-done, f32[32,2,7,1024]{3,1,2,0:T(2,128)S(1)} %all-to-all-done), kind=kOutput, calls=%fused_computation.9 | convolution fusion | flops 2818572288 | bytes 4849664 | tf_op jit(solution)/shard_map/dot_general | solution.py:65
  168.5 2.2 collective-permute-start.4
  170.7 14.4 %collective-permute-done.4 = f32[32,7,512]{2,0,1:T(8,128)S(1)} collective-permute-done((f32[32,7,512]{2,0,1:T(8,128)S(1)}, f32[32,7,512]{2,0,1:T(8,128)S(1)}, u32[]{:S(2)}, u32[]{:S(2)}) %collective-permute-start.4) | collective-permute-done | bytes 458784 | tf_op jit(solution)/shard_map/ppermute | solution.py:69
  185.5 24.1 %all_to_all.25 = f32[32,7,512]{2,1,0:T(8,128)S(1)} all-to-all(f32[32,7,512]{2,1,0:T(8,128)S(1)} %copy.65), channel_id=1, replica_groups=mesh['pair'=32,'gy'=4,'gx'=2] {'pair'}, dimensions={0} | all-to-all | bytes 917504 | tf_op jit(solution)/shard_map/all_to_all | solution.py:71
  209.8 1.2 copy.66
  211.0 4.2 %reshape.134 = f32[1,7,65536]{2,0,1:T(1,128)} reshape(f32[7,32,4,512]{3,2,1,0:T(4,128)S(1)} %copy.66) | data formatting | bytes 3670016 | tf_op jit(solution)/shard_map/reshape | solution.py:73
  (55 shorter events, 4.2 us)
Async XLA Ops:
  6.5 3.9 %copy-start = (s32[16]{0:T(128)S(1)}, s32[16]{0:T(128)}, u32[]{:S(2)}) copy-start(s32[16]{0:T(128)} %param.13) | copy-start | bytes 196
  6.5 3.8 %copy-start.1 = (f32[1,7,2048]{2,0,1:T(1,128)S(1)}, f32[1,7,2048]{2,0,1:T(1,128)}, u32[]{:S(2)}) copy-start(f32[1,7,2048]{2,0,1:T(1,128)} %param.11) | copy-start | bytes 172036
  6.5 40.2 %all-gather.9.cloned.1.call-start = ((), (), s32[]{:S(2)}) async-start(), calls=%async_computation.7 | async-start | bytes 2621440 | tf_op jit(solution)/shard_map/all_gather | solution.py:60
  9.6 85.0 %all-gather.7.cloned.1.call-start = ((), (), s32[]{:S(2)}) async-start(), calls=%async_computation.6 | async-start | bytes 2621440 | tf_op jit(solution)/shard_map/all_gather | solution.py:60
  10.3 113.0 %all-gather.5.cloned.1.call-start = ((), (), s32[]{:S(2)}) async-start(), calls=%async_computation.5 | async-start | bytes 2621440 | tf_op jit(solution)/shard_map/all_gather | solution.py:60
  11.8 5.0 %collective-permute-start = (f32[7,1024]{1,0:T(8,128)S(1)}, f32[7,1024]{1,0:T(8,128)S(1)}, u32[]{:S(2)}, u32[]{:S(2)}) collective-permute-start(f32[7,1024]{1,0:T(8,128)S(1)} %select_bitcast_fusion), channel_id=1, source_target_pairs={{0,1},{1,0},{2,3},{3,2},{4,5},{5,4},{6,7},{7,6},{8,9},{9,8},{10,11... | collective-permute-start | bytes 86024 | tf_op jit(solution)/shard_map/ppermute | solution.py:46
  18.5 12.3 %copy-start.3 = (s32[1,2,224]{2,1,0:T(2,128)S(1)}, s32[1,2,224]{2,1,0:T(2,128)}, u32[]{:S(2)}) copy-start(s32[1,2,224]{2,1,0:T(2,128)} %param.14) | copy-start | bytes 5380
  18.5 12.3 %copy-start.4 = (f32[64]{0:T(128)S(1)}, f32[64]{0:T(128)}, u32[]{:S(2)}) copy-start(f32[64]{0:T(128)} %param.16) | copy-start | bytes 772
  18.5 56.3 %all-to-all-start = ((f32[32,2,7,1024]{3,1,2,0:T(2,128)}), f32[32,2,7,1024]{3,1,2,0:T(2,128)S(1)}, u32[]{:S(2)}, u32[]{:S(2)}) async-start(f32[32,2,7,1024]{3,1,2,0:T(2,128)} %broadcast_in_dim.46), calls=%async_computation | async-start | bytes 3670016 | tf_op jit(solution)/shard_map/all_to_all | solution.py:49
  30.2 124.2 %all-gather.11.cloned.1.call-start = ((), (), s32[]{:S(2)}) async-start(), calls=%async_computation.8 | async-start | bytes 2621440 | tf_op jit(solution)/shard_map/all_gather | solution.py:60
  32.0 50.6 %copy-start.2 = (f32[512]{0:T(512)S(1)}, f32[512]{0:T(512)}, u32[]{:S(2)}) copy-start(f32[512]{0:T(512)} %param.17) | copy-start | bytes 6148
  80.1 13.3 %collective-permute-start.1 = (f32[32,7,512]{2,0,1:T(8,128)S(1)}, f32[32,7,512]{2,0,1:T(8,128)}, u32[]{:S(2)}, u32[]{:S(2)}) collective-permute-start(f32[32,7,512]{2,0,1:T(8,128)S(1)} %dynamic-slice_bitcast_fusion.3), channel_id=1, source_target_pairs={{0,1},{1,0},{2,3},{3,2},{4,5},{5,4},{6,7},{7,6},{8,9},{9,8},{10,11... | collective-permute-start | bytes 1376264 | tf_op jit(solution)/shard_map/ppermute | solution.py:69
  95.7 28.7 %all-to-all-start.1 = ((f32[32,7,512]{2,1,0:T(8,128)}), f32[32,7,512]{2,1,0:T(8,128)S(1)}, u32[]{:S(2)}, u32[]{:S(2)}) async-start(f32[32,7,512]{2,1,0:T(8,128)} %copy.60), calls=%async_computation.1 | async-start | bytes 1048576 | tf_op jit(solution)/shard_map/all_to_all | solution.py:71
  106.4 16.7 %collective-permute-start.2 = (f32[32,7,512]{2,0,1:T(8,128)S(1)}, f32[32,7,512]{2,0,1:T(8,128)S(1)}, u32[]{:S(2)}, u32[]{:S(2)}) collective-permute-start(f32[32,7,512]{2,0,1:T(8,128)S(1)} %dynamic-slice_bitcast_fusion.2), channel_id=1, source_target_pairs={{0,1},{1,0},{2,3},{3,2},{4,5},{5,4},{6,7},{7,6},{8,9},{9,8},{10,11... | collective-permute-start | bytes 1376264 | tf_op jit(solution)/shard_map/ppermute | solution.py:69
  124.4 30.0 %all-to-all-start.2 = ((f32[32,7,512]{2,1,0:T(8,128)}), f32[32,7,512]{2,1,0:T(8,128)S(1)}, u32[]{:S(2)}, u32[]{:S(2)}) async-start(f32[32,7,512]{2,1,0:T(8,128)} %copy.62), calls=%async_computation.2 | async-start | bytes 1048576 | tf_op jit(solution)/shard_map/all_to_all | solution.py:71
  137.6 16.6 %collective-permute-start.3 = (f32[32,7,512]{2,0,1:T(8,128)S(1)}, f32[32,7,512]{2,0,1:T(8,128)S(1)}, u32[]{:S(2)}, u32[]{:S(2)}) collective-permute-start(f32[32,7,512]{2,0,1:T(8,128)S(1)} %dynamic-slice_bitcast_fusion.1), channel_id=1, source_target_pairs={{0,1},{1,0},{2,3},{3,2},{4,5},{5,4},{6,7},{7,6},{8,9},{9,8},{10,11... | collective-permute-start | bytes 1376264 | tf_op jit(solution)/shard_map/ppermute | solution.py:69
  155.5 30.0 %all-to-all-start.3 = ((f32[32,7,512]{2,1,0:T(8,128)}), f32[32,7,512]{2,1,0:T(8,128)S(1)}, u32[]{:S(2)}, u32[]{:S(2)}) async-start(f32[32,7,512]{2,1,0:T(8,128)} %copy.63), calls=%async_computation.3 | async-start | bytes 1048576 | tf_op jit(solution)/shard_map/all_to_all | solution.py:71
  168.5 16.6 %collective-permute-start.4 = (f32[32,7,512]{2,0,1:T(8,128)S(1)}, f32[32,7,512]{2,0,1:T(8,128)S(1)}, u32[]{:S(2)}, u32[]{:S(2)}) collective-permute-start(f32[32,7,512]{2,0,1:T(8,128)S(1)} %dynamic-slice_bitcast_fusion), channel_id=1, source_target_pairs={{0,1},{1,0},{2,3},{3,2},{4,5},{5,4},{6,7},{7,6},{8,9},{9,8},{10,11... | collective-permute-start | bytes 1376264 | tf_op jit(solution)/shard_map/ppermute | solution.py:69
Sparse Core Ops, SparseCore 0:
  9.7 36.9 all-gather.8
  48.5 33.3 all-gather.6
  83.7 33.3 all-gather.4
  118.8 33.3 all-gather.10

commit v3 on v2

--- a/solution.py
+++ b/solution.py
@@ -4,7 +4,7 @@
 from jax import lax
 from jax.sharding import Mesh, PartitionSpec as P
 
-N_CHUNK = 4
+CHUNK_PARTS = (4, 5, 5, 2)
 
 
 def lookup(energy, idx):
@@ -53,13 +53,14 @@
     vir_local = lax.dynamic_slice_in_dim(vir_pairs, p * columns, columns, 1)
     vir_sum = pair_energies(vir_energy, vir_local)
 
-    w = columns // N_CHUNK
+    unit = columns // sum(CHUNK_PARTS)
+    bounds = np.cumsum((0,) + CHUNK_PARTS) * unit
     outs = []
     works = []
-    for c in range(N_CHUNK):
-        piece = lax.all_gather(integrals[:, c * w:(c + 1) * w], "gy", axis=0, tiled=True)
-        if c >= 1:
-            piece, works[c - 1] = lax.optimization_barrier((piece, works[c - 1]))
+    for c in range(len(CHUNK_PARTS)):
+        lo, hi = int(bounds[c]), int(bounds[c + 1])
+        w = hi - lo
+        piece = lax.all_gather(integrals[:, lo:hi], "gy", axis=0, tiled=True)
         if c >= 2:
             piece, outs[c - 2] = lax.optimization_barrier((piece, outs[c - 2]))
         part = jnp.dot(lhs, piece, precision=lax.Precision.HIGHEST, preferred_element_type=jnp.float32)
@@ -67,10 +68,10 @@
         keep = lax.dynamic_index_in_dim(part, gx, 1, keepdims=False)
         send = lax.dynamic_index_in_dim(part, 1 - gx, 1, keepdims=False)
         works.append(keep + lax.ppermute(send, "gx", swap))
-        payload = works[c] / (occ_sum[:, :, None] - vir_sum[None, None, c * w:(c + 1) * w])
+        payload = works[c] / (occ_sum[:, :, None] - vir_sum[None, None, lo:hi])
         outs.append(lax.all_to_all(payload, "pair", 0, 0, tiled=True))
-    res = jnp.stack(outs, axis=2)
-    res = jnp.transpose(res, (1, 0, 2, 3)).reshape(1, rows_l, npair * columns)
+    res = jnp.concatenate(outs, axis=2)
+    res = jnp.transpose(res, (1, 0, 2)).reshape(1, rows_l, npair * columns)
     return res
 
 

time: 223 us -> 235 us (1.054)
  waiting for transfers between devices: 96 us -> 109 us
  blocking collectives: 24.1 us -> 16.5 us
  local copies, waits for them, and re-layouts: 17.3 us -> 20.8 us
    ppermute x4, waiting for transfers between devices: 51.9 us -> 31.6 us  [on_device(): works.append(keep + lax.ppermute(send, 'gx', swap))]
    all_to_all x3, waiting for transfers between devices: 0.01 us -> 20.2 us  [on_device(): outs.append(lax.all_to_all(payload, 'pair', 0, 0, tiled=True))]
    all_gather x4, waiting for transfers between devices: 14.8 us -> 27 us  [on_device(): piece = lax.all_gather(integrals[:, lo:hi], 'gy', axis=0, tiled=True)]
    all_to_all x1, blocking collectives: 24.1 us -> 16.5 us  [on_device(): outs.append(lax.all_to_all(payload, 'pair', 0, 0, tiled=True))]
    slice x2 -> x6, local copies, waits for them, and re-layouts: 3.01 us -> 6.13 us  [the longest x3 6.11 us: on_device(): piece = lax.all_gather(integrals[:, lo:hi], 'gy', axis=0, tiled=True)]
  transfers between devices with their start and end apart: 13 -> 13, of which waited for: 6 -> 8; matrix products, arithmetic and copies ran while one was open for 15% -> 18% of each run, Pallas kernels for 0% -> 0%
where the time goes in v3:
time: 235 us; the launch traced here: 234 us
  waiting for transfers between devices  109 us (46%)
  starting transfers between devices  46 us (20%)
  matrix products  22.3 us (9%)
  local copies, waits for them, and re-layouts  20.8 us (9%)
  blocking collectives  16.5 us (7%)
  between operations  13.5 us (6%)
  other arithmetic  6 us (3%)
    ppermute x4, waiting for transfers between devices, on_device(): works.append(keep + lax.ppermute(send, 'gx', swap))  31.6 us
    all_to_all x1, waiting for transfers between devices, on_device(): t_all = lax.all_to_all(spread, 'pair', 0, 0, tiled=True)  29.3 us
    all_gather x4, waiting for transfers between devices, on_device(): piece = lax.all_gather(integrals[:, lo:hi], 'gy', axis=0, tiled=True)  27 us
    dot_general x4, matrix products, on_device(): jnp.dot(lhs, piece, precision=lax.Precision.HIGHEST, preferred_element_ty...  22.3 us
    all_to_all x3, starting transfers between devices, on_device(): outs.append(lax.all_to_all(payload, 'pair', 0, 0, tiled=True))  20.3 us
    all_to_all x3, waiting for transfers between devices, on_device(): outs.append(lax.all_to_all(payload, 'pair', 0, 0, tiled=True))  20.2 us
    all_to_all x1, blocking collectives, on_device(): outs.append(lax.all_to_all(payload, 'pair', 0, 0, tiled=True))  16.5 us
    all_to_all x1, starting transfers between devices, on_device(): t_all = lax.all_to_all(spread, 'pair', 0, 0, tiled=True)  11.6 us
  transfers between devices with their start and end apart: 13, of which 8 were waited for; matrix products, arithmetic and copies ran while one was open for 18% of the time, Pallas kernels for 0%

profile of v3, /device:TPU:1, one launch (start us, length us, event | category | flops | bytes accessed | tf_op | source)
XLA Modules:
  0.0 233.9 jit_solution(7991842334645575070)
XLA Ops:
  6.5 1.9 slice.39
  8.5 2.5 %fusion.17 = (f32[256,640]{1,0:T(8,128)}, f32[256,640]{1,0:T(8,128)}) fusion(f32[256,2048]{1,0:T(8,128)} %param.12), kind=kLoop, calls=%fused_computation.59 | loop fusion | bytes 2621440 | tf_op jit(solution)/shard_map/slice | solution.py:63
  12.5 3.6 %collective-permute-start = (f32[7,1024]{1,0:T(8,128)S(1)}, f32[7,1024]{1,0:T(8,128)S(1)}, u32[]{:S(2)}, u32[]{:S(2)}) collective-permute-start(f32[7,1024]{1,0:T(8,128)S(1)} %select_bitcast_fusion), channel_id=1, source_target_pairs={{0,1},{1,0},{2,3},{3,2},{4,5},{5,4},{6,7},{7,6},{8,9},{9,8},{10,11... | collective-permute-start | bytes 86024 | tf_op jit(solution)/shard_map/ppermute | solution.py:46
  17.5 1.7 broadcast_in_dim.46
  19.2 11.6 %all-to-all-start = ((f32[32,2,7,1024]{3,1,2,0:T(2,128)}), f32[32,2,7,1024]{3,1,2,0:T(2,128)S(1)}, u32[]{:S(2)}, u32[]{:S(2)}) async-start(f32[32,2,7,1024]{3,1,2,0:T(2,128)} %broadcast_in_dim.46), calls=%async_computation | async-start | bytes 3670016 | tf_op jit(solution)/shard_map/all_to_all | solution.py:49
  32.4 13.7 %all-gather.7.cloned.1.call-done = f32[1024,512]{1,0:T(8,128)} async-done(((f32[256,512]{1,0:T(8,128)}), f32[1024,512]{1,0:T(8,128)}) %all-gather.7.cloned.1.call-update) | async-done | bytes 2097168 | tf_op jit(solution)/shard_map/all_gather | solution.py:63
  46.1 29.3 %all-to-all-done = f32[32,2,7,1024]{3,1,2,0:T(2,128)S(1)} async-done(((f32[32,2,7,1024]{3,1,2,0:T(2,128)}), f32[32,2,7,1024]{3,1,2,0:T(2,128)S(1)}, u32[]{:S(2)}, u32[]{:S(2)}) %all-to-all-start) | async-done | bytes 1835040 | tf_op jit(solution)/shard_map/all_to_all | solution.py:49
  75.4 5.2 %fusion.4 = f32[32,2,7,512]{3,0,2,1:T(8,128)S(1)} fusion(f32[1024,512]{1,0:T(8,128)} %all-gather.7.cloned.1.call-done, f32[32,2,7,1024]{3,1,2,0:T(2,128)S(1)} %all-to-all-done), kind=kOutput, calls=%fused_computation.13 | convolution fusion | flops 2818572288 | bytes 4849664 | tf_op jit(solution)/shard_map/dot_general | solution.py:66
  80.7 2.5 %collective-permute-start.1 = (f32[32,7,512]{2,0,1:T(8,128)S(1)}, f32[32,7,512]{2,0,1:T(8,128)}, u32[]{:S(2)}, u32[]{:S(2)}) collective-permute-start(f32[32,7,512]{2,0,1:T(8,128)S(1)} %dynamic-slice_bitcast_fusion.2), channel_id=1, source_target_pairs={{0,1},{1,0},{2,3},{3,2},{4,5},{5,4},{6,7},{7,6},{8,9},{9,8},{10,11... | collective-permute-start | bytes 1376264 | tf_op jit(solution)/shard_map/ppermute | solution.py:70
  83.2 1.6 select_reduce_fusion
  85.1 8.9 %collective-permute-done.1 = f32[32,7,512]{2,0,1:T(8,128)} collective-permute-done((f32[32,7,512]{2,0,1:T(8,128)S(1)}, f32[32,7,512]{2,0,1:T(8,128)}, u32[]{:S(2)}, u32[]{:S(2)}) %collective-permute-start.1) | collective-permute-done | bytes 458784 | tf_op jit(solution)/shard_map/ppermute | solution.py:70
  94.0 1.2 fusion.14
  96.2 5.4 %all-to-all-start.1 = ((f32[32,7,512]{2,1,0:T(8,128)}), f32[32,7,512]{2,1,0:T(8,128)S(1)}, u32[]{:S(2)}, u32[]{:S(2)}) async-start(f32[32,7,512]{2,1,0:T(8,128)} %copy.56), calls=%async_computation.1 | async-start | bytes 1048576 | tf_op jit(solution)/shard_map/all_to_all | solution.py:72
  102.0 6.8 %fusion.2 = f32[32,2,7,640]{3,0,2,1:T(8,128)S(1)} fusion(f32[1024,640]{1,0:T(8,128)} %all-gather.11.cloned.1.call-done, f32[32,2,7,1024]{3,1,2,0:T(2,128)S(1)} %all-to-all-done), kind=kOutput, calls=%fused_computation.10 | convolution fusion | flops 3523215360 | bytes 5603328 | tf_op jit(solution)/shard_map/dot_general | solution.py:66
  109.6 2.5 %collective-permute-start.2 = (f32[32,7,640]{2,0,1:T(8,128)}, f32[32,7,640]{2,0,1:T(8,128)}, u32[]{:S(2)}, u32[]{:S(2)}) collective-permute-start(f32[32,7,640]{2,0,1:T(8,128)} %dynamic-slice_bitcast_fusion.1), channel_id=1, source_target_pairs={{0,1},{1,0},{2,3},{3,2},{4,5},{5,4},{6,7},{7,6},{8,9},{9,8},{10,11... | collective-permute-start | bytes 1720328 | tf_op jit(solution)/shard_map/ppermute | solution.py:70
  112.1 13.3 %all-gather.5.cloned.1.call-done = f32[1024,640]{1,0:T(8,128)} async-done(((f32[256,640]{1,0:T(8,128)}), f32[1024,640]{1,0:T(8,128)}) %all-gather.5.cloned.1.call-update) | async-done | bytes 2621456 | tf_op jit(solution)/shard_map/all_gather | solution.py:63
  125.4 7.0 %fusion = f32[32,2,7,640]{3,0,2,1:T(8,128)S(1)} fusion(f32[1024,640]{1,0:T(8,128)} %all-gather.5.cloned.1.call-done, f32[32,2,7,1024]{3,1,2,0:T(2,128)S(1)} %all-to-all-done), kind=kOutput, calls=%fused_computation.8 | convolution fusion | flops 3523215360 | bytes 5603328 | tf_op jit(solution)/shard_map/dot_general | solution.py:66
  134.2 2.7 %collective-permute-start.3 = (f32[32,7,640]{2,0,1:T(8,128)}, f32[32,7,640]{2,0,1:T(8,128)}, u32[]{:S(2)}, u32[]{:S(2)}) collective-permute-start(f32[32,7,640]{2,0,1:T(8,128)} %dynamic-slice_bitcast_fusion), channel_id=1, source_target_pairs={{0,1},{1,0},{2,3},{3,2},{4,5},{5,4},{6,7},{7,6},{8,9},{9,8},{10,11... | collective-permute-start | bytes 1720328 | tf_op jit(solution)/shard_map/ppermute | solution.py:70
  136.9 1.7 slice.45
  138.7 11.1 %collective-permute-done.3 = f32[32,7,640]{2,0,1:T(8,128)} collective-permute-done((f32[32,7,640]{2,0,1:T(8,128)}, f32[32,7,640]{2,0,1:T(8,128)}, u32[]{:S(2)}, u32[]{:S(2)}) %collective-permute-start.3) | collective-permute-done | bytes 573472 | tf_op jit(solution)/shard_map/ppermute | solution.py:70
  149.8 2.6 %fusion.12 = (f32[32,7,640]{2,0,1:T(8,128)}, f32[32,7,640]{2,0,1:T(8,128)S(1)}) fusion(f32[32,7,640]{2,0,1:T(8,128)} %collective-permute-done.3, f32[32,2,7,640]{3,0,2,1:T(8,128)} %copy-done.1, s32[]{:T(128)S(6)} %select_n.79, f32[640]{0:T(1024)S(1)} %get-tuple-element.27, f32[32,7]{0,1:T(8,128)S(1)} %copy.55, f32[640]{0:T(1024)S(1)} %get-tuple-element.28, ...), kind=kLoop, calls=%fused_computation.22 | loop fusion | flops 860160 | bytes 3446660 | tf_op jit(solution)/shard_map/div | solution.py:71
  152.3 1.2 copy.59
  153.5 9.7 %all-to-all-start.2 = ((f32[32,7,640]{2,1,0:T(8,128)}), f32[32,7,640]{2,1,0:T(8,128)S(1)}, u32[]{:S(2)}, u32[]{:S(2)}) async-start(f32[32,7,640]{2,1,0:T(8,128)} %copy.59), calls=%async_computation.2 | async-start | bytes 1310720 | tf_op jit(solution)/shard_map/all_to_all | solution.py:72
  163.2 1.2 copy.61
  164.4 18.4 %all-to-all-done.2 = f32[32,7,640]{2,1,0:T(8,128)S(1)} async-done(((f32[32,7,640]{2,1,0:T(8,128)}), f32[32,7,640]{2,1,0:T(8,128)S(1)}, u32[]{:S(2)}, u32[]{:S(2)}) %all-to-all-start.2) | async-done | bytes 573472 | tf_op jit(solution)/shard_map/all_to_all | solution.py:72
  182.8 5.1 %all-to-all-start.3 = ((f32[32,7,640]{2,1,0:T(8,128)}), f32[32,7,640]{2,1,0:T(8,128)S(1)}, u32[]{:S(2)}, u32[]{:S(2)}) async-start(f32[32,7,640]{2,1,0:T(8,128)} %copy.61), calls=%async_computation.3 | async-start | bytes 1310720 | tf_op jit(solution)/shard_map/all_to_all | solution.py:72
  187.9 3.3 %fusion.6 = f32[32,2,7,256]{3,0,2,1:T(8,128)S(1)} fusion(f32[32,2,7,1024]{3,1,2,0:T(2,128)S(1)} %all-to-all-done, f32[1024,256]{1,0:T(8,128)} %all-gather.9.cloned.1.call-done), kind=kOutput, calls=%fused_computation.15 | convolution fusion | flops 1409286144 | bytes 3342336 | tf_op jit(solution)/shard_map/dot_general | solution.py:66
  191.2 2.5 %collective-permute-start.4 = (f32[32,7,256]{2,0,1:T(8,128)S(1)}, f32[32,7,256]{2,0,1:T(8,128)S(1)}, u32[]{:S(2)}, u32[]{:S(2)}) collective-permute-start(f32[32,7,256]{2,0,1:T(8,128)S(1)} %dynamic-slice_bitcast_fusion.3), channel_id=1, source_target_pairs={{0,1},{1,0},{2,3},{3,2},{4,5},{5,4},{6,7},{7,6},{8,9},{9,8},{10,11... | collective-permute-start | bytes 688136 | tf_op jit(solution)/shard_map/ppermute | solution.py:70
  193.7 11.6 %collective-permute-done.4 = f32[32,7,256]{2,0,1:T(8,128)S(1)} collective-permute-done((f32[32,7,256]{2,0,1:T(8,128)S(1)}, f32[32,7,256]{2,0,1:T(8,128)S(1)}, u32[]{:S(2)}, u32[]{:S(2)}) %collective-permute-start.4) | collective-permute-done | bytes 229408 | tf_op jit(solution)/shard_map/ppermute | solution.py:70
  205.6 1.9 all-to-all-done.3
  207.5 16.5 %all_to_all.25 = f32[32,7,256]{2,1,0:T(8,128)S(1)} all-to-all(f32[32,7,256]{2,1,0:T(8,128)S(1)} %copy.64), channel_id=1, replica_groups=mesh['pair'=32,'gy'=4,'gx'=2] {'pair'}, dimensions={0} | all-to-all | bytes 458752 | tf_op jit(solution)/shard_map/all_to_all | solution.py:72
  224.2 3.1 %copy.65 = f32[1,7,65536]{2,0,1:T(1,128)} copy(f32[1,7,65536]{2,1,0:T(8,128)S(1)} %bitcast.61) | data formatting | bytes 3670016 | tf_op jit(solution)/shard_map/reshape | solution.py:74
  (65 shorter events, 9.3 us)
Async XLA Ops:
  6.5 4.6 %copy-start = (s32[16]{0:T(128)S(1)}, s32[16]{0:T(128)}, u32[]{:S(2)}) copy-start(s32[16]{0:T(128)} %param.13) | copy-start | bytes 196
  6.5 39.6 %all-gather.7.cloned.1.call-start = ((), (), s32[]{:S(2)}) async-start(), calls=%async_computation.6 | async-start | bytes 2621440 | tf_op jit(solution)/shard_map/all_gather | solution.py:63
  8.4 2.6 %copy-start.5 = (f32[1,7,2048]{2,0,1:T(1,128)S(1)}, f32[1,7,2048]{2,0,1:T(1,128)}, u32[]{:S(2)}) copy-start(f32[1,7,2048]{2,0,1:T(1,128)} %param.11) | copy-start | bytes 172036
  8.5 93.5 %all-gather.11.cloned.1.call-start = ((), (), s32[]{:S(2)}) async-start(), calls=%async_computation.8 | async-start | bytes 3276800 | tf_op jit(solution)/shard_map/all_gather | solution.py:63
  12.5 4.9 %collective-permute-start = (f32[7,1024]{1,0:T(8,128)S(1)}, f32[7,1024]{1,0:T(8,128)S(1)}, u32[]{:S(2)}, u32[]{:S(2)}) collective-permute-start(f32[7,1024]{1,0:T(8,128)S(1)} %select_bitcast_fusion), channel_id=1, source_target_pairs={{0,1},{1,0},{2,3},{3,2},{4,5},{5,4},{6,7},{7,6},{8,9},{9,8},{10,11... | collective-permute-start | bytes 86024 | tf_op jit(solution)/shard_map/ppermute | solution.py:46
  19.2 56.2 %all-to-all-start = ((f32[32,2,7,1024]{3,1,2,0:T(2,128)}), f32[32,2,7,1024]{3,1,2,0:T(2,128)S(1)}, u32[]{:S(2)}, u32[]{:S(2)}) async-start(f32[32,2,7,1024]{3,1,2,0:T(2,128)} %broadcast_in_dim.46), calls=%async_computation | async-start | bytes 3670016 | tf_op jit(solution)/shard_map/all_to_all | solution.py:49
  30.8 94.6 %all-gather.5.cloned.1.call-start = ((), (), s32[]{:S(2)}) async-start(), calls=%async_computation.5 | async-start | bytes 3276800 | tf_op jit(solution)/shard_map/all_gather | solution.py:63
  32.4 50.8 %copy-start.6 = (f32[512]{0:T(512)S(1)}, f32[512]{0:T(512)}, u32[]{:S(2)}) copy-start(f32[512]{0:T(512)} %param.17) | copy-start | bytes 6148
  32.4 52.4 %copy-start.7 = (s32[1,2,224]{2,1,0:T(2,128)S(1)}, s32[1,2,224]{2,1,0:T(2,128)}, u32[]{:S(2)}) copy-start(s32[1,2,224]{2,1,0:T(2,128)} %param.14) | copy-start | bytes 5380
  32.4 52.4 %copy-start.8 = (f32[64]{0:T(128)S(1)}, f32[64]{0:T(128)}, u32[]{:S(2)}) copy-start(f32[64]{0:T(128)} %param.16) | copy-start | bytes 772
  80.7 13.3 %collective-permute-start.1 = (f32[32,7,512]{2,0,1:T(8,128)S(1)}, f32[32,7,512]{2,0,1:T(8,128)}, u32[]{:S(2)}, u32[]{:S(2)}) collective-permute-start(f32[32,7,512]{2,0,1:T(8,128)S(1)} %dynamic-slice_bitcast_fusion.2), channel_id=1, source_target_pairs={{0,1},{1,0},{2,3},{3,2},{4,5},{5,4},{6,7},{7,6},{8,9},{9,8},{10,11... | collective-permute-start | bytes 1376264 | tf_op jit(solution)/shard_map/ppermute | solution.py:70
  96.2 29.1 %all-to-all-start.1 = ((f32[32,7,512]{2,1,0:T(8,128)}), f32[32,7,512]{2,1,0:T(8,128)S(1)}, u32[]{:S(2)}, u32[]{:S(2)}) async-start(f32[32,7,512]{2,1,0:T(8,128)} %copy.56), calls=%async_computation.1 | async-start | bytes 1048576 | tf_op jit(solution)/shard_map/all_to_all | solution.py:72
  101.7 86.2 %all-gather.9.cloned.1.call-start = ((), (), s32[]{:S(2)}) async-start(), calls=%async_computation.7 | async-start | bytes 1310720 | tf_op jit(solution)/shard_map/all_gather | solution.py:63
  109.6 29.1 %collective-permute-start.2 = (f32[32,7,640]{2,0,1:T(8,128)}, f32[32,7,640]{2,0,1:T(8,128)}, u32[]{:S(2)}, u32[]{:S(2)}) collective-permute-start(f32[32,7,640]{2,0,1:T(8,128)} %dynamic-slice_bitcast_fusion.1), channel_id=1, source_target_pairs={{0,1},{1,0},{2,3},{3,2},{4,5},{5,4},{6,7},{7,6},{8,9},{9,8},{10,11... | collective-permute-start | bytes 1720328 | tf_op jit(solution)/shard_map/ppermute | solution.py:70
  125.4 7.0 %copy-start.3 = (f32[32,7,512]{2,1,0:T(8,128)}, f32[32,7,512]{2,1,0:T(8,128)S(1)}, u32[]{:S(2)}) copy-start(f32[32,7,512]{2,1,0:T(8,128)S(1)} %all-to-all-done.1) | copy-start | bytes 1376260
  132.4 1.0 copy-start.1
  134.2 15.5 %collective-permute-start.3 = (f32[32,7,640]{2,0,1:T(8,128)}, f32[32,7,640]{2,0,1:T(8,128)}, u32[]{:S(2)}, u32[]{:S(2)}) collective-permute-start(f32[32,7,640]{2,0,1:T(8,128)} %dynamic-slice_bitcast_fusion), channel_id=1, source_target_pairs={{0,1},{1,0},{2,3},{3,2},{4,5},{5,4},{6,7},{7,6},{8,9},{9,8},{10,11... | collective-permute-start | bytes 1720328 | tf_op jit(solution)/shard_map/ppermute | solution.py:70
  152.3 10.9 %copy-start.2 = (f32[32,7,640]{2,0,1:T(8,128)S(1)}, f32[32,7,640]{2,0,1:T(8,128)}, u32[]{:S(2)}) copy-start(f32[32,7,640]{2,0,1:T(8,128)} %get-tuple-element.29) | copy-start | bytes 1720324
  153.5 29.2 %all-to-all-start.2 = ((f32[32,7,640]{2,1,0:T(8,128)}), f32[32,7,640]{2,1,0:T(8,128)S(1)}, u32[]{:S(2)}, u32[]{:S(2)}) async-start(f32[32,7,640]{2,1,0:T(8,128)} %copy.59), calls=%async_computation.2 | async-start | bytes 1310720 | tf_op jit(solution)/shard_map/all_to_all | solution.py:72
  182.8 24.7 %all-to-all-start.3 = ((f32[32,7,640]{2,1,0:T(8,128)}), f32[32,7,640]{2,1,0:T(8,128)S(1)}, u32[]{:S(2)}, u32[]{:S(2)}) async-start(f32[32,7,640]{2,1,0:T(8,128)} %copy.61), calls=%async_computation.3 | async-start | bytes 1310720 | tf_op jit(solution)/shard_map/all_to_all | solution.py:72
  191.2 32.8 %copy-start.4 = (f32[32,7,512]{2,1,0:T(8,128)S(1)}, f32[32,7,512]{2,1,0:T(8,128)}, u32[]{:S(2)}) copy-start(f32[32,7,512]{2,1,0:T(8,128)} %copy-done.3) | copy-start | bytes 1376260
  191.2 14.1 %collective-permute-start.4 = (f32[32,7,256]{2,0,1:T(8,128)S(1)}, f32[32,7,256]{2,0,1:T(8,128)S(1)}, u32[]{:S(2)}, u32[]{:S(2)}) collective-permute-start(f32[32,7,256]{2,0,1:T(8,128)S(1)} %dynamic-slice_bitcast_fusion.3), channel_id=1, source_target_pairs={{0,1},{1,0},{2,3},{3,2},{4,5},{5,4},{6,7},{7,6},{8,9},{9,8},{10,11... | collective-permute-start | bytes 688136 | tf_op jit(solution)/shard_map/ppermute | solution.py:70
Sparse Core Ops, SparseCore 0:
  9.1 36.9 all-gather.6
  48.0 37.7 all-gather.10
  87.5 37.8 all-gather.4
  138.8 23.3 all-gather.8

commit v4 on v2

--- a/solution.py
+++ b/solution.py
@@ -53,22 +53,22 @@
     vir_local = lax.dynamic_slice_in_dim(vir_pairs, p * columns, columns, 1)
     vir_sum = pair_energies(vir_energy, vir_local)
 
+    occ_got = lax.ppermute(occ_sum, "gx", swap)
+    occ_both = jnp.where(gx == 0, jnp.stack([occ_sum, occ_got], 1), jnp.stack([occ_got, occ_sum], 1))
+
     w = columns // N_CHUNK
     outs = []
-    works = []
     for c in range(N_CHUNK):
         piece = lax.all_gather(integrals[:, c * w:(c + 1) * w], "gy", axis=0, tiled=True)
-        if c >= 1:
-            piece, works[c - 1] = lax.optimization_barrier((piece, works[c - 1]))
         if c >= 2:
             piece, outs[c - 2] = lax.optimization_barrier((piece, outs[c - 2]))
         part = jnp.dot(lhs, piece, precision=lax.Precision.HIGHEST, preferred_element_type=jnp.float32)
         part = part.reshape(npair, nx, rows_l, w)
-        keep = lax.dynamic_index_in_dim(part, gx, 1, keepdims=False)
-        send = lax.dynamic_index_in_dim(part, 1 - gx, 1, keepdims=False)
-        works.append(keep + lax.ppermute(send, "gx", swap))
-        payload = works[c] / (occ_sum[:, :, None] - vir_sum[None, None, c * w:(c + 1) * w])
-        outs.append(lax.all_to_all(payload, "pair", 0, 0, tiled=True))
+        payload = part / (occ_both[:, :, :, None] - vir_sum[None, None, None, c * w:(c + 1) * w])
+        payload = payload.reshape(npair * nx, rows_l, w)
+        outs.append(lax.all_to_all(payload, ("pair", "gx"), 0, 0, tiled=True))
+    outs = [o.reshape(npair, nx, rows_l, w) for o in outs]
+    outs = [o[:, 0] + o[:, 1] for o in outs]
     res = jnp.stack(outs, axis=2)
     res = jnp.transpose(res, (1, 0, 2, 3)).reshape(1, rows_l, npair * columns)
     return res

time: 223 us -> 237 us (1.063)
  waiting for transfers between devices: 96 us -> 127 us
  blocking collectives: 24.1 us -> 0 us
  local copies, waits for them, and re-layouts: 17.3 us -> 22.2 us
    all_to_all x3 -> x4, waiting for transfers between devices: 0.01 us -> 85 us  [on_device(): outs.append(lax.all_to_all(payload, ('pair', 'gx'), 0, 0, tiled=True))]
    ppermute x4 -> x1, waiting for transfers between devices: 51.9 us -> 1.11 us  [on_device(): occ_got = lax.ppermute(occ_sum, 'gx', swap)]
    all_to_all x1 -> x0, blocking collectives: 24.1 us -> none  [on_device(): outs.append(lax.all_to_all(payload, 'pair', 0, 0, tiled=True))]
    ppermute x4 -> x1, starting transfers between devices: 9.72 us -> 2.54 us  [on_device(): occ_got = lax.ppermute(occ_sum, 'gx', swap)]
    all_to_all x3 -> x4, starting transfers between devices: 21.1 us -> 27.9 us  [on_device(): outs.append(lax.all_to_all(payload, ('pair', 'gx'), 0, 0, tiled=True))]
    reshape x0 -> x4, local copies, waits for them, and re-layouts: none -> 6.12 us  [on_device(): payload = payload.reshape(npair * nx, rows_l, w)]
    div x4 -> x0, local copies, waits for them, and re-layouts: 3.49 us -> none  [on_device(): works[c] / (occ_sum[:, :, None] - vir_sum[None, None, c * w:(c + 1) * w])]
  transfers between devices with their start and end apart: 13 -> 11, of which waited for: 6 -> 8; matrix products, arithmetic and copies ran while one was open for 15% -> 16% of each run, Pallas kernels for 0% -> 0%
where the time goes in v4:
time: 237 us; the launch traced here: 235 us
  waiting for transfers between devices  127 us (54%)
  starting transfers between devices  45.8 us (19%)
  matrix products  22.4 us (9%)
  local copies, waits for them, and re-layouts  22.2 us (9%)
  between operations  13.5 us (6%)
  other arithmetic  4.35 us (2%)
    all_to_all x4, waiting for transfers between devices, on_device(): outs.append(lax.all_to_all(payload, ('pair', 'gx'), 0, 0, tiled=True))  85 us
    all_to_all x4, starting transfers between devices, on_device(): outs.append(lax.all_to_all(payload, ('pair', 'gx'), 0, 0, tiled=True))  27.9 us
    all_to_all x1, waiting for transfers between devices, on_device(): t_all = lax.all_to_all(spread, 'pair', 0, 0, tiled=True)  27.4 us
    dot_general x4, matrix products, on_device(): jnp.dot(lhs, piece, precision=lax.Precision.HIGHEST, preferred_element_ty...  22.4 us
    all_gather x4, waiting for transfers between devices, on_device(): lax.all_gather(integrals[:, c * w:(c + 1) * w], 'gy', axis=0, tiled=True)  12.4 us
    all_to_all x1, starting transfers between devices, on_device(): t_all = lax.all_to_all(spread, 'pair', 0, 0, tiled=True)  11.6 us
    reshape x4, local copies, waits for them, and re-layouts, on_device(): payload = payload.reshape(npair * nx, rows_l, w)  6.12 us
  transfers between devices with their start and end apart: 11, of which 8 were waited for; matrix products, arithmetic and copies ran while one was open for 16% of the time, Pallas kernels for 0%

profile of v4, /device:TPU:1, one launch (start us, length us, event | category | flops | bytes accessed | tf_op | source)
XLA Modules:
  0.0 234.8 jit_solution(10082254479967806319)
XLA Ops:
  6.5 2.9 %fusion.36 = (f32[256,512]{1,0:T(8,128)}, f32[256,512]{1,0:T(8,128)}, f32[256,512]{1,0:T(8,128)}, f32[256,512]{1,0:T(8,128)}) fusion(f32[256,2048]{1,0:T(8,128)} %param.12), kind=kLoop, calls=%fused_computation.60 | loop fusion | bytes 4194304 | tf_op jit(solution)/shard_map/slice | solution.py:62
  10.9 3.6 %collective-permute-start = (f32[7,1024]{1,0:T(8,128)S(1)}, f32[7,1024]{1,0:T(8,128)S(1)}, u32[]{:S(2)}, u32[]{:S(2)}) collective-permute-start(f32[7,1024]{1,0:T(8,128)S(1)} %select_bitcast_fusion), channel_id=1, source_target_pairs={{0,1},{1,0},{2,3},{3,2},{4,5},{5,4},{6,7},{7,6},{8,9},{9,8},{10,11... | collective-permute-start | bytes 86024 | tf_op jit(solution)/shard_map/ppermute | solution.py:46
  16.0 1.7 broadcast_in_dim.50
  17.7 11.6 %all-to-all-start = ((f32[32,2,7,1024]{3,1,2,0:T(2,128)}), f32[32,2,7,1024]{3,1,2,0:T(2,128)S(1)}, u32[]{:S(2)}, u32[]{:S(2)}) async-start(f32[32,2,7,1024]{3,1,2,0:T(2,128)} %broadcast_in_dim.50), calls=%async_computation | async-start | bytes 3670016 | tf_op jit(solution)/shard_map/all_to_all | solution.py:49
  29.6 2.5 %collective-permute-start.1 = (f32[32,7]{1,0:T(8,128)S(1)}, f32[32,7]{1,0:T(8,128)S(1)}, u32[]{:S(2)}, u32[]{:S(2)}) collective-permute-start(f32[32,7]{1,0:T(8,128)S(1)} %add.122), channel_id=1, source_target_pairs={{0,1},{1,0},{2,3},{3,2},{4,5},{5,4},{6,7},{7,6},{8,9},{9,8},{10,11... | collective-permute-start | bytes 2696 | tf_op jit(solution)/shard_map/ppermute | solution.py:56
  32.2 0.9 constant_dynamic-slice_fusion
  33.1 1.6 select_reduce_fusion
  34.9 1.1 collective-permute-done.1
  36.1 10.5 %all-gather.7.cloned.1.call-done = f32[1024,512]{1,0:T(8,128)} async-done(((f32[256,512]{1,0:T(8,128)}), f32[1024,512]{1,0:T(8,128)}) %all-gather.7.cloned.1.call-update) | async-done | bytes 2097168 | tf_op jit(solution)/shard_map/all_gather | solution.py:62
  46.6 27.4 %all-to-all-done = f32[32,2,7,1024]{3,1,2,0:T(2,128)S(1)} async-done(((f32[32,2,7,1024]{3,1,2,0:T(2,128)}), f32[32,2,7,1024]{3,1,2,0:T(2,128)S(1)}, u32[]{:S(2)}, u32[]{:S(2)}) %all-to-all-start) | async-done | bytes 1835040 | tf_op jit(solution)/shard_map/all_to_all | solution.py:49
  74.0 5.9 %fusion.12 = f32[32,2,7,512]{3,0,2,1:T(8,128)S(1)} fusion(f32[1024,512]{1,0:T(8,128)} %all-gather.7.cloned.1.call-done, f32[32,2,7,1024]{3,1,2,0:T(2,128)S(1)} %all-to-all-done, f32[512]{0:T(512)S(1)} %get-tuple-element.40, f32[32,2,7]{0,2,1:T(8,128)S(1)} %copy.105), kind=kOutput, calls=%fused_computation.21 | convolution fusion | flops 2819031040 | bytes 4853504 | tf_op jit(solution)/shard_map/dot_general | solution.py:65
  79.9 1.5 copy.133
  81.4 6.6 %all-to-all-start.1 = ((f32[64,7,512]{2,1,0:T(8,128)}), f32[64,7,512]{2,1,0:T(8,128)S(1)}, u32[]{:S(2)}, u32[]{:S(2)}) async-start(f32[64,7,512]{2,1,0:T(8,128)} %bitcast.14), calls=%async_computation.1 | async-start | bytes 2097152 | tf_op jit(solution)/shard_map/all_to_all | solution.py:69
  88.1 5.2 %fusion.17 = f32[32,2,7,512]{3,0,2,1:T(8,128)S(1)} fusion(f32[1024,512]{1,0:T(8,128)} %all-gather.11.cloned.1.call-done, f32[32,2,7,1024]{3,1,2,0:T(2,128)S(1)} %all-to-all-done, f32[512]{0:T(512)S(1)} %get-tuple-element.39, f32[32,2,7]{0,2,1:T(8,128)S(1)} %copy.105), kind=kOutput, calls=%fused_computation.22 | convolution fusion | flops 2819031040 | bytes 4853504 | tf_op jit(solution)/shard_map/dot_general | solution.py:65
  93.3 1.6 copy.135
  94.9 21.0 %all-to-all-done.1 = f32[64,7,512]{2,1,0:T(8,128)S(1)} async-done(((f32[64,7,512]{2,1,0:T(8,128)}), f32[64,7,512]{2,1,0:T(8,128)S(1)}, u32[]{:S(2)}, u32[]{:S(2)}) %all-to-all-start.1) | async-done | bytes 917536 | tf_op jit(solution)/shard_map/all_to_all | solution.py:69
  115.8 6.9 %all-to-all-start.2 = ((f32[64,7,512]{2,1,0:T(8,128)}), f32[64,7,512]{2,1,0:T(8,128)S(1)}, u32[]{:S(2)}, u32[]{:S(2)}) async-start(f32[64,7,512]{2,1,0:T(8,128)} %bitcast.18), calls=%async_computation.2 | async-start | bytes 2097152 | tf_op jit(solution)/shard_map/all_to_all | solution.py:69
  123.3 5.6 %fusion.22 = f32[32,2,7,512]{3,0,2,1:T(8,128)S(1)} fusion(f32[1024,512]{1,0:T(8,128)} %all-gather.5.cloned.1.call-done, f32[32,2,7,1024]{3,1,2,0:T(2,128)} %copy-done.2, f32[512]{0:T(512)S(1)} %get-tuple-element.37, f32[32,2,7]{0,2,1:T(8,128)S(1)} %copy.105), kind=kOutput, calls=%fused_computation.23 | convolution fusion | flops 2819031040 | bytes 4853504 | tf_op jit(solution)/shard_map/dot_general | solution.py:65
  128.9 1.5 copy.139
  130.5 20.0 %all-to-all-done.2 = f32[64,7,512]{2,1,0:T(8,128)S(1)} async-done(((f32[64,7,512]{2,1,0:T(8,128)}), f32[64,7,512]{2,1,0:T(8,128)S(1)}, u32[]{:S(2)}, u32[]{:S(2)}) %all-to-all-start.2) | async-done | bytes 917536 | tf_op jit(solution)/shard_map/all_to_all | solution.py:69
  150.5 6.9 %all-to-all-start.3 = ((f32[64,7,512]{2,1,0:T(8,128)}), f32[64,7,512]{2,1,0:T(8,128)S(1)}, u32[]{:S(2)}, u32[]{:S(2)}) async-start(f32[64,7,512]{2,1,0:T(8,128)} %bitcast.66), calls=%async_computation.3 | async-start | bytes 2097152 | tf_op jit(solution)/shard_map/all_to_all | solution.py:69
  157.3 1.9 all-gather.9.cloned.1.call-done
  159.3 5.6 %fusion.27 = f32[32,2,7,512]{3,0,2,1:T(8,128)S(1)} fusion(f32[1024,512]{1,0:T(8,128)} %all-gather.9.cloned.1.call-done, f32[32,2,7,1024]{3,1,2,0:T(2,128)} %copy-done.2, f32[512]{0:T(512)S(1)} %get-tuple-element.38, f32[32,2,7]{0,2,1:T(8,128)S(1)} %copy.105), kind=kOutput, calls=%fused_computation.24 | convolution fusion | flops 2819031040 | bytes 4853504 | tf_op jit(solution)/shard_map/dot_general | solution.py:65
  164.9 1.5 copy.143
  166.4 18.7 %all-to-all-done.3 = f32[64,7,512]{2,1,0:T(8,128)S(1)} async-done(((f32[64,7,512]{2,1,0:T(8,128)}), f32[64,7,512]{2,1,0:T(8,128)S(1)}, u32[]{:S(2)}, u32[]{:S(2)}) %all-to-all-start.3) | async-done | bytes 917536 | tf_op jit(solution)/shard_map/all_to_all | solution.py:69
  185.1 7.5 %all-to-all-start.4 = ((f32[64,7,512]{2,1,0:T(8,128)}), f32[64,7,512]{2,1,0:T(8,128)}, u32[]{:S(2)}, u32[]{:S(2)}) async-start(f32[64,7,512]{2,1,0:T(8,128)} %bitcast.65), calls=%async_computation.4 | async-start | bytes 2097152 | tf_op jit(solution)/shard_map/all_to_all | solution.py:69
  193.4 0.8 copy.191
  194.9 25.4 %all-to-all-done.4 = f32[64,7,512]{2,1,0:T(8,128)} async-done(((f32[64,7,512]{2,1,0:T(8,128)}), f32[64,7,512]{2,1,0:T(8,128)}, u32[]{:S(2)}, u32[]{:S(2)}) %all-to-all-start.4) | async-done | bytes 917536 | tf_op jit(solution)/shard_map/all_to_all | solution.py:69
  220.3 1.3 fusion.40
  221.6 1.0 fusion.32
  222.8 1.2 copy.127
  224.0 4.2 %reshape.283 = f32[1,7,65536]{2,0,1:T(1,128)} reshape(f32[7,32,4,512]{3,2,1,0:T(4,128)S(1)} %copy.127) | data formatting | bytes 3670016 | tf_op jit(solution)/shard_map/reshape | solution.py:73
  (59 shorter events, 5.6 us)
Async XLA Ops:
  6.5 3.1 %copy-start = (s32[16]{0:T(128)S(1)}, s32[16]{0:T(128)}, u32[]{:S(2)}) copy-start(s32[16]{0:T(128)} %param.13) | copy-start | bytes 196
  6.5 3.0 %copy-start.3 = (f32[1,7,2048]{2,0,1:T(1,128)S(1)}, f32[1,7,2048]{2,0,1:T(1,128)}, u32[]{:S(2)}) copy-start(f32[1,7,2048]{2,0,1:T(1,128)} %param.11) | copy-start | bytes 172036
  6.5 40.0 %all-gather.7.cloned.1.call-start = ((), (), s32[]{:S(2)}) async-start(), calls=%async_computation.6 | async-start | bytes 2621440 | tf_op jit(solution)/shard_map/all_gather | solution.py:62
  9.5 78.6 %all-gather.11.cloned.1.call-start = ((), (), s32[]{:S(2)}) async-start(), calls=%async_computation.8 | async-start | bytes 2621440 | tf_op jit(solution)/shard_map/all_gather | solution.py:62
  10.9 5.0 %collective-permute-start = (f32[7,1024]{1,0:T(8,128)S(1)}, f32[7,1024]{1,0:T(8,128)S(1)}, u32[]{:S(2)}, u32[]{:S(2)}) collective-permute-start(f32[7,1024]{1,0:T(8,128)S(1)} %select_bitcast_fusion), channel_id=1, source_target_pairs={{0,1},{1,0},{2,3},{3,2},{4,5},{5,4},{6,7},{7,6},{8,9},{9,8},{10,11... | collective-permute-start | bytes 86024 | tf_op jit(solution)/shard_map/ppermute | solution.py:46
  17.7 11.7 %copy-start.5 = (s32[1,2,224]{2,1,0:T(2,128)S(1)}, s32[1,2,224]{2,1,0:T(2,128)}, u32[]{:S(2)}) copy-start(s32[1,2,224]{2,1,0:T(2,128)} %param.14) | copy-start | bytes 5380
  17.7 11.7 %copy-start.6 = (f32[64]{0:T(128)S(1)}, f32[64]{0:T(128)}, u32[]{:S(2)}) copy-start(f32[64]{0:T(128)} %param.16) | copy-start | bytes 772
  17.7 15.4 %copy-start.4 = (f32[512]{0:T(512)S(1)}, f32[512]{0:T(512)}, u32[]{:S(2)}) copy-start(f32[512]{0:T(512)} %param.17) | copy-start | bytes 6148
  17.7 56.3 %all-to-all-start = ((f32[32,2,7,1024]{3,1,2,0:T(2,128)}), f32[32,2,7,1024]{3,1,2,0:T(2,128)S(1)}, u32[]{:S(2)}, u32[]{:S(2)}) async-start(f32[32,2,7,1024]{3,1,2,0:T(2,128)} %broadcast_in_dim.50), calls=%async_computation | async-start | bytes 3670016 | tf_op jit(solution)/shard_map/all_to_all | solution.py:49
  29.3 93.9 %all-gather.5.cloned.1.call-start = ((), (), s32[]{:S(2)}) async-start(), calls=%async_computation.5 | async-start | bytes 2621440 | tf_op jit(solution)/shard_map/all_gather | solution.py:62
  29.6 6.3 %collective-permute-start.1 = (f32[32,7]{1,0:T(8,128)S(1)}, f32[32,7]{1,0:T(8,128)S(1)}, u32[]{:S(2)}, u32[]{:S(2)}) collective-permute-start(f32[32,7]{1,0:T(8,128)S(1)} %add.122), channel_id=1, source_target_pairs={{0,1},{1,0},{2,3},{3,2},{4,5},{5,4},{6,7},{7,6},{8,9},{9,8},{10,11... | collective-permute-start | bytes 2696 | tf_op jit(solution)/shard_map/ppermute | solution.py:56
  74.0 14.1 %copy-start.2 = (f32[32,2,7,1024]{3,1,2,0:T(2,128)}, f32[32,2,7,1024]{3,1,2,0:T(2,128)S(1)}, u32[]{:S(2)}) copy-start(f32[32,2,7,1024]{3,1,2,0:T(2,128)S(1)} %all-to-all-done) | copy-start | bytes 5505028
  81.4 34.4 %all-to-all-start.1 = ((f32[64,7,512]{2,1,0:T(8,128)}), f32[64,7,512]{2,1,0:T(8,128)S(1)}, u32[]{:S(2)}, u32[]{:S(2)}) async-start(f32[64,7,512]{2,1,0:T(8,128)} %bitcast.14), calls=%async_computation.1 | async-start | bytes 2097152 | tf_op jit(solution)/shard_map/all_to_all | solution.py:69
  115.8 34.6 %all-to-all-start.2 = ((f32[64,7,512]{2,1,0:T(8,128)}), f32[64,7,512]{2,1,0:T(8,128)S(1)}, u32[]{:S(2)}, u32[]{:S(2)}) async-start(f32[64,7,512]{2,1,0:T(8,128)} %bitcast.18), calls=%async_computation.2 | async-start | bytes 2097152 | tf_op jit(solution)/shard_map/all_to_all | solution.py:69
  122.7 36.6 %all-gather.9.cloned.1.call-start = ((), (), s32[]{:S(2)}) async-start(), calls=%async_computation.7 | async-start | bytes 2621440 | tf_op jit(solution)/shard_map/all_gather | solution.py:62
  150.5 34.6 %all-to-all-start.3 = ((f32[64,7,512]{2,1,0:T(8,128)}), f32[64,7,512]{2,1,0:T(8,128)S(1)}, u32[]{:S(2)}, u32[]{:S(2)}) async-start(f32[64,7,512]{2,1,0:T(8,128)} %bitcast.66), calls=%async_computation.3 | async-start | bytes 2097152 | tf_op jit(solution)/shard_map/all_to_all | solution.py:69
  185.1 35.2 %all-to-all-start.4 = ((f32[64,7,512]{2,1,0:T(8,128)}), f32[64,7,512]{2,1,0:T(8,128)}, u32[]{:S(2)}, u32[]{:S(2)}) async-start(f32[64,7,512]{2,1,0:T(8,128)} %bitcast.65), calls=%async_computation.4 | async-start | bytes 2097152 | tf_op jit(solution)/shard_map/all_to_all | solution.py:69
  221.6 1.0 copy-start.1
Sparse Core Ops, SparseCore 0:
  9.6 36.9 all-gather.6
  48.4 33.3 all-gather.10
  83.6 33.3 all-gather.4
  125.0 34.2 all-gather.8

commit v5 on v2

--- a/solution.py
+++ b/solution.py
@@ -62,7 +62,7 @@
             piece, works[c - 1] = lax.optimization_barrier((piece, works[c - 1]))
         if c >= 2:
             piece, outs[c - 2] = lax.optimization_barrier((piece, outs[c - 2]))
-        part = jnp.dot(lhs, piece, precision=lax.Precision.HIGHEST, preferred_element_type=jnp.float32)
+        part = jnp.dot(lhs, piece, precision=lax.Precision.HIGH, preferred_element_type=jnp.float32)
         part = part.reshape(npair, nx, rows_l, w)
         keep = lax.dynamic_index_in_dim(part, gx, 1, keepdims=False)
         send = lax.dynamic_index_in_dim(part, 1 - gx, 1, keepdims=False)

time: 223 us -> 221 us (level)
  matrix products: 20.9 us -> 14.8 us
  waiting for transfers between devices: 96 us -> 99.7 us
    dot_general x4, matrix products: 20.9 us -> 14.8 us  [on_device(): jnp.dot(lhs, piece, precision=lax.Precision.HIGH, preferred_element_type=...]
    ppermute x4, waiting for transfers between devices: 51.9 us -> 54.7 us  [on_device(): works.append(keep + lax.ppermute(send, 'gx', swap))]
  transfers between devices with their start and end apart: 13 -> 13, of which waited for: 6 -> 7; matrix products, arithmetic and copies ran while one was open for 15% -> 12% of each run, Pallas kernels for 0% -> 0%
where the time goes in v5:
time: 221 us; the launch traced here: 220 us
  waiting for transfers between devices  99.7 us (45%)
  starting transfers between devices  47.2 us (21%)
  blocking collectives  23.6 us (11%)
  local copies, waits for them, and re-layouts  17.3 us (8%)
  matrix products  14.8 us (7%)
  between operations  13.5 us (6%)
  other arithmetic  3.74 us (2%)
    ppermute x4, waiting for transfers between devices, on_device(): works.append(keep + lax.ppermute(send, 'gx', swap))  54.7 us
    all_to_all x1, waiting for transfers between devices, on_device(): t_all = lax.all_to_all(spread, 'pair', 0, 0, tiled=True)  28.1 us
    all_to_all x1, blocking collectives, on_device(): outs.append(lax.all_to_all(payload, 'pair', 0, 0, tiled=True))  23.6 us
    all_to_all x3, starting transfers between devices, on_device(): outs.append(lax.all_to_all(payload, 'pair', 0, 0, tiled=True))  21.6 us
    all_gather x4, waiting for transfers between devices, on_device(): lax.all_gather(integrals[:, c * w:(c + 1) * w], 'gy', axis=0, tiled=True)  15.7 us
    dot_general x4, matrix products, on_device(): jnp.dot(lhs, piece, precision=lax.Precision.HIGH, preferred_element_type=...  14.8 us
    all_to_all x1, starting transfers between devices, on_device(): t_all = lax.all_to_all(spread, 'pair', 0, 0, tiled=True)  11.7 us
    ppermute x4, starting transfers between devices, on_device(): works.append(keep + lax.ppermute(send, 'gx', swap))  10.2 us
  transfers between devices with their start and end apart: 13, of which 7 were waited for; matrix products, arithmetic and copies ran while one was open for 12% of the time, Pallas kernels for 0%

profile of v5, /device:TPU:1, one launch (start us, length us, event | category | flops | bytes accessed | tf_op | source)
XLA Modules:
  0.0 220.0 jit_solution(11946066768691317837)
XLA Ops:
  6.5 3.0 %fusion.14 = (f32[256,512]{1,0:T(8,128)}, f32[256,512]{1,0:T(8,128)}, f32[256,512]{1,0:T(8,128)}, f32[256,512]{1,0:T(8,128)}) fusion(f32[256,2048]{1,0:T(8,128)} %param.12), kind=kLoop, calls=%fused_computation.59 | loop fusion | bytes 4194304 | tf_op jit(solution)/shard_map/slice | solution.py:60
  9.6 0.7 all-gather.7.cloned.1.call-update
  11.8 3.6 %collective-permute-start = (f32[7,1024]{1,0:T(8,128)S(1)}, f32[7,1024]{1,0:T(8,128)S(1)}, u32[]{:S(2)}, u32[]{:S(2)}) collective-permute-start(f32[7,1024]{1,0:T(8,128)S(1)} %select_bitcast_fusion), channel_id=1, source_target_pairs={{0,1},{1,0},{2,3},{3,2},{4,5},{5,4},{6,7},{7,6},{8,9},{9,8},{10,11... | collective-permute-start | bytes 86024 | tf_op jit(solution)/shard_map/ppermute | solution.py:46
  16.8 1.7 broadcast_in_dim.46
  18.5 11.7 %all-to-all-start = ((f32[32,2,7,1024]{3,1,2,0:T(2,128)}), f32[32,2,7,1024]{3,1,2,0:T(2,128)S(1)}, u32[]{:S(2)}, u32[]{:S(2)}) async-start(f32[32,2,7,1024]{3,1,2,0:T(2,128)} %broadcast_in_dim.46), calls=%async_computation | async-start | bytes 3670016 | tf_op jit(solution)/shard_map/all_to_all | solution.py:49
  31.1 0.9 constant_dynamic-slice_fusion
  32.0 14.7 %all-gather.9.cloned.1.call-done = f32[1024,512]{1,0:T(8,128)} async-done(((f32[256,512]{1,0:T(8,128)}), f32[1024,512]{1,0:T(8,128)}) %all-gather.9.cloned.1.call-update) | async-done | bytes 2097168 | tf_op jit(solution)/shard_map/all_gather | solution.py:60
  46.7 28.1 %all-to-all-done = f32[32,2,7,1024]{3,1,2,0:T(2,128)S(1)} async-done(((f32[32,2,7,1024]{3,1,2,0:T(2,128)}), f32[32,2,7,1024]{3,1,2,0:T(2,128)S(1)}, u32[]{:S(2)}, u32[]{:S(2)}) %all-to-all-start) | async-done | bytes 1835040 | tf_op jit(solution)/shard_map/all_to_all | solution.py:49
  74.8 3.7 %fusion.6 = f32[32,2,7,512]{3,0,2,1:T(8,128)S(1)} fusion(f32[1024,512]{1,0:T(8,128)} %all-gather.9.cloned.1.call-done, f32[32,2,7,1024]{3,1,2,0:T(2,128)S(1)} %all-to-all-done), kind=kOutput, calls=%fused_computation.15 | convolution fusion | flops 1409286144 | bytes 4849664 | tf_op jit(solution)/shard_map/dot_general | solution.py:65
  78.6 2.5 %collective-permute-start.1 = (f32[32,7,512]{2,0,1:T(8,128)S(1)}, f32[32,7,512]{2,0,1:T(8,128)}, u32[]{:S(2)}, u32[]{:S(2)}) collective-permute-start(f32[32,7,512]{2,0,1:T(8,128)S(1)} %dynamic-slice_bitcast_fusion.3), channel_id=1, source_target_pairs={{0,1},{1,0},{2,3},{3,2},{4,5},{5,4},{6,7},{7,6},{8,9},{9,8},{10,11... | collective-permute-start | bytes 1376264 | tf_op jit(solution)/shard_map/ppermute | solution.py:69
  81.1 1.6 select_reduce_fusion
  82.7 9.2 %collective-permute-done.1 = f32[32,7,512]{2,0,1:T(8,128)} collective-permute-done((f32[32,7,512]{2,0,1:T(8,128)S(1)}, f32[32,7,512]{2,0,1:T(8,128)}, u32[]{:S(2)}, u32[]{:S(2)}) %collective-permute-start.1) | collective-permute-done | bytes 458784 | tf_op jit(solution)/shard_map/ppermute | solution.py:69
  91.9 1.2 subtract_divide_fusion.2
  93.1 1.1 copy.60
  94.2 5.5 %all-to-all-start.1 = ((f32[32,7,512]{2,1,0:T(8,128)}), f32[32,7,512]{2,1,0:T(8,128)S(1)}, u32[]{:S(2)}, u32[]{:S(2)}) async-start(f32[32,7,512]{2,1,0:T(8,128)} %copy.60), calls=%async_computation.1 | async-start | bytes 1048576 | tf_op jit(solution)/shard_map/all_to_all | solution.py:71
  99.6 3.7 %fusion.4 = f32[32,2,7,512]{3,0,2,1:T(8,128)S(1)} fusion(f32[1024,512]{1,0:T(8,128)} %all-gather.7.cloned.1.call-done, f32[32,2,7,1024]{3,1,2,0:T(2,128)S(1)} %all-to-all-done), kind=kOutput, calls=%fused_computation.13 | convolution fusion | flops 1409286144 | bytes 4849664 | tf_op jit(solution)/shard_map/dot_general | solution.py:65
  103.4 2.5 %collective-permute-start.2 = (f32[32,7,512]{2,0,1:T(8,128)S(1)}, f32[32,7,512]{2,0,1:T(8,128)S(1)}, u32[]{:S(2)}, u32[]{:S(2)}) collective-permute-start(f32[32,7,512]{2,0,1:T(8,128)S(1)} %dynamic-slice_bitcast_fusion.2), channel_id=1, source_target_pairs={{0,1},{1,0},{2,3},{3,2},{4,5},{5,4},{6,7},{7,6},{8,9},{9,8},{10,11... | collective-permute-start | bytes 1376264 | tf_op jit(solution)/shard_map/ppermute | solution.py:69
  105.9 15.3 %collective-permute-done.2 = f32[32,7,512]{2,0,1:T(8,128)S(1)} collective-permute-done((f32[32,7,512]{2,0,1:T(8,128)S(1)}, f32[32,7,512]{2,0,1:T(8,128)S(1)}, u32[]{:S(2)}, u32[]{:S(2)}) %collective-permute-start.2) | collective-permute-done | bytes 458784 | tf_op jit(solution)/shard_map/ppermute | solution.py:69
  121.4 1.1 copy.62
  122.5 7.2 %all-to-all-start.2 = ((f32[32,7,512]{2,1,0:T(8,128)}), f32[32,7,512]{2,1,0:T(8,128)S(1)}, u32[]{:S(2)}, u32[]{:S(2)}) async-start(f32[32,7,512]{2,1,0:T(8,128)} %copy.62), calls=%async_computation.2 | async-start | bytes 1048576 | tf_op jit(solution)/shard_map/all_to_all | solution.py:71
  129.7 3.8 %fusion.2 = f32[32,2,7,512]{3,0,2,1:T(8,128)S(1)} fusion(f32[1024,512]{1,0:T(8,128)} %all-gather.5.cloned.1.call-done, f32[32,2,7,1024]{3,1,2,0:T(2,128)S(1)} %all-to-all-done), kind=kOutput, calls=%fused_computation.11 | convolution fusion | flops 1409286144 | bytes 4849664 | tf_op jit(solution)/shard_map/dot_general | solution.py:65
  133.5 2.7 %collective-permute-start.3 = (f32[32,7,512]{2,0,1:T(8,128)S(1)}, f32[32,7,512]{2,0,1:T(8,128)S(1)}, u32[]{:S(2)}, u32[]{:S(2)}) collective-permute-start(f32[32,7,512]{2,0,1:T(8,128)S(1)} %dynamic-slice_bitcast_fusion.1), channel_id=1, source_target_pairs={{0,1},{1,0},{2,3},{3,2},{4,5},{5,4},{6,7},{7,6},{8,9},{9,8},{10,11... | collective-permute-start | bytes 1376264 | tf_op jit(solution)/shard_map/ppermute | solution.py:69
  136.2 14.9 %collective-permute-done.3 = f32[32,7,512]{2,0,1:T(8,128)S(1)} collective-permute-done((f32[32,7,512]{2,0,1:T(8,128)S(1)}, f32[32,7,512]{2,0,1:T(8,128)S(1)}, u32[]{:S(2)}, u32[]{:S(2)}) %collective-permute-start.3) | collective-permute-done | bytes 458784 | tf_op jit(solution)/shard_map/ppermute | solution.py:69
  151.3 0.9 all-gather.11.cloned.1.call-done
  152.2 1.1 copy.63
  153.3 8.9 %all-to-all-start.3 = ((f32[32,7,512]{2,1,0:T(8,128)}), f32[32,7,512]{2,1,0:T(8,128)S(1)}, u32[]{:S(2)}, u32[]{:S(2)}) async-start(f32[32,7,512]{2,1,0:T(8,128)} %copy.63), calls=%async_computation.3 | async-start | bytes 1048576 | tf_op jit(solution)/shard_map/all_to_all | solution.py:71
  162.2 3.7 %fusion = f32[32,2,7,512]{3,0,2,1:T(8,128)S(1)} fusion(f32[1024,512]{1,0:T(8,128)} %all-gather.11.cloned.1.call-done, f32[32,2,7,1024]{3,1,2,0:T(2,128)S(1)} %all-to-all-done), kind=kOutput, calls=%fused_computation.9 | convolution fusion | flops 1409286144 | bytes 4849664 | tf_op jit(solution)/shard_map/dot_general | solution.py:65
  165.9 2.5 %collective-permute-start.4 = (f32[32,7,512]{2,0,1:T(8,128)S(1)}, f32[32,7,512]{2,0,1:T(8,128)S(1)}, u32[]{:S(2)}, u32[]{:S(2)}) collective-permute-start(f32[32,7,512]{2,0,1:T(8,128)S(1)} %dynamic-slice_bitcast_fusion), channel_id=1, source_target_pairs={{0,1},{1,0},{2,3},{3,2},{4,5},{5,4},{6,7},{7,6},{8,9},{9,8},{10,11... | collective-permute-start | bytes 1376264 | tf_op jit(solution)/shard_map/ppermute | solution.py:69
  168.4 15.3 %collective-permute-done.4 = f32[32,7,512]{2,0,1:T(8,128)S(1)} collective-permute-done((f32[32,7,512]{2,0,1:T(8,128)S(1)}, f32[32,7,512]{2,0,1:T(8,128)S(1)}, u32[]{:S(2)}, u32[]{:S(2)}) %collective-permute-start.4) | collective-permute-done | bytes 458784 | tf_op jit(solution)/shard_map/ppermute | solution.py:69
  184.2 23.6 %all_to_all.25 = f32[32,7,512]{2,1,0:T(8,128)S(1)} all-to-all(f32[32,7,512]{2,1,0:T(8,128)S(1)} %copy.65), channel_id=1, replica_groups=mesh['pair'=32,'gy'=4,'gx'=2] {'pair'}, dimensions={0} | all-to-all | bytes 917504 | tf_op jit(solution)/shard_map/all_to_all | solution.py:71
  208.0 1.2 copy.66
  209.2 4.2 %reshape.134 = f32[1,7,65536]{2,0,1:T(1,128)} reshape(f32[7,32,4,512]{3,2,1,0:T(4,128)S(1)} %copy.66) | data formatting | bytes 3670016 | tf_op jit(solution)/shard_map/reshape | solution.py:73
  (55 shorter events, 4.8 us)
Async XLA Ops:
  6.5 3.9 %copy-start = (s32[16]{0:T(128)S(1)}, s32[16]{0:T(128)}, u32[]{:S(2)}) copy-start(s32[16]{0:T(128)} %param.13) | copy-start | bytes 196
  6.5 3.8 %copy-start.1 = (f32[1,7,2048]{2,0,1:T(1,128)S(1)}, f32[1,7,2048]{2,0,1:T(1,128)}, u32[]{:S(2)}) copy-start(f32[1,7,2048]{2,0,1:T(1,128)} %param.11) | copy-start | bytes 172036
  6.5 40.2 %all-gather.9.cloned.1.call-start = ((), (), s32[]{:S(2)}) async-start(), calls=%async_computation.7 | async-start | bytes 2621440 | tf_op jit(solution)/shard_map/all_gather | solution.py:60
  9.6 83.5 %all-gather.7.cloned.1.call-start = ((), (), s32[]{:S(2)}) async-start(), calls=%async_computation.6 | async-start | bytes 2621440 | tf_op jit(solution)/shard_map/all_gather | solution.py:60
  10.3 111.0 %all-gather.5.cloned.1.call-start = ((), (), s32[]{:S(2)}) async-start(), calls=%async_computation.5 | async-start | bytes 2621440 | tf_op jit(solution)/shard_map/all_gather | solution.py:60
  11.8 5.0 %collective-permute-start = (f32[7,1024]{1,0:T(8,128)S(1)}, f32[7,1024]{1,0:T(8,128)S(1)}, u32[]{:S(2)}, u32[]{:S(2)}) collective-permute-start(f32[7,1024]{1,0:T(8,128)S(1)} %select_bitcast_fusion), channel_id=1, source_target_pairs={{0,1},{1,0},{2,3},{3,2},{4,5},{5,4},{6,7},{7,6},{8,9},{9,8},{10,11... | collective-permute-start | bytes 86024 | tf_op jit(solution)/shard_map/ppermute | solution.py:46
  18.5 12.3 %copy-start.3 = (s32[1,2,224]{2,1,0:T(2,128)S(1)}, s32[1,2,224]{2,1,0:T(2,128)}, u32[]{:S(2)}) copy-start(s32[1,2,224]{2,1,0:T(2,128)} %param.14) | copy-start | bytes 5380
  18.5 12.3 %copy-start.4 = (f32[64]{0:T(128)S(1)}, f32[64]{0:T(128)}, u32[]{:S(2)}) copy-start(f32[64]{0:T(128)} %param.16) | copy-start | bytes 772
  18.5 56.3 %all-to-all-start = ((f32[32,2,7,1024]{3,1,2,0:T(2,128)}), f32[32,2,7,1024]{3,1,2,0:T(2,128)S(1)}, u32[]{:S(2)}, u32[]{:S(2)}) async-start(f32[32,2,7,1024]{3,1,2,0:T(2,128)} %broadcast_in_dim.46), calls=%async_computation | async-start | bytes 3670016 | tf_op jit(solution)/shard_map/all_to_all | solution.py:49
  30.2 122.0 %all-gather.11.cloned.1.call-start = ((), (), s32[]{:S(2)}) async-start(), calls=%async_computation.8 | async-start | bytes 2621440 | tf_op jit(solution)/shard_map/all_gather | solution.py:60
  32.0 49.1 %copy-start.2 = (f32[512]{0:T(512)S(1)}, f32[512]{0:T(512)}, u32[]{:S(2)}) copy-start(f32[512]{0:T(512)} %param.17) | copy-start | bytes 6148
  78.6 13.3 %collective-permute-start.1 = (f32[32,7,512]{2,0,1:T(8,128)S(1)}, f32[32,7,512]{2,0,1:T(8,128)}, u32[]{:S(2)}, u32[]{:S(2)}) collective-permute-start(f32[32,7,512]{2,0,1:T(8,128)S(1)} %dynamic-slice_bitcast_fusion.3), channel_id=1, source_target_pairs={{0,1},{1,0},{2,3},{3,2},{4,5},{5,4},{6,7},{7,6},{8,9},{9,8},{10,11... | collective-permute-start | bytes 1376264 | tf_op jit(solution)/shard_map/ppermute | solution.py:69
  94.2 28.3 %all-to-all-start.1 = ((f32[32,7,512]{2,1,0:T(8,128)}), f32[32,7,512]{2,1,0:T(8,128)S(1)}, u32[]{:S(2)}, u32[]{:S(2)}) async-start(f32[32,7,512]{2,1,0:T(8,128)} %copy.60), calls=%async_computation.1 | async-start | bytes 1048576 | tf_op jit(solution)/shard_map/all_to_all | solution.py:71
  103.4 17.8 %collective-permute-start.2 = (f32[32,7,512]{2,0,1:T(8,128)S(1)}, f32[32,7,512]{2,0,1:T(8,128)S(1)}, u32[]{:S(2)}, u32[]{:S(2)}) collective-permute-start(f32[32,7,512]{2,0,1:T(8,128)S(1)} %dynamic-slice_bitcast_fusion.2), channel_id=1, source_target_pairs={{0,1},{1,0},{2,3},{3,2},{4,5},{5,4},{6,7},{7,6},{8,9},{9,8},{10,11... | collective-permute-start | bytes 1376264 | tf_op jit(solution)/shard_map/ppermute | solution.py:69
  122.5 29.8 %all-to-all-start.2 = ((f32[32,7,512]{2,1,0:T(8,128)}), f32[32,7,512]{2,1,0:T(8,128)S(1)}, u32[]{:S(2)}, u32[]{:S(2)}) async-start(f32[32,7,512]{2,1,0:T(8,128)} %copy.62), calls=%async_computation.2 | async-start | bytes 1048576 | tf_op jit(solution)/shard_map/all_to_all | solution.py:71
  133.5 17.6 %collective-permute-start.3 = (f32[32,7,512]{2,0,1:T(8,128)S(1)}, f32[32,7,512]{2,0,1:T(8,128)S(1)}, u32[]{:S(2)}, u32[]{:S(2)}) collective-permute-start(f32[32,7,512]{2,0,1:T(8,128)S(1)} %dynamic-slice_bitcast_fusion.1), channel_id=1, source_target_pairs={{0,1},{1,0},{2,3},{3,2},{4,5},{5,4},{6,7},{7,6},{8,9},{9,8},{10,11... | collective-permute-start | bytes 1376264 | tf_op jit(solution)/shard_map/ppermute | solution.py:69
  153.3 30.9 %all-to-all-start.3 = ((f32[32,7,512]{2,1,0:T(8,128)}), f32[32,7,512]{2,1,0:T(8,128)S(1)}, u32[]{:S(2)}, u32[]{:S(2)}) async-start(f32[32,7,512]{2,1,0:T(8,128)} %copy.63), calls=%async_computation.3 | async-start | bytes 1048576 | tf_op jit(solution)/shard_map/all_to_all | solution.py:71
  165.9 17.8 %collective-permute-start.4 = (f32[32,7,512]{2,0,1:T(8,128)S(1)}, f32[32,7,512]{2,0,1:T(8,128)S(1)}, u32[]{:S(2)}, u32[]{:S(2)}) collective-permute-start(f32[32,7,512]{2,0,1:T(8,128)S(1)} %dynamic-slice_bitcast_fusion), channel_id=1, source_target_pairs={{0,1},{1,0},{2,3},{3,2},{4,5},{5,4},{6,7},{7,6},{8,9},{9,8},{10,11... | collective-permute-start | bytes 1376264 | tf_op jit(solution)/shard_map/ppermute | solution.py:69
Sparse Core Ops, SparseCore 0:
  9.7 36.9 all-gather.8
  48.5 33.3 all-gather.6
  83.7 33.3 all-gather.4
  118.8 33.3 all-gather.10

commit v6 on v3

--- a/solution.py
+++ b/solution.py
@@ -4,7 +4,7 @@
 from jax import lax
 from jax.sharding import Mesh, PartitionSpec as P
 
-CHUNK_PARTS = (4, 5, 5, 2)
+CHUNK_PARTS = (6, 5, 5)
 
 
 def lookup(energy, idx):
@@ -61,9 +61,11 @@
         lo, hi = int(bounds[c]), int(bounds[c + 1])
         w = hi - lo
         piece = lax.all_gather(integrals[:, lo:hi], "gy", axis=0, tiled=True)
+        if c >= 1:
+            piece, works[c - 1] = lax.optimization_barrier((piece, works[c - 1]))
         if c >= 2:
             piece, outs[c - 2] = lax.optimization_barrier((piece, outs[c - 2]))
-        part = jnp.dot(lhs, piece, precision=lax.Precision.HIGHEST, preferred_element_type=jnp.float32)
+        part = jnp.dot(lhs, piece, precision=lax.Precision.HIGH, preferred_element_type=jnp.float32)
         part = part.reshape(npair, nx, rows_l, w)
         keep = lax.dynamic_index_in_dim(part, gx, 1, keepdims=False)
         send = lax.dynamic_index_in_dim(part, 1 - gx, 1, keepdims=False)

time: 235 us -> 208 us (0.89)
  waiting for transfers between devices: 109 us -> 95.8 us
  blocking collectives: 16.5 us -> 27 us
  starting transfers between devices: 46 us -> 37.2 us
  matrix products: 22.3 us -> 14.4 us
  local copies, waits for them, and re-layouts: 20.8 us -> 15.7 us
    all_gather x4 -> x3, waiting for transfers between devices: 27 us -> 0.56 us  [on_device(): piece = lax.all_gather(integrals[:, lo:hi], 'gy', axis=0, tiled=True)]
    all_to_all x3 -> x2, waiting for transfers between devices: 20.2 us -> 0.01 us  [on_device(): outs.append(lax.all_to_all(payload, 'pair', 0, 0, tiled=True))]
    ppermute x4 -> x3, waiting for transfers between devices: 31.6 us -> 50.7 us  [on_device(): works.append(keep + lax.ppermute(send, 'gx', swap))]
    all_to_all x1, waiting for transfers between devices: 29.3 us -> 43.8 us  [on_device(): t_all = lax.all_to_all(spread, 'pair', 0, 0, tiled=True)]
    all_to_all x1, blocking collectives: 16.5 us -> 27 us  [on_device(): outs.append(lax.all_to_all(payload, 'pair', 0, 0, tiled=True))]
    dot_general x4 -> x3, matrix products: 22.3 us -> 14.4 us  [on_device(): jnp.dot(lhs, piece, precision=lax.Precision.HIGH, preferred_element_type=...]
    all_to_all x3 -> x2, starting transfers between devices: 20.3 us -> 14.6 us  [on_device(): outs.append(lax.all_to_all(payload, 'pair', 0, 0, tiled=True))]
    ppermute x4 -> x3, starting transfers between devices: 10.2 us -> 7.39 us  [on_device(): works.append(keep + lax.ppermute(send, 'gx', swap))]
  transfers between devices with their start and end apart: 13 -> 10, of which waited for: 8 -> 5; matrix products, arithmetic and copies ran while one was open for 18% -> 14% of each run, Pallas kernels for 0% -> 0%
where the time goes in v6:
time: 208 us; the launch traced here: 207 us
  waiting for transfers between devices  95.8 us (46%)
  starting transfers between devices  37.2 us (18%)
  blocking collectives  27 us (13%)
  local copies, waits for them, and re-layouts  15.7 us (8%)
  matrix products  14.4 us (7%)
  between operations  13.4 us (6%)
  other arithmetic  3.8 us (2%)
    ppermute x3, waiting for transfers between devices, on_device(): works.append(keep + lax.ppermute(send, 'gx', swap))  50.7 us
    all_to_all x1, waiting for transfers between devices, on_device(): t_all = lax.all_to_all(spread, 'pair', 0, 0, tiled=True)  43.8 us
    all_to_all x1, blocking collectives, on_device(): outs.append(lax.all_to_all(payload, 'pair', 0, 0, tiled=True))  27 us
    all_to_all x2, starting transfers between devices, on_device(): outs.append(lax.all_to_all(payload, 'pair', 0, 0, tiled=True))  14.6 us
    dot_general x3, matrix products, on_device(): jnp.dot(lhs, piece, precision=lax.Precision.HIGH, preferred_element_type=...  14.4 us
    all_to_all x1, starting transfers between devices, on_device(): t_all = lax.all_to_all(spread, 'pair', 0, 0, tiled=True)  11.6 us
    ppermute x3, starting transfers between devices, on_device(): works.append(keep + lax.ppermute(send, 'gx', swap))  7.39 us
  transfers between devices with their start and end apart: 10, of which 5 were waited for; matrix products, arithmetic and copies ran while one was open for 14% of the time, Pallas kernels for 0%

profile of v6, /device:TPU:1, one launch (start us, length us, event | category | flops | bytes accessed | tf_op | source)
XLA Modules:
  0.0 207.3 jit_solution(6696389047656756444)
XLA Ops:
  6.5 2.3 %slice.34 = f32[256,768]{1,0:T(8,128)} slice(f32[256,2048]{1,0:T(8,128)} %param.12), slice={[0:256], [0:768]} | slice | bytes 1572864 | tf_op jit(solution)/shard_map/slice | solution.py:63
  8.9 1.2 fusion.11
  10.2 0.6 gather_fusion.2
  10.9 0.6 gather_fusion.3
  11.5 3.6 %collective-permute-start = (f32[7,1024]{1,0:T(8,128)S(1)}, f32[7,1024]{1,0:T(8,128)S(1)}, u32[]{:S(2)}, u32[]{:S(2)}) collective-permute-start(f32[7,1024]{1,0:T(8,128)S(1)} %select_bitcast_fusion), channel_id=1, source_target_pairs={{0,1},{1,0},{2,3},{3,2},{4,5},{5,4},{6,7},{7,6},{8,9},{9,8},{10,11... | collective-permute-start | bytes 86024 | tf_op jit(solution)/shard_map/ppermute | solution.py:46
  15.1 0.6 gather_fusion
  15.8 0.6 gather_fusion.1
  16.5 1.7 broadcast_in_dim.45
  18.2 11.6 %all-to-all-start = ((f32[32,2,7,1024]{3,1,2,0:T(2,128)}), f32[32,2,7,1024]{3,1,2,0:T(2,128)S(1)}, u32[]{:S(2)}, u32[]{:S(2)}) async-start(f32[32,2,7,1024]{3,1,2,0:T(2,128)} %broadcast_in_dim.45), calls=%async_computation | async-start | bytes 3670016 | tf_op jit(solution)/shard_map/all_to_all | solution.py:49
  29.9 0.7 all-gather.4.cloned.1.call-update
  30.6 43.8 %all-to-all-done = f32[32,2,7,1024]{3,1,2,0:T(2,128)S(1)} async-done(((f32[32,2,7,1024]{3,1,2,0:T(2,128)}), f32[32,2,7,1024]{3,1,2,0:T(2,128)S(1)}, u32[]{:S(2)}, u32[]{:S(2)}) %all-to-all-start) | async-done | bytes 1835040 | tf_op jit(solution)/shard_map/all_to_all | solution.py:49
  74.4 4.9 %fusion = f32[32,2,7,768]{3,0,2,1:T(8,128)S(1)} fusion(f32[1024,768]{1,0:T(8,128)} %all-gather.8.cloned.1.call-done, f32[32,2,7,1024]{3,1,2,0:T(2,128)S(1)} %all-to-all-done), kind=kOutput, calls=%fused_computation.8 | convolution fusion | flops 2113929216 | bytes 6356992 | tf_op jit(solution)/shard_map/dot_general | solution.py:68
  79.3 0.9 dynamic-slice_bitcast_fusion
  80.2 2.5 %collective-permute-start.1 = (f32[32,7,768]{2,0,1:T(8,128)}, f32[32,7,768]{2,0,1:T(8,128)}, u32[]{:S(2)}, u32[]{:S(2)}) collective-permute-start(f32[32,7,768]{2,0,1:T(8,128)} %dynamic-slice_bitcast_fusion), channel_id=1, source_target_pairs={{0,1},{1,0},{2,3},{3,2},{4,5},{5,4},{6,7},{7,6},{8,9},{9,8},{10,11... | collective-permute-start | bytes 2064392 | tf_op jit(solution)/shard_map/ppermute | solution.py:72
  82.7 0.9 constant_dynamic-slice_fusion
  83.6 1.6 select_reduce_fusion
  85.5 13.1 %collective-permute-done.1 = f32[32,7,768]{2,0,1:T(8,128)} collective-permute-done((f32[32,7,768]{2,0,1:T(8,128)}, f32[32,7,768]{2,0,1:T(8,128)}, u32[]{:S(2)}, u32[]{:S(2)}) %collective-permute-start.1) | collective-permute-done | bytes 688160 | tf_op jit(solution)/shard_map/ppermute | solution.py:72
  98.6 1.3 subtract_divide_fusion
  99.8 1.3 copy.48
  101.1 5.5 %all-to-all-start.1 = ((f32[32,7,768]{2,1,0:T(8,128)}), f32[32,7,768]{2,1,0:T(8,128)S(1)}, u32[]{:S(2)}, u32[]{:S(2)}) async-start(f32[32,7,768]{2,1,0:T(8,128)} %copy.48), calls=%async_computation.1 | async-start | bytes 1572864 | tf_op jit(solution)/shard_map/all_to_all | solution.py:74
  106.7 4.8 %fusion.4 = f32[32,2,7,640]{3,0,2,1:T(8,128)S(1)} fusion(f32[1024,640]{1,0:T(8,128)} %all-gather.6.cloned.1.call-done, f32[32,2,7,1024]{3,1,2,0:T(2,128)S(1)} %all-to-all-done), kind=kOutput, calls=%fused_computation.12 | convolution fusion | flops 1761607680 | bytes 5603328 | tf_op jit(solution)/shard_map/dot_general | solution.py:68
  111.5 2.4 %collective-permute-start.2 = (f32[32,7,640]{2,0,1:T(8,128)S(1)}, f32[32,7,640]{2,0,1:T(8,128)S(1)}, u32[]{:S(2)}, u32[]{:S(2)}) collective-permute-start(f32[32,7,640]{2,0,1:T(8,128)S(1)} %dynamic-slice_bitcast_fusion.2), channel_id=1, source_target_pairs={{0,1},{1,0},{2,3},{3,2},{4,5},{5,4},{6,7},{7,6},{8,9},{9,8},{10,11... | collective-permute-start | bytes 1720328 | tf_op jit(solution)/shard_map/ppermute | solution.py:72
  114.0 19.6 %collective-permute-done.2 = f32[32,7,640]{2,0,1:T(8,128)S(1)} collective-permute-done((f32[32,7,640]{2,0,1:T(8,128)S(1)}, f32[32,7,640]{2,0,1:T(8,128)S(1)}, u32[]{:S(2)}, u32[]{:S(2)}) %collective-permute-start.2) | collective-permute-done | bytes 573472 | tf_op jit(solution)/shard_map/ppermute | solution.py:72
  133.7 0.5 all-gather.4.cloned.1.call-done
  134.3 1.2 copy.50
  135.5 9.1 %all-to-all-start.2 = ((f32[32,7,640]{2,1,0:T(8,128)}), f32[32,7,640]{2,1,0:T(8,128)S(1)}, u32[]{:S(2)}, u32[]{:S(2)}) async-start(f32[32,7,640]{2,1,0:T(8,128)} %copy.50), calls=%async_computation.2 | async-start | bytes 1310720 | tf_op jit(solution)/shard_map/all_to_all | solution.py:74
  144.6 4.7 %fusion.2 = f32[32,2,7,640]{3,0,2,1:T(8,128)S(1)} fusion(f32[1024,640]{1,0:T(8,128)} %all-gather.4.cloned.1.call-done, f32[32,2,7,1024]{3,1,2,0:T(2,128)S(1)} %all-to-all-done), kind=kOutput, calls=%fused_computation.10 | convolution fusion | flops 1761607680 | bytes 5603328 | tf_op jit(solution)/shard_map/dot_general | solution.py:68
  149.3 2.5 %collective-permute-start.3 = (f32[32,7,640]{2,0,1:T(8,128)S(1)}, f32[32,7,640]{2,0,1:T(8,128)S(1)}, u32[]{:S(2)}, u32[]{:S(2)}) collective-permute-start(f32[32,7,640]{2,0,1:T(8,128)S(1)} %dynamic-slice_bitcast_fusion.1), channel_id=1, source_target_pairs={{0,1},{1,0},{2,3},{3,2},{4,5},{5,4},{6,7},{7,6},{8,9},{9,8},{10,11... | collective-permute-start | bytes 1720328 | tf_op jit(solution)/shard_map/ppermute | solution.py:72
  151.8 18.0 %collective-permute-done.3 = f32[32,7,640]{2,0,1:T(8,128)S(1)} collective-permute-done((f32[32,7,640]{2,0,1:T(8,128)S(1)}, f32[32,7,640]{2,0,1:T(8,128)S(1)}, u32[]{:S(2)}, u32[]{:S(2)}) %collective-permute-start.3) | collective-permute-done | bytes 573472 | tf_op jit(solution)/shard_map/ppermute | solution.py:72
  170.0 0.3 copy.52
  170.4 27.0 %all_to_all.20 = f32[32,7,640]{2,1,0:T(8,128)S(1)} all-to-all(f32[32,7,640]{2,1,0:T(8,128)S(1)} %copy.52), channel_id=1, replica_groups=mesh['pair'=32,'gy'=4,'gx'=2] {'pair'}, dimensions={0} | all-to-all | bytes 1146880 | tf_op jit(solution)/shard_map/all_to_all | solution.py:74
  197.7 3.1 %copy.53 = f32[1,7,65536]{2,0,1:T(1,128)} copy(f32[1,7,65536]{2,1,0:T(8,128)S(1)} %bitcast.48) | data formatting | bytes 3670016 | tf_op jit(solution)/shard_map/reshape | solution.py:76
  (47 shorter events, 1.5 us)
Async XLA Ops:
  6.5 3.6 %copy-start = (s32[16]{0:T(128)S(1)}, s32[16]{0:T(128)}, u32[]{:S(2)}) copy-start(s32[16]{0:T(128)} %param.13) | copy-start | bytes 196
  6.5 2.4 %copy-start.1 = (f32[256,2048]{1,0:T(8,128)S(1)}, f32[256,2048]{1,0:T(8,128)}, u32[]{:S(2)}) copy-start(f32[256,2048]{1,0:T(8,128)} %param.12) | copy-start | bytes 6291460
  6.5 67.9 %all-gather.8.cloned.1.call-start = ((), (), s32[]{:S(2)}) async-start(), calls=%async_computation.6 | async-start | bytes 3932160 | tf_op jit(solution)/shard_map/all_gather | solution.py:63
  8.8 1.3 copy-start.2
  8.9 97.8 %all-gather.6.cloned.1.call-start = ((), (), s32[]{:S(2)}) async-start(), calls=%async_computation.5 | async-start | bytes 3276800 | tf_op jit(solution)/shard_map/all_gather | solution.py:63
  11.5 4.9 %collective-permute-start = (f32[7,1024]{1,0:T(8,128)S(1)}, f32[7,1024]{1,0:T(8,128)S(1)}, u32[]{:S(2)}, u32[]{:S(2)}) collective-permute-start(f32[7,1024]{1,0:T(8,128)S(1)} %select_bitcast_fusion), channel_id=1, source_target_pairs={{0,1},{1,0},{2,3},{3,2},{4,5},{5,4},{6,7},{7,6},{8,9},{9,8},{10,11... | collective-permute-start | bytes 86024 | tf_op jit(solution)/shard_map/ppermute | solution.py:46
  18.2 56.2 %all-to-all-start = ((f32[32,2,7,1024]{3,1,2,0:T(2,128)}), f32[32,2,7,1024]{3,1,2,0:T(2,128)S(1)}, u32[]{:S(2)}, u32[]{:S(2)}) async-start(f32[32,2,7,1024]{3,1,2,0:T(2,128)} %broadcast_in_dim.45), calls=%async_computation | async-start | bytes 3670016 | tf_op jit(solution)/shard_map/all_to_all | solution.py:49
  29.8 104.5 %all-gather.4.cloned.1.call-start = ((), (), s32[]{:S(2)}) async-start(), calls=%async_computation.4 | async-start | bytes 3276800 | tf_op jit(solution)/shard_map/all_gather | solution.py:63
  30.5 53.0 %copy-start.3 = (f32[512]{0:T(512)S(1)}, f32[512]{0:T(512)}, u32[]{:S(2)}) copy-start(f32[512]{0:T(512)} %param.17) | copy-start | bytes 6148
  30.6 54.6 %copy-start.4 = (s32[1,2,224]{2,1,0:T(2,128)S(1)}, s32[1,2,224]{2,1,0:T(2,128)}, u32[]{:S(2)}) copy-start(s32[1,2,224]{2,1,0:T(2,128)} %param.14) | copy-start | bytes 5380
  30.6 54.6 %copy-start.5 = (f32[64]{0:T(128)S(1)}, f32[64]{0:T(128)}, u32[]{:S(2)}) copy-start(f32[64]{0:T(128)} %param.16) | copy-start | bytes 772
  80.2 18.3 %collective-permute-start.1 = (f32[32,7,768]{2,0,1:T(8,128)}, f32[32,7,768]{2,0,1:T(8,128)}, u32[]{:S(2)}, u32[]{:S(2)}) collective-permute-start(f32[32,7,768]{2,0,1:T(8,128)} %dynamic-slice_bitcast_fusion), channel_id=1, source_target_pairs={{0,1},{1,0},{2,3},{3,2},{4,5},{5,4},{6,7},{7,6},{8,9},{9,8},{10,11... | collective-permute-start | bytes 2064392 | tf_op jit(solution)/shard_map/ppermute | solution.py:72
  101.1 34.3 %all-to-all-start.1 = ((f32[32,7,768]{2,1,0:T(8,128)}), f32[32,7,768]{2,1,0:T(8,128)S(1)}, u32[]{:S(2)}, u32[]{:S(2)}) async-start(f32[32,7,768]{2,1,0:T(8,128)} %copy.48), calls=%async_computation.1 | async-start | bytes 1572864 | tf_op jit(solution)/shard_map/all_to_all | solution.py:74
  111.5 22.0 %collective-permute-start.2 = (f32[32,7,640]{2,0,1:T(8,128)S(1)}, f32[32,7,640]{2,0,1:T(8,128)S(1)}, u32[]{:S(2)}, u32[]{:S(2)}) collective-permute-start(f32[32,7,640]{2,0,1:T(8,128)S(1)} %dynamic-slice_bitcast_fusion.2), channel_id=1, source_target_pairs={{0,1},{1,0},{2,3},{3,2},{4,5},{5,4},{6,7},{7,6},{8,9},{9,8},{10,11... | collective-permute-start | bytes 1720328 | tf_op jit(solution)/shard_map/ppermute | solution.py:72
  135.5 34.9 %all-to-all-start.2 = ((f32[32,7,640]{2,1,0:T(8,128)}), f32[32,7,640]{2,1,0:T(8,128)S(1)}, u32[]{:S(2)}, u32[]{:S(2)}) async-start(f32[32,7,640]{2,1,0:T(8,128)} %copy.50), calls=%async_computation.2 | async-start | bytes 1310720 | tf_op jit(solution)/shard_map/all_to_all | solution.py:74
  149.3 20.5 %collective-permute-start.3 = (f32[32,7,640]{2,0,1:T(8,128)S(1)}, f32[32,7,640]{2,0,1:T(8,128)S(1)}, u32[]{:S(2)}, u32[]{:S(2)}) collective-permute-start(f32[32,7,640]{2,0,1:T(8,128)S(1)} %dynamic-slice_bitcast_fusion.1), channel_id=1, source_target_pairs={{0,1},{1,0},{2,3},{3,2},{4,5},{5,4},{6,7},{7,6},{8,9},{9,8},{10,11... | collective-permute-start | bytes 1720328 | tf_op jit(solution)/shard_map/ppermute | solution.py:72
Sparse Core Ops, SparseCore 0:
  9.1 45.6 all-gather.7
  56.7 37.8 all-gather.5
  96.4 37.8 all-gather.3

commit v7 on v6

--- a/solution.py
+++ b/solution.py
@@ -5,6 +5,9 @@
 from jax.sharding import Mesh, PartitionSpec as P
 
 CHUNK_PARTS = (6, 5, 5)
+
+
+PAIR = ("pz", "pq")
 
 
 def lookup(energy, idx):
@@ -26,9 +29,11 @@
     per_block = block // sub
     ny = lax.axis_size("gy")
     nx = lax.axis_size("gx")
-    npair = lax.axis_size("pair")
+    nz = lax.axis_size("pz")
+    nq = lax.axis_size("pq")
+    npair = nz * nq
     gx = lax.axis_index("gx")
-    p = lax.axis_index("pair")
+    p = lax.axis_index("pz") * nq + lax.axis_index("pq")
 
     def half_blocks(x):
         m = jnp.arange(ny * per_block, dtype=jnp.int32)
@@ -45,8 +50,8 @@
     swap = [(0, 1), (1, 0)]
     got = lax.ppermute(other, "gx", swap)
     both = jnp.where(gx == 0, jnp.stack([mine, got]), jnp.stack([got, mine]))
-    spread = jnp.broadcast_to(both[None], (npair,) + both.shape)
-    t_all = lax.all_to_all(spread, "pair", 0, 0, tiled=True)
+    near = lax.all_to_all(jnp.broadcast_to(both[None], (nq,) + both.shape), "pq", 0, 0, tiled=True)
+    t_all = lax.all_to_all(jnp.broadcast_to(near[None], (nz,) + near.shape), "pz", 0, 0, tiled=True)
     lhs = t_all.reshape(npair * nx * rows_l, -1)
 
     occ_sum = pair_energies(occ_energy, occ_pairs[0]).reshape(npair, rows_l)
@@ -71,7 +76,7 @@
         send = lax.dynamic_index_in_dim(part, 1 - gx, 1, keepdims=False)
         works.append(keep + lax.ppermute(send, "gx", swap))
         payload = works[c] / (occ_sum[:, :, None] - vir_sum[None, None, lo:hi])
-        outs.append(lax.all_to_all(payload, "pair", 0, 0, tiled=True))
+        outs.append(lax.all_to_all(payload, PAIR, 0, 0, tiled=True))
     res = jnp.concatenate(outs, axis=2)
     res = jnp.transpose(res, (1, 0, 2)).reshape(1, rows_l, npair * columns)
     return res
@@ -81,20 +86,21 @@
     devs = np.asarray(mesh.devices)
     npair, ngrp = devs.shape
     nx = 2
-    sub_mesh = Mesh(devs.reshape(npair, ngrp // nx, nx), ("pair", "gy", "gx"))
+    nq = 4
+    sub_mesh = Mesh(devs.reshape(npair // nq, nq, ngrp // nx, nx), ("pz", "pq", "gy", "gx"))
     g = ("gy", "gx")
     return jax.shard_map(
         on_device,
         mesh=sub_mesh,
         in_specs=(
-            P(g, "pair", None),
-            P(g, "pair"),
+            P(g, PAIR, None),
+            P(g, PAIR),
             P(),
             P(g, None, None),
             P(),
             P(),
             P(),
         ),
-        out_specs=P(g, "pair", None),
+        out_specs=P(g, PAIR, None),
         check_vma=False,
     )

time: 208 us -> 215 us (1.034)
  blocking collectives: 27 us -> 38 us
  starting transfers between devices: 37.2 us -> 29.3 us
  local copies, waits for them, and re-layouts: 15.7 us -> 19.1 us
    all_to_all x1 -> x2, blocking collectives: 27 us -> 38 us  [the longest x1 27.2 us: on_device(): outs.append(lax.all_to_all(payload, PAIR, 0, 0, tiled=True))]
    all_to_all x3, starting transfers between devices: 26.2 us -> 18.5 us  [the longest x2 11.9 us: on_device(): outs.append(lax.all_to_all(payload, PAIR, 0, 0, tiled=True))]
  transfers between devices with their start and end apart: 10 -> 10, of which waited for: 5 -> 4; matrix products, arithmetic and copies ran while one was open for 14% -> 14% of each run, Pallas kernels for 0% -> 0%
where the time goes in v7:
time: 215 us; the launch traced here: 214 us
  waiting for transfers between devices  97.7 us (45%)
  blocking collectives  38 us (18%)
  starting transfers between devices  29.3 us (14%)
  local copies, waits for them, and re-layouts  19.1 us (9%)
  between operations  13.5 us (6%)
  matrix products  12.9 us (6%)
  other arithmetic  3.85 us (2%)
    ppermute x3, waiting for transfers between devices, on_device(): works.append(keep + lax.ppermute(send, 'gx', swap))  51.6 us
    all_to_all x1, waiting for transfers between devices, on_device(): lax.all_to_all(jnp.broadcast_to(near[None], (nz,) + near.shape), 'pz', 0,...  45.3 us
    all_to_all x1, blocking collectives, on_device(): outs.append(lax.all_to_all(payload, PAIR, 0, 0, tiled=True))  27.2 us
    dot_general x3, matrix products, on_device(): jnp.dot(lhs, piece, precision=lax.Precision.HIGH, preferred_element_type=...  12.9 us
    all_to_all x2, starting transfers between devices, on_device(): outs.append(lax.all_to_all(payload, PAIR, 0, 0, tiled=True))  11.9 us
    all_to_all x1, blocking collectives, on_device(): lax.all_to_all(jnp.broadcast_to(both[None], (nq,) + both.shape), 'pq', 0,...  10.8 us
    ppermute x3, starting transfers between devices, on_device(): works.append(keep + lax.ppermute(send, 'gx', swap))  7.1 us
    all_to_all x1, starting transfers between devices, on_device(): lax.all_to_all(jnp.broadcast_to(near[None], (nz,) + near.shape), 'pz', 0,...  6.66 us
  transfers between devices with their start and end apart: 10, of which 4 were waited for; matrix products, arithmetic and copies ran while one was open for 14% of the time, Pallas kernels for 0%

profile of v7, /device:TPU:1, one launch (start us, length us, event | category | flops | bytes accessed | tf_op | source)
XLA Modules:
  0.0 214.4 jit_solution(9315737236635453201)
XLA Ops:
  6.5 2.3 %slice.34 = f32[256,768]{1,0:T(8,128)} slice(f32[256,2048]{1,0:T(8,128)} %param.12), slice={[0:256], [0:768]} | slice | bytes 1572864 | tf_op jit(solution)/shard_map/slice | solution.py:68
  8.9 1.2 fusion.8
  10.2 0.6 gather_fusion.2
  10.9 0.6 gather_fusion.3
  11.5 3.6 %collective-permute-start = (f32[7,1024]{1,0:T(8,128)S(1)}, f32[7,1024]{1,0:T(8,128)S(1)}, u32[]{:S(2)}, u32[]{:S(2)}) collective-permute-start(f32[7,1024]{1,0:T(8,128)S(1)} %select_bitcast_fusion), channel_id=1, source_target_pairs={{0,1},{1,0},{2,3},{3,2},{4,5},{5,4},{6,7},{7,6},{8,9},{9,8},{10,11... | collective-permute-start | bytes 86024 | tf_op jit(solution)/shard_map/ppermute | solution.py:51
  15.1 0.6 gather_fusion
  16.6 10.8 %all_to_all.25 = f32[4,2,7,1024]{3,1,2,0:T(2,128)S(1)} all-to-all(f32[4,2,7,1024]{3,1,2,0:T(2,128)S(1)} %broadcast_in_dim.51), channel_id=1, replica_groups=mesh['pz'=8,'pq'=4,'gy'=4,'gx'=2] {'pq'}, dimensions={0} | all-to-all | bytes 458752 | tf_op jit(solution)/shard_map/all_to_all | solution.py:53
  27.5 1.7 broadcast_in_dim.52
  29.2 6.7 %all-to-all-start.1 = ((f32[8,4,2,7,1024]{4,1,3,2,0:T(4,128)}), f32[8,4,2,7,1024]{4,1,3,2,0:T(4,128)S(1)}, u32[]{:S(2)}, u32[]{:S(2)}) async-start(f32[8,4,2,7,1024]{4,1,3,2,0:T(4,128)} %broadcast_in_dim.52), calls=%async_computation.1 | async-start | bytes 3670016 | tf_op jit(solution)/shard_map/all_to_all | solution.py:54
  35.9 0.7 all-gather.4.cloned.1.call-update
  36.6 45.3 %all-to-all-done.1 = f32[8,4,2,7,1024]{4,1,3,2,0:T(4,128)S(1)} async-done(((f32[8,4,2,7,1024]{4,1,3,2,0:T(4,128)}), f32[8,4,2,7,1024]{4,1,3,2,0:T(4,128)S(1)}, u32[]{:S(2)}, u32[]{:S(2)}) %all-to-all-start.1) | async-done | bytes 1835040 | tf_op jit(solution)/shard_map/all_to_all | solution.py:54
  81.9 1.4 copy.43
  83.4 1.9 dot_general.11
  85.3 4.4 %fusion = f32[32,2,7,768]{3,0,2,1:T(8,128)S(1)} fusion(f32[32,2,7,1024]{3,0,2,1:T(8,128)S(1)} %dot_general.11, f32[1024,768]{1,0:T(8,128)} %all-gather.8.cloned.1.call-done), kind=kOutput, calls=%fused_computation.8 | convolution fusion | flops 2113929216 | bytes 6356992 | tf_op jit(solution)/shard_map/dot_general | solution.py:73
  89.7 0.9 dynamic-slice_bitcast_fusion
  90.7 2.6 %collective-permute-start.1 = (f32[32,7,768]{2,0,1:T(8,128)}, f32[32,7,768]{2,0,1:T(8,128)}, u32[]{:S(2)}, u32[]{:S(2)}) collective-permute-start(f32[32,7,768]{2,0,1:T(8,128)} %dynamic-slice_bitcast_fusion), channel_id=1, source_target_pairs={{0,1},{1,0},{2,3},{3,2},{4,5},{5,4},{6,7},{7,6},{8,9},{9,8},{10,11... | collective-permute-start | bytes 2064392 | tf_op jit(solution)/shard_map/ppermute | solution.py:77
  93.2 0.9 constant_dynamic-slice_fusion
  94.1 1.6 select_reduce_fusion
  96.0 13.0 %collective-permute-done.1 = f32[32,7,768]{2,0,1:T(8,128)} collective-permute-done((f32[32,7,768]{2,0,1:T(8,128)}, f32[32,7,768]{2,0,1:T(8,128)}, u32[]{:S(2)}, u32[]{:S(2)}) %collective-permute-start.1) | collective-permute-done | bytes 688160 | tf_op jit(solution)/shard_map/ppermute | solution.py:77
  109.0 1.3 subtract_divide_fusion
  110.3 1.3 copy.45
  111.6 4.9 %all-to-all-start.2 = ((f32[32,7,768]{2,1,0:T(8,128)}), f32[32,7,768]{2,1,0:T(8,128)S(1)}, u32[]{:S(2)}, u32[]{:S(2)}) async-start(f32[32,7,768]{2,1,0:T(8,128)} %copy.45), calls=%async_computation.2 | async-start | bytes 1572864 | tf_op jit(solution)/shard_map/all_to_all | solution.py:79
  116.5 4.2 %fusion.4 = f32[32,2,7,640]{3,0,2,1:T(8,128)S(1)} fusion(f32[32,2,7,1024]{3,0,2,1:T(8,128)S(1)} %dot_general.11, f32[1024,640]{1,0:T(8,128)} %all-gather.6.cloned.1.call-done), kind=kOutput, calls=%fused_computation.12 | convolution fusion | flops 1761607680 | bytes 5603328 | tf_op jit(solution)/shard_map/dot_general | solution.py:73
  120.8 2.6 %collective-permute-start.2 = (f32[32,7,640]{2,0,1:T(8,128)S(1)}, f32[32,7,640]{2,0,1:T(8,128)S(1)}, u32[]{:S(2)}, u32[]{:S(2)}) collective-permute-start(f32[32,7,640]{2,0,1:T(8,128)S(1)} %dynamic-slice_bitcast_fusion.2), channel_id=1, source_target_pairs={{0,1},{1,0},{2,3},{3,2},{4,5},{5,4},{6,7},{7,6},{8,9},{9,8},{10,11... | collective-permute-start | bytes 1720328 | tf_op jit(solution)/shard_map/ppermute | solution.py:77
  123.5 20.2 %collective-permute-done.2 = f32[32,7,640]{2,0,1:T(8,128)S(1)} collective-permute-done((f32[32,7,640]{2,0,1:T(8,128)S(1)}, f32[32,7,640]{2,0,1:T(8,128)S(1)}, u32[]{:S(2)}, u32[]{:S(2)}) %collective-permute-start.2) | collective-permute-done | bytes 573472 | tf_op jit(solution)/shard_map/ppermute | solution.py:77
  143.9 1.2 copy.47
  145.1 7.0 %all-to-all-start.3 = ((f32[32,7,640]{2,1,0:T(8,128)}), f32[32,7,640]{2,1,0:T(8,128)S(1)}, u32[]{:S(2)}, u32[]{:S(2)}) async-start(f32[32,7,640]{2,1,0:T(8,128)} %copy.47), calls=%async_computation.3 | async-start | bytes 1310720 | tf_op jit(solution)/shard_map/all_to_all | solution.py:79
  152.1 4.2 %fusion.2 = f32[32,2,7,640]{3,0,2,1:T(8,128)S(1)} fusion(f32[32,2,7,1024]{3,0,2,1:T(8,128)S(1)} %dot_general.11, f32[1024,640]{1,0:T(8,128)} %all-gather.4.cloned.1.call-done), kind=kOutput, calls=%fused_computation.10 | convolution fusion | flops 1761607680 | bytes 5603328 | tf_op jit(solution)/shard_map/dot_general | solution.py:73
  156.4 1.9 collective-permute-start.3
  158.3 18.4 %collective-permute-done.3 = f32[32,7,640]{2,0,1:T(8,128)S(1)} collective-permute-done((f32[32,7,640]{2,0,1:T(8,128)S(1)}, f32[32,7,640]{2,0,1:T(8,128)S(1)}, u32[]{:S(2)}, u32[]{:S(2)}) %collective-permute-start.3) | collective-permute-done | bytes 573472 | tf_op jit(solution)/shard_map/ppermute | solution.py:77
  177.2 27.2 %all_to_all.26 = f32[32,7,640]{2,1,0:T(8,128)S(1)} all-to-all(f32[32,7,640]{2,1,0:T(8,128)S(1)} %copy.48), channel_id=1, replica_groups=mesh['pz'=8,'pq'=4,'gy'=4,'gx'=2] {'pz','pq'}, dimensions={0} | all-to-all | bytes 1146880 | tf_op jit(solution)/shard_map/all_to_all | solution.py:79
  204.7 3.1 %copy.49 = f32[1,7,65536]{2,0,1:T(1,128)} copy(f32[1,7,65536]{2,1,0:T(8,128)S(1)} %bitcast.53) | data formatting | bytes 3670016 | tf_op jit(solution)/shard_map/reshape | solution.py:81
  (52 shorter events, 2.6 us)
Async XLA Ops:
  6.5 3.6 %copy-start = (s32[16]{0:T(128)S(1)}, s32[16]{0:T(128)}, u32[]{:S(2)}) copy-start(s32[16]{0:T(128)} %param.13) | copy-start | bytes 196
  6.5 2.4 %copy-start.1 = (f32[256,2048]{1,0:T(8,128)S(1)}, f32[256,2048]{1,0:T(8,128)}, u32[]{:S(2)}) copy-start(f32[256,2048]{1,0:T(8,128)} %param.12) | copy-start | bytes 6291460
  6.5 78.8 %all-gather.8.cloned.1.call-start = ((), (), s32[]{:S(2)}) async-start(), calls=%async_computation.7 | async-start | bytes 3932160 | tf_op jit(solution)/shard_map/all_gather | solution.py:68
  8.8 1.3 copy-start.2
  8.9 107.6 %all-gather.6.cloned.1.call-start = ((), (), s32[]{:S(2)}) async-start(), calls=%async_computation.6 | async-start | bytes 3276800 | tf_op jit(solution)/shard_map/all_gather | solution.py:68
  11.5 4.9 %collective-permute-start = (f32[7,1024]{1,0:T(8,128)S(1)}, f32[7,1024]{1,0:T(8,128)S(1)}, u32[]{:S(2)}, u32[]{:S(2)}) collective-permute-start(f32[7,1024]{1,0:T(8,128)S(1)} %select_bitcast_fusion), channel_id=1, source_target_pairs={{0,1},{1,0},{2,3},{3,2},{4,5},{5,4},{6,7},{7,6},{8,9},{9,8},{10,11... | collective-permute-start | bytes 86024 | tf_op jit(solution)/shard_map/ppermute | solution.py:51
  29.2 52.7 %all-to-all-start.1 = ((f32[8,4,2,7,1024]{4,1,3,2,0:T(4,128)}), f32[8,4,2,7,1024]{4,1,3,2,0:T(4,128)S(1)}, u32[]{:S(2)}, u32[]{:S(2)}) async-start(f32[8,4,2,7,1024]{4,1,3,2,0:T(4,128)} %broadcast_in_dim.52), calls=%async_computation.1 | async-start | bytes 3670016 | tf_op jit(solution)/shard_map/all_to_all | solution.py:54
  35.9 108.0 %all-gather.4.cloned.1.call-start = ((), (), s32[]{:S(2)}) async-start(), calls=%async_computation.5 | async-start | bytes 3276800 | tf_op jit(solution)/shard_map/all_gather | solution.py:68
  85.3 8.8 %copy-start.3 = (f32[512]{0:T(512)S(1)}, f32[512]{0:T(512)}, u32[]{:S(2)}) copy-start(f32[512]{0:T(512)} %param.17) | copy-start | bytes 6148
  85.3 10.4 %copy-start.4 = (s32[1,2,224]{2,1,0:T(2,128)S(1)}, s32[1,2,224]{2,1,0:T(2,128)}, u32[]{:S(2)}) copy-start(s32[1,2,224]{2,1,0:T(2,128)} %param.14) | copy-start | bytes 5380
  85.3 10.4 %copy-start.5 = (f32[64]{0:T(128)S(1)}, f32[64]{0:T(128)}, u32[]{:S(2)}) copy-start(f32[64]{0:T(128)} %param.16) | copy-start | bytes 772
  90.7 18.3 %collective-permute-start.1 = (f32[32,7,768]{2,0,1:T(8,128)}, f32[32,7,768]{2,0,1:T(8,128)}, u32[]{:S(2)}, u32[]{:S(2)}) collective-permute-start(f32[32,7,768]{2,0,1:T(8,128)} %dynamic-slice_bitcast_fusion), channel_id=1, source_target_pairs={{0,1},{1,0},{2,3},{3,2},{4,5},{5,4},{6,7},{7,6},{8,9},{9,8},{10,11... | collective-permute-start | bytes 2064392 | tf_op jit(solution)/shard_map/ppermute | solution.py:77
  111.6 33.5 %all-to-all-start.2 = ((f32[32,7,768]{2,1,0:T(8,128)}), f32[32,7,768]{2,1,0:T(8,128)S(1)}, u32[]{:S(2)}, u32[]{:S(2)}) async-start(f32[32,7,768]{2,1,0:T(8,128)} %copy.45), calls=%async_computation.2 | async-start | bytes 1572864 | tf_op jit(solution)/shard_map/all_to_all | solution.py:79
  120.8 22.9 %collective-permute-start.2 = (f32[32,7,640]{2,0,1:T(8,128)S(1)}, f32[32,7,640]{2,0,1:T(8,128)S(1)}, u32[]{:S(2)}, u32[]{:S(2)}) collective-permute-start(f32[32,7,640]{2,0,1:T(8,128)S(1)} %dynamic-slice_bitcast_fusion.2), channel_id=1, source_target_pairs={{0,1},{1,0},{2,3},{3,2},{4,5},{5,4},{6,7},{7,6},{8,9},{9,8},{10,11... | collective-permute-start | bytes 1720328 | tf_op jit(solution)/shard_map/ppermute | solution.py:77
  145.1 32.1 %all-to-all-start.3 = ((f32[32,7,640]{2,1,0:T(8,128)}), f32[32,7,640]{2,1,0:T(8,128)S(1)}, u32[]{:S(2)}, u32[]{:S(2)}) async-start(f32[32,7,640]{2,1,0:T(8,128)} %copy.47), calls=%async_computation.3 | async-start | bytes 1310720 | tf_op jit(solution)/shard_map/all_to_all | solution.py:79
  156.4 20.3 %collective-permute-start.3 = (f32[32,7,640]{2,0,1:T(8,128)S(1)}, f32[32,7,640]{2,0,1:T(8,128)S(1)}, u32[]{:S(2)}, u32[]{:S(2)}) collective-permute-start(f32[32,7,640]{2,0,1:T(8,128)S(1)} %dynamic-slice_bitcast_fusion.1), channel_id=1, source_target_pairs={{0,1},{1,0},{2,3},{3,2},{4,5},{5,4},{6,7},{7,6},{8,9},{9,8},{10,11... | collective-permute-start | bytes 1720328 | tf_op jit(solution)/shard_map/ppermute | solution.py:77
Sparse Core Ops, SparseCore 0:
  9.1 45.6 all-gather.7
  56.7 37.8 all-gather.5
  96.4 37.8 all-gather.3

commit v8 on v6

--- a/solution.py
+++ b/solution.py
@@ -4,7 +4,7 @@
 from jax import lax
 from jax.sharding import Mesh, PartitionSpec as P
 
-CHUNK_PARTS = (6, 5, 5)
+CHUNK_PARTS = (8, 4, 4)
 
 
 def lookup(energy, idx):

time: 208 us -> 204 us (0.981)
  blocking collectives: 27 us -> 24 us
  local copies, waits for them, and re-layouts: 15.7 us -> 18.2 us
  starting transfers between devices: 37.2 us -> 34.9 us
    all_to_all x1, blocking collectives: 27 us -> 24 us  [on_device(): outs.append(lax.all_to_all(payload, 'pair', 0, 0, tiled=True))]
    all_to_all x1, waiting for transfers between devices: 43.8 us -> 41.5 us  [on_device(): t_all = lax.all_to_all(spread, 'pair', 0, 0, tiled=True)]
    all_to_all x2, starting transfers between devices: 14.6 us -> 12.3 us  [on_device(): outs.append(lax.all_to_all(payload, 'pair', 0, 0, tiled=True))]
where the time goes in v8:
time: 204 us; the launch traced here: 203 us
  waiting for transfers between devices  95.6 us (47%)
  starting transfers between devices  34.9 us (17%)
  blocking collectives  24 us (12%)
  local copies, waits for them, and re-layouts  18.2 us (9%)
  matrix products  13.5 us (7%)
  between operations  13.4 us (7%)
  other arithmetic  3.78 us (2%)
    ppermute x3, waiting for transfers between devices, on_device(): works.append(keep + lax.ppermute(send, 'gx', swap))  52.6 us
    all_to_all x1, waiting for transfers between devices, on_device(): t_all = lax.all_to_all(spread, 'pair', 0, 0, tiled=True)  41.5 us
    all_to_all x1, blocking collectives, on_device(): outs.append(lax.all_to_all(payload, 'pair', 0, 0, tiled=True))  24 us
    dot_general x3, matrix products, on_device(): jnp.dot(lhs, piece, precision=lax.Precision.HIGH, preferred_element_type=...  13.5 us
    all_to_all x2, starting transfers between devices, on_device(): outs.append(lax.all_to_all(payload, 'pair', 0, 0, tiled=True))  12.3 us
    all_to_all x1, starting transfers between devices, on_device(): t_all = lax.all_to_all(spread, 'pair', 0, 0, tiled=True)  11.6 us
    ppermute x3, starting transfers between devices, on_device(): works.append(keep + lax.ppermute(send, 'gx', swap))  7.37 us
    slice x2, local copies, waits for them, and re-layouts, on_device(): piece = lax.all_gather(integrals[:, lo:hi], 'gy', axis=0, tiled=True)  4.69 us
  transfers between devices with their start and end apart: 10, of which 5 were waited for; matrix products, arithmetic and copies ran while one was open for 14% of the time, Pallas kernels for 0%

profile of v8, /device:TPU:1, one launch (start us, length us, event | category | flops | bytes accessed | tf_op | source)
XLA Modules:
  0.0 203.5 jit_solution(11339281095394732284)
XLA Ops:
  6.5 2.4 %slice.34 = f32[256,1024]{1,0:T(8,128)} slice(f32[256,2048]{1,0:T(8,128)} %param.12), slice={[0:256], [0:1024]} | slice | bytes 2097152 | tf_op jit(solution)/shard_map/slice | solution.py:63
  9.1 0.6 gather_fusion.2
  9.8 0.6 gather_fusion.3
  10.4 3.6 %collective-permute-start = (f32[7,1024]{1,0:T(8,128)S(1)}, f32[7,1024]{1,0:T(8,128)S(1)}, u32[]{:S(2)}, u32[]{:S(2)}) collective-permute-start(f32[7,1024]{1,0:T(8,128)S(1)} %select_bitcast_fusion), channel_id=1, source_target_pairs={{0,1},{1,0},{2,3},{3,2},{4,5},{5,4},{6,7},{7,6},{8,9},{9,8},{10,11... | collective-permute-start | bytes 86024 | tf_op jit(solution)/shard_map/ppermute | solution.py:46
  14.0 0.6 gather_fusion
  14.7 0.6 gather_fusion.1
  15.4 1.7 broadcast_in_dim.45
  17.1 11.6 %all-to-all-start = ((f32[32,2,7,1024]{3,1,2,0:T(2,128)}), f32[32,2,7,1024]{3,1,2,0:T(2,128)S(1)}, u32[]{:S(2)}, u32[]{:S(2)}) async-start(f32[32,2,7,1024]{3,1,2,0:T(2,128)} %broadcast_in_dim.45), calls=%async_computation | async-start | bytes 3670016 | tf_op jit(solution)/shard_map/all_to_all | solution.py:49
  28.7 2.3 %fusion.11 = (f32[256,512]{1,0:T(8,128)}, f32[256,512]{1,0:T(8,128)}) fusion(f32[256,2048]{1,0:T(8,128)} %param.12), kind=kLoop, calls=%fused_computation.53 | loop fusion | bytes 2097152 | tf_op jit(solution)/shard_map/slice | solution.py:63
  31.1 0.7 all-gather.4.cloned.1.call-update
  31.8 41.5 %all-to-all-done = f32[32,2,7,1024]{3,1,2,0:T(2,128)S(1)} async-done(((f32[32,2,7,1024]{3,1,2,0:T(2,128)}), f32[32,2,7,1024]{3,1,2,0:T(2,128)S(1)}, u32[]{:S(2)}, u32[]{:S(2)}) %all-to-all-start) | async-done | bytes 1835040 | tf_op jit(solution)/shard_map/all_to_all | solution.py:49
  73.3 6.1 %fusion = f32[32,2,7,1024]{3,0,2,1:T(8,128)S(1)} fusion(f32[1024,1024]{1,0:T(8,128)} %all-gather.8.cloned.1.call-done, f32[32,2,7,1024]{3,1,2,0:T(2,128)S(1)} %all-to-all-done), kind=kOutput, calls=%fused_computation.4 | convolution fusion | flops 2818572288 | bytes 7864320 | tf_op jit(solution)/shard_map/dot_general | solution.py:68
  79.4 1.2 copy-done.1
  80.7 1.0 dynamic-slice_bitcast_fusion
  81.7 2.4 %collective-permute-start.1 = (f32[32,7,1024]{2,0,1:T(8,128)}, f32[32,7,1024]{2,0,1:T(8,128)S(1)}, u32[]{:S(2)}, u32[]{:S(2)}) collective-permute-start(f32[32,7,1024]{2,0,1:T(8,128)} %dynamic-slice_bitcast_fusion), channel_id=1, source_target_pairs={{0,1},{1,0},{2,3},{3,2},{4,5},{5,4},{6,7},{7,6},{8,9},{9,8},{10,11... | collective-permute-start | bytes 2752520 | tf_op jit(solution)/shard_map/ppermute | solution.py:72
  84.1 0.9 constant_dynamic-slice_fusion
  85.0 1.6 select_reduce_fusion
  86.9 17.9 %collective-permute-done.1 = f32[32,7,1024]{2,0,1:T(8,128)S(1)} collective-permute-done((f32[32,7,1024]{2,0,1:T(8,128)}, f32[32,7,1024]{2,0,1:T(8,128)S(1)}, u32[]{:S(2)}, u32[]{:S(2)}) %collective-permute-start.1) | collective-permute-done | bytes 917536 | tf_op jit(solution)/shard_map/ppermute | solution.py:72
  104.8 1.4 subtract_divide_fusion
  106.2 1.5 copy.48
  107.7 5.5 %all-to-all-start.1 = ((f32[32,7,1024]{2,1,0:T(8,128)}), f32[32,7,1024]{2,1,0:T(8,128)S(1)}, u32[]{:S(2)}, u32[]{:S(2)}) async-start(f32[32,7,1024]{2,1,0:T(8,128)} %copy.48), calls=%async_computation.1 | async-start | bytes 2097152 | tf_op jit(solution)/shard_map/all_to_all | solution.py:74
  113.2 3.7 %fusion.4 = f32[32,2,7,512]{3,0,2,1:T(8,128)S(1)} fusion(f32[1024,512]{1,0:T(8,128)} %all-gather.6.cloned.1.call-done, f32[32,2,7,1024]{3,1,2,0:T(2,128)S(1)} %all-to-all-done), kind=kOutput, calls=%fused_computation.13 | convolution fusion | flops 1409286144 | bytes 4849664 | tf_op jit(solution)/shard_map/dot_general | solution.py:68
  117.0 2.6 %collective-permute-start.2 = (f32[32,7,512]{2,0,1:T(8,128)S(1)}, f32[32,7,512]{2,0,1:T(8,128)S(1)}, u32[]{:S(2)}, u32[]{:S(2)}) collective-permute-start(f32[32,7,512]{2,0,1:T(8,128)S(1)} %dynamic-slice_bitcast_fusion.2), channel_id=1, source_target_pairs={{0,1},{1,0},{2,3},{3,2},{4,5},{5,4},{6,7},{7,6},{8,9},{9,8},{10,11... | collective-permute-start | bytes 1376264 | tf_op jit(solution)/shard_map/ppermute | solution.py:72
  119.6 19.7 %collective-permute-done.2 = f32[32,7,512]{2,0,1:T(8,128)S(1)} collective-permute-done((f32[32,7,512]{2,0,1:T(8,128)S(1)}, f32[32,7,512]{2,0,1:T(8,128)S(1)}, u32[]{:S(2)}, u32[]{:S(2)}) %collective-permute-start.2) | collective-permute-done | bytes 458784 | tf_op jit(solution)/shard_map/ppermute | solution.py:72
  139.5 1.1 copy.50
  140.6 0.7 all-to-all-done.1
  141.3 6.8 %all-to-all-start.2 = ((f32[32,7,512]{2,1,0:T(8,128)}), f32[32,7,512]{2,1,0:T(8,128)S(1)}, u32[]{:S(2)}, u32[]{:S(2)}) async-start(f32[32,7,512]{2,1,0:T(8,128)} %copy.50), calls=%async_computation.2 | async-start | bytes 1048576 | tf_op jit(solution)/shard_map/all_to_all | solution.py:74
  148.1 3.7 %fusion.2 = f32[32,2,7,512]{3,0,2,1:T(8,128)S(1)} fusion(f32[1024,512]{1,0:T(8,128)} %all-gather.4.cloned.1.call-done, f32[32,2,7,1024]{3,1,2,0:T(2,128)S(1)} %all-to-all-done), kind=kOutput, calls=%fused_computation.11 | convolution fusion | flops 1409286144 | bytes 4849664 | tf_op jit(solution)/shard_map/dot_general | solution.py:68
  151.8 2.3 %collective-permute-start.3 = (f32[32,7,512]{2,0,1:T(8,128)S(1)}, f32[32,7,512]{2,0,1:T(8,128)S(1)}, u32[]{:S(2)}, u32[]{:S(2)}) collective-permute-start(f32[32,7,512]{2,0,1:T(8,128)S(1)} %dynamic-slice_bitcast_fusion.1), channel_id=1, source_target_pairs={{0,1},{1,0},{2,3},{3,2},{4,5},{5,4},{6,7},{7,6},{8,9},{9,8},{10,11... | collective-permute-start | bytes 1376264 | tf_op jit(solution)/shard_map/ppermute | solution.py:72
  154.1 15.1 %collective-permute-done.3 = f32[32,7,512]{2,0,1:T(8,128)S(1)} collective-permute-done((f32[32,7,512]{2,0,1:T(8,128)S(1)}, f32[32,7,512]{2,0,1:T(8,128)S(1)}, u32[]{:S(2)}, u32[]{:S(2)}) %collective-permute-start.3) | collective-permute-done | bytes 458784 | tf_op jit(solution)/shard_map/ppermute | solution.py:72
  169.6 24.0 %all_to_all.20 = f32[32,7,512]{2,1,0:T(8,128)S(1)} all-to-all(f32[32,7,512]{2,1,0:T(8,128)S(1)} %copy.52), channel_id=1, replica_groups=mesh['pair'=32,'gy'=4,'gx'=2] {'pair'}, dimensions={0} | all-to-all | bytes 917504 | tf_op jit(solution)/shard_map/all_to_all | solution.py:74
  193.8 3.1 %copy.53 = f32[1,7,65536]{2,0,1:T(1,128)} copy(f32[1,7,65536]{2,1,0:T(8,128)S(1)} %bitcast.48) | data formatting | bytes 3670016 | tf_op jit(solution)/shard_map/reshape | solution.py:76
  (47 shorter events, 1.6 us)
Async XLA Ops:
  6.5 2.5 %copy-start = (s32[16]{0:T(128)S(1)}, s32[16]{0:T(128)}, u32[]{:S(2)}) copy-start(s32[16]{0:T(128)} %param.13) | copy-start | bytes 196
  6.5 2.5 %copy-start.2 = (f32[1,7,2048]{2,0,1:T(1,128)S(1)}, f32[1,7,2048]{2,0,1:T(1,128)}, u32[]{:S(2)}) copy-start(f32[1,7,2048]{2,0,1:T(1,128)} %param.11) | copy-start | bytes 172036
  6.5 66.8 %all-gather.8.cloned.1.call-start = ((), (), s32[]{:S(2)}) async-start(), calls=%async_computation.6 | async-start | bytes 5242880 | tf_op jit(solution)/shard_map/all_gather | solution.py:63
  10.4 4.9 %collective-permute-start = (f32[7,1024]{1,0:T(8,128)S(1)}, f32[7,1024]{1,0:T(8,128)S(1)}, u32[]{:S(2)}, u32[]{:S(2)}) collective-permute-start(f32[7,1024]{1,0:T(8,128)S(1)} %select_bitcast_fusion), channel_id=1, source_target_pairs={{0,1},{1,0},{2,3},{3,2},{4,5},{5,4},{6,7},{7,6},{8,9},{9,8},{10,11... | collective-permute-start | bytes 86024 | tf_op jit(solution)/shard_map/ppermute | solution.py:46
  17.1 56.2 %all-to-all-start = ((f32[32,2,7,1024]{3,1,2,0:T(2,128)}), f32[32,2,7,1024]{3,1,2,0:T(2,128)S(1)}, u32[]{:S(2)}, u32[]{:S(2)}) async-start(f32[32,2,7,1024]{3,1,2,0:T(2,128)} %broadcast_in_dim.45), calls=%async_computation | async-start | bytes 3670016 | tf_op jit(solution)/shard_map/all_to_all | solution.py:49
  28.7 84.5 %all-gather.6.cloned.1.call-start = ((), (), s32[]{:S(2)}) async-start(), calls=%async_computation.5 | async-start | bytes 2621440 | tf_op jit(solution)/shard_map/all_gather | solution.py:63
  31.0 108.5 %all-gather.4.cloned.1.call-start = ((), (), s32[]{:S(2)}) async-start(), calls=%async_computation.4 | async-start | bytes 2621440 | tf_op jit(solution)/shard_map/all_gather | solution.py:63
  31.8 53.2 %copy-start.3 = (f32[512]{0:T(512)S(1)}, f32[512]{0:T(512)}, u32[]{:S(2)}) copy-start(f32[512]{0:T(512)} %param.17) | copy-start | bytes 6148
  31.8 54.8 %copy-start.4 = (s32[1,2,224]{2,1,0:T(2,128)S(1)}, s32[1,2,224]{2,1,0:T(2,128)}, u32[]{:S(2)}) copy-start(s32[1,2,224]{2,1,0:T(2,128)} %param.14) | copy-start | bytes 5380
  31.8 54.8 %copy-start.5 = (f32[64]{0:T(128)S(1)}, f32[64]{0:T(128)}, u32[]{:S(2)}) copy-start(f32[64]{0:T(128)} %param.16) | copy-start | bytes 772
  79.4 1.2 copy-start.1
  81.7 23.1 %collective-permute-start.1 = (f32[32,7,1024]{2,0,1:T(8,128)}, f32[32,7,1024]{2,0,1:T(8,128)S(1)}, u32[]{:S(2)}, u32[]{:S(2)}) collective-permute-start(f32[32,7,1024]{2,0,1:T(8,128)} %dynamic-slice_bitcast_fusion), channel_id=1, source_target_pairs={{0,1},{1,0},{2,3},{3,2},{4,5},{5,4},{6,7},{7,6},{8,9},{9,8},{10,11... | collective-permute-start | bytes 2752520 | tf_op jit(solution)/shard_map/ppermute | solution.py:72
  107.7 33.6 %all-to-all-start.1 = ((f32[32,7,1024]{2,1,0:T(8,128)}), f32[32,7,1024]{2,1,0:T(8,128)S(1)}, u32[]{:S(2)}, u32[]{:S(2)}) async-start(f32[32,7,1024]{2,1,0:T(8,128)} %copy.48), calls=%async_computation.1 | async-start | bytes 2097152 | tf_op jit(solution)/shard_map/all_to_all | solution.py:74
  117.0 22.3 %collective-permute-start.2 = (f32[32,7,512]{2,0,1:T(8,128)S(1)}, f32[32,7,512]{2,0,1:T(8,128)S(1)}, u32[]{:S(2)}, u32[]{:S(2)}) collective-permute-start(f32[32,7,512]{2,0,1:T(8,128)S(1)} %dynamic-slice_bitcast_fusion.2), channel_id=1, source_target_pairs={{0,1},{1,0},{2,3},{3,2},{4,5},{5,4},{6,7},{7,6},{8,9},{9,8},{10,11... | collective-permute-start | bytes 1376264 | tf_op jit(solution)/shard_map/ppermute | solution.py:72
  141.3 28.3 %all-to-all-start.2 = ((f32[32,7,512]{2,1,0:T(8,128)}), f32[32,7,512]{2,1,0:T(8,128)S(1)}, u32[]{:S(2)}, u32[]{:S(2)}) async-start(f32[32,7,512]{2,1,0:T(8,128)} %copy.50), calls=%async_computation.2 | async-start | bytes 1048576 | tf_op jit(solution)/shard_map/all_to_all | solution.py:74
  151.8 17.4 %collective-permute-start.3 = (f32[32,7,512]{2,0,1:T(8,128)S(1)}, f32[32,7,512]{2,0,1:T(8,128)S(1)}, u32[]{:S(2)}, u32[]{:S(2)}) collective-permute-start(f32[32,7,512]{2,0,1:T(8,128)S(1)} %dynamic-slice_bitcast_fusion.1), channel_id=1, source_target_pairs={{0,1},{1,0},{2,3},{3,2},{4,5},{5,4},{6,7},{7,6},{8,9},{9,8},{10,11... | collective-permute-start | bytes 1376264 | tf_op jit(solution)/shard_map/ppermute | solution.py:72
Sparse Core Ops, SparseCore 0:
  9.1 54.3 all-gather.7
  65.4 33.6 all-gather.5
  100.9 33.3 all-gather.3

commit v9 on v8

--- a/solution.py
+++ b/solution.py
@@ -4,7 +4,7 @@
 from jax import lax
 from jax.sharding import Mesh, PartitionSpec as P
 
-CHUNK_PARTS = (8, 4, 4)
+CHUNK_PARTS = (9, 4, 3)
 
 
 def lookup(energy, idx):

time: 204 us -> 203 us (level)
  blocking collectives: 24 us -> 20.8 us
    all_to_all x1, blocking collectives: 24 us -> 20.8 us  [on_device(): outs.append(lax.all_to_all(payload, 'pair', 0, 0, tiled=True))]
    slice x2 -> x3, local copies, waits for them, and re-layouts: 4.69 us -> 6.1 us  [on_device(): piece = lax.all_gather(integrals[:, lo:hi], 'gy', axis=0, tiled=True)]
  transfers between devices with their start and end apart: 10 -> 10, of which waited for: 5 -> 5; matrix products, arithmetic and copies ran while one was open for 14% -> 15% of each run, Pallas kernels for 0% -> 0%
where the time goes in v9:
time: 203 us; the launch traced here: 202 us
  waiting for transfers between devices  97.3 us (48%)
  starting transfers between devices  33 us (16%)
  blocking collectives  20.8 us (10%)
  local copies, waits for them, and re-layouts  19.8 us (10%)
  matrix products  14 us (7%)
  between operations  13.4 us (7%)
  other arithmetic  3.89 us (2%)
    ppermute x3, waiting for transfers between devices, on_device(): works.append(keep + lax.ppermute(send, 'gx', swap))  52.5 us
    all_to_all x1, waiting for transfers between devices, on_device(): t_all = lax.all_to_all(spread, 'pair', 0, 0, tiled=True)  42.6 us
    all_to_all x1, blocking collectives, on_device(): outs.append(lax.all_to_all(payload, 'pair', 0, 0, tiled=True))  20.8 us
    dot_general x3, matrix products, on_device(): jnp.dot(lhs, piece, precision=lax.Precision.HIGH, preferred_element_type=...  14 us
    all_to_all x1, starting transfers between devices, on_device(): t_all = lax.all_to_all(spread, 'pair', 0, 0, tiled=True)  11.6 us
    all_to_all x2, starting transfers between devices, on_device(): outs.append(lax.all_to_all(payload, 'pair', 0, 0, tiled=True))  10.4 us
    ppermute x3, starting transfers between devices, on_device(): works.append(keep + lax.ppermute(send, 'gx', swap))  7.32 us
    slice x3, local copies, waits for them, and re-layouts, on_device(): piece = lax.all_gather(integrals[:, lo:hi], 'gy', axis=0, tiled=True)  6.1 us
  transfers between devices with their start and end apart: 10, of which 5 were waited for; matrix products, arithmetic and copies ran while one was open for 15% of the time, Pallas kernels for 0%

profile of v9, /device:TPU:1, one launch (start us, length us, event | category | flops | bytes accessed | tf_op | source)
XLA Modules:
  0.0 202.3 jit_solution(15734334797136145437)
XLA Ops:
  6.5 2.4 %slice.34 = f32[256,1152]{1,0:T(8,128)} slice(f32[256,2048]{1,0:T(8,128)} %param.12), slice={[0:256], [0:1152]} | slice | bytes 2359296 | tf_op jit(solution)/shard_map/slice | solution.py:63
  9.1 0.6 gather_fusion.2
  9.7 0.6 gather_fusion.3
  10.4 3.6 %collective-permute-start = (f32[7,1024]{1,0:T(8,128)S(1)}, f32[7,1024]{1,0:T(8,128)S(1)}, u32[]{:S(2)}, u32[]{:S(2)}) collective-permute-start(f32[7,1024]{1,0:T(8,128)S(1)} %select_bitcast_fusion), channel_id=1, source_target_pairs={{0,1},{1,0},{2,3},{3,2},{4,5},{5,4},{6,7},{7,6},{8,9},{9,8},{10,11... | collective-permute-start | bytes 86024 | tf_op jit(solution)/shard_map/ppermute | solution.py:46
  14.0 0.6 gather_fusion
  14.7 0.6 gather_fusion.1
  15.4 1.7 broadcast_in_dim.45
  17.1 11.6 %all-to-all-start = ((f32[32,2,7,1024]{3,1,2,0:T(2,128)}), f32[32,2,7,1024]{3,1,2,0:T(2,128)S(1)}, u32[]{:S(2)}, u32[]{:S(2)}) async-start(f32[32,2,7,1024]{3,1,2,0:T(2,128)} %broadcast_in_dim.45), calls=%async_computation | async-start | bytes 3670016 | tf_op jit(solution)/shard_map/all_to_all | solution.py:49
  28.7 1.9 slice.33
  30.7 42.6 %all-to-all-done = f32[32,2,7,1024]{3,1,2,0:T(2,128)S(1)} async-done(((f32[32,2,7,1024]{3,1,2,0:T(2,128)}), f32[32,2,7,1024]{3,1,2,0:T(2,128)S(1)}, u32[]{:S(2)}, u32[]{:S(2)}) %all-to-all-start) | async-done | bytes 1835040 | tf_op jit(solution)/shard_map/all_to_all | solution.py:49
  73.3 6.9 %fusion = f32[32,2,7,1152]{3,0,2,1:T(8,128)S(1)} fusion(f32[1024,1152]{1,0:T(8,128)} %all-gather.8.cloned.1.call-done, f32[32,2,7,1024]{3,1,2,0:T(2,128)S(1)} %all-to-all-done), kind=kOutput, calls=%fused_computation.4 | convolution fusion | flops 3170893824 | bytes 8617984 | tf_op jit(solution)/shard_map/dot_general | solution.py:68
  80.2 1.3 copy-done.1
  81.5 1.0 dynamic-slice_bitcast_fusion
  82.5 2.5 %collective-permute-start.1 = (f32[32,7,1152]{2,0,1:T(8,128)}, f32[32,7,1152]{2,0,1:T(8,128)S(1)}, u32[]{:S(2)}, u32[]{:S(2)}) collective-permute-start(f32[32,7,1152]{2,0,1:T(8,128)} %dynamic-slice_bitcast_fusion), channel_id=1, source_target_pairs={{0,1},{1,0},{2,3},{3,2},{4,5},{5,4},{6,7},{7,6},{8,9},{9,8},{10,11... | collective-permute-start | bytes 3096584 | tf_op jit(solution)/shard_map/ppermute | solution.py:72
  85.0 1.8 slice.32
  87.1 0.9 constant_dynamic-slice_fusion
  88.0 1.6 select_reduce_fusion
  89.6 18.5 %collective-permute-done.1 = f32[32,7,1152]{2,0,1:T(8,128)S(1)} collective-permute-done((f32[32,7,1152]{2,0,1:T(8,128)}, f32[32,7,1152]{2,0,1:T(8,128)S(1)}, u32[]{:S(2)}, u32[]{:S(2)}) %collective-permute-start.1) | collective-permute-done | bytes 1032224 | tf_op jit(solution)/shard_map/ppermute | solution.py:72
  108.1 1.5 subtract_divide_fusion
  109.6 1.6 copy.52
  111.2 5.5 %all-to-all-start.1 = ((f32[32,7,1152]{2,1,0:T(8,128)}), f32[32,7,1152]{2,1,0:T(8,128)S(1)}, u32[]{:S(2)}, u32[]{:S(2)}) async-start(f32[32,7,1152]{2,1,0:T(8,128)} %copy.52), calls=%async_computation.1 | async-start | bytes 2359296 | tf_op jit(solution)/shard_map/all_to_all | solution.py:74
  116.7 3.8 %fusion.2 = f32[32,2,7,512]{3,0,2,1:T(8,128)S(1)} fusion(f32[1024,512]{1,0:T(8,128)} %all-gather.6.cloned.1.call-done, f32[32,2,7,1024]{3,1,2,0:T(2,128)S(1)} %all-to-all-done), kind=kOutput, calls=%fused_computation.11 | convolution fusion | flops 1409286144 | bytes 4849664 | tf_op jit(solution)/shard_map/dot_general | solution.py:68
  120.6 2.7 %collective-permute-start.2 = (f32[32,7,512]{2,0,1:T(8,128)S(1)}, f32[32,7,512]{2,0,1:T(8,128)S(1)}, u32[]{:S(2)}, u32[]{:S(2)}) collective-permute-start(f32[32,7,512]{2,0,1:T(8,128)S(1)} %dynamic-slice_bitcast_fusion.1), channel_id=1, source_target_pairs={{0,1},{1,0},{2,3},{3,2},{4,5},{5,4},{6,7},{7,6},{8,9},{9,8},{10,11... | collective-permute-start | bytes 1376264 | tf_op jit(solution)/shard_map/ppermute | solution.py:72
  123.3 20.8 %collective-permute-done.2 = f32[32,7,512]{2,0,1:T(8,128)S(1)} collective-permute-done((f32[32,7,512]{2,0,1:T(8,128)S(1)}, f32[32,7,512]{2,0,1:T(8,128)S(1)}, u32[]{:S(2)}, u32[]{:S(2)}) %collective-permute-start.2) | collective-permute-done | bytes 458784 | tf_op jit(solution)/shard_map/ppermute | solution.py:72
  144.3 1.1 copy.54
  145.3 2.2 %all-to-all-done.1 = f32[32,7,1152]{2,1,0:T(8,128)S(1)} async-done(((f32[32,7,1152]{2,1,0:T(8,128)}), f32[32,7,1152]{2,1,0:T(8,128)S(1)}, u32[]{:S(2)}, u32[]{:S(2)}) %all-to-all-start.1) | async-done | bytes 1032224 | tf_op jit(solution)/shard_map/all_to_all | solution.py:74
  147.5 4.9 %all-to-all-start.2 = ((f32[32,7,512]{2,1,0:T(8,128)}), f32[32,7,512]{2,1,0:T(8,128)S(1)}, u32[]{:S(2)}, u32[]{:S(2)}) async-start(f32[32,7,512]{2,1,0:T(8,128)} %copy.54), calls=%async_computation.2 | async-start | bytes 1048576 | tf_op jit(solution)/shard_map/all_to_all | solution.py:74
  152.5 3.4 %fusion.4 = f32[32,2,7,384]{3,0,2,1:T(8,128)S(1)} fusion(f32[32,2,7,1024]{3,1,2,0:T(2,128)S(1)} %all-to-all-done, f32[1024,384]{1,0:T(8,128)} %all-gather.4.cloned.1.call-done), kind=kOutput, calls=%fused_computation.13 | convolution fusion | flops 1056964608 | bytes 4096000 | tf_op jit(solution)/shard_map/dot_general | solution.py:68
  155.9 2.2 %collective-permute-start.3 = (f32[32,7,384]{2,0,1:T(8,128)S(1)}, f32[32,7,384]{2,0,1:T(8,128)S(1)}, u32[]{:S(2)}, u32[]{:S(2)}) collective-permute-start(f32[32,7,384]{2,0,1:T(8,128)S(1)} %dynamic-slice_bitcast_fusion.2), channel_id=1, source_target_pairs={{0,1},{1,0},{2,3},{3,2},{4,5},{5,4},{6,7},{7,6},{8,9},{9,8},{10,11... | collective-permute-start | bytes 1032200 | tf_op jit(solution)/shard_map/ppermute | solution.py:72
  158.1 13.1 %collective-permute-done.3 = f32[32,7,384]{2,0,1:T(8,128)S(1)} collective-permute-done((f32[32,7,384]{2,0,1:T(8,128)S(1)}, f32[32,7,384]{2,0,1:T(8,128)S(1)}, u32[]{:S(2)}, u32[]{:S(2)}) %collective-permute-start.3) | collective-permute-done | bytes 344096 | tf_op jit(solution)/shard_map/ppermute | solution.py:72
  171.6 20.8 %all_to_all.20 = f32[32,7,384]{2,1,0:T(8,128)S(1)} all-to-all(f32[32,7,384]{2,1,0:T(8,128)S(1)} %copy.57), channel_id=1, replica_groups=mesh['pair'=32,'gy'=4,'gx'=2] {'pair'}, dimensions={0} | all-to-all | bytes 688128 | tf_op jit(solution)/shard_map/all_to_all | solution.py:74
  192.6 3.1 %copy.58 = f32[1,7,65536]{2,0,1:T(1,128)} copy(f32[1,7,65536]{2,1,0:T(8,128)S(1)} %bitcast.49) | data formatting | bytes 3670016 | tf_op jit(solution)/shard_map/reshape | solution.py:76
  (48 shorter events, 1.6 us)
Async XLA Ops:
  6.5 2.5 %copy-start = (s32[16]{0:T(128)S(1)}, s32[16]{0:T(128)}, u32[]{:S(2)}) copy-start(s32[16]{0:T(128)} %param.13) | copy-start | bytes 196
  6.5 2.4 %copy-start.2 = (f32[1,7,2048]{2,0,1:T(1,128)S(1)}, f32[1,7,2048]{2,0,1:T(1,128)}, u32[]{:S(2)}) copy-start(f32[1,7,2048]{2,0,1:T(1,128)} %param.11) | copy-start | bytes 172036
  6.5 66.8 %all-gather.8.cloned.1.call-start = ((), (), s32[]{:S(2)}) async-start(), calls=%async_computation.6 | async-start | bytes 5898240 | tf_op jit(solution)/shard_map/all_gather | solution.py:63
  10.4 4.9 %collective-permute-start = (f32[7,1024]{1,0:T(8,128)S(1)}, f32[7,1024]{1,0:T(8,128)S(1)}, u32[]{:S(2)}, u32[]{:S(2)}) collective-permute-start(f32[7,1024]{1,0:T(8,128)S(1)} %select_bitcast_fusion), channel_id=1, source_target_pairs={{0,1},{1,0},{2,3},{3,2},{4,5},{5,4},{6,7},{7,6},{8,9},{9,8},{10,11... | collective-permute-start | bytes 86024 | tf_op jit(solution)/shard_map/ppermute | solution.py:46
  17.1 56.2 %all-to-all-start = ((f32[32,2,7,1024]{3,1,2,0:T(2,128)}), f32[32,2,7,1024]{3,1,2,0:T(2,128)S(1)}, u32[]{:S(2)}, u32[]{:S(2)}) async-start(f32[32,2,7,1024]{3,1,2,0:T(2,128)} %broadcast_in_dim.45), calls=%async_computation | async-start | bytes 3670016 | tf_op jit(solution)/shard_map/all_to_all | solution.py:49
  28.7 88.0 %all-gather.6.cloned.1.call-start = ((), (), s32[]{:S(2)}) async-start(), calls=%async_computation.5 | async-start | bytes 2621440 | tf_op jit(solution)/shard_map/all_gather | solution.py:63
  30.7 113.6 %all-gather.4.cloned.1.call-start = ((), (), s32[]{:S(2)}) async-start(), calls=%async_computation.4 | async-start | bytes 1966080 | tf_op jit(solution)/shard_map/all_gather | solution.py:63
  80.2 1.3 copy-start.1
  81.5 5.3 %copy-start.4 = (s32[1,2,224]{2,1,0:T(2,128)S(1)}, s32[1,2,224]{2,1,0:T(2,128)}, u32[]{:S(2)}) copy-start(s32[1,2,224]{2,1,0:T(2,128)} %param.14) | copy-start | bytes 5380
  81.5 5.3 %copy-start.5 = (f32[64]{0:T(128)S(1)}, f32[64]{0:T(128)}, u32[]{:S(2)}) copy-start(f32[64]{0:T(128)} %param.16) | copy-start | bytes 772
  81.5 6.5 %copy-start.3 = (f32[512]{0:T(512)S(1)}, f32[512]{0:T(512)}, u32[]{:S(2)}) copy-start(f32[512]{0:T(512)} %param.17) | copy-start | bytes 6148
  82.5 25.6 %collective-permute-start.1 = (f32[32,7,1152]{2,0,1:T(8,128)}, f32[32,7,1152]{2,0,1:T(8,128)S(1)}, u32[]{:S(2)}, u32[]{:S(2)}) collective-permute-start(f32[32,7,1152]{2,0,1:T(8,128)} %dynamic-slice_bitcast_fusion), channel_id=1, source_target_pairs={{0,1},{1,0},{2,3},{3,2},{4,5},{5,4},{6,7},{7,6},{8,9},{9,8},{10,11... | collective-permute-start | bytes 3096584 | tf_op jit(solution)/shard_map/ppermute | solution.py:72
  111.2 36.4 %all-to-all-start.1 = ((f32[32,7,1152]{2,1,0:T(8,128)}), f32[32,7,1152]{2,1,0:T(8,128)S(1)}, u32[]{:S(2)}, u32[]{:S(2)}) async-start(f32[32,7,1152]{2,1,0:T(8,128)} %copy.52), calls=%async_computation.1 | async-start | bytes 2359296 | tf_op jit(solution)/shard_map/all_to_all | solution.py:74
  120.6 23.5 %collective-permute-start.2 = (f32[32,7,512]{2,0,1:T(8,128)S(1)}, f32[32,7,512]{2,0,1:T(8,128)S(1)}, u32[]{:S(2)}, u32[]{:S(2)}) collective-permute-start(f32[32,7,512]{2,0,1:T(8,128)S(1)} %dynamic-slice_bitcast_fusion.1), channel_id=1, source_target_pairs={{0,1},{1,0},{2,3},{3,2},{4,5},{5,4},{6,7},{7,6},{8,9},{9,8},{10,11... | collective-permute-start | bytes 1376264 | tf_op jit(solution)/shard_map/ppermute | solution.py:72
  147.5 24.0 %all-to-all-start.2 = ((f32[32,7,512]{2,1,0:T(8,128)}), f32[32,7,512]{2,1,0:T(8,128)S(1)}, u32[]{:S(2)}, u32[]{:S(2)}) async-start(f32[32,7,512]{2,1,0:T(8,128)} %copy.54), calls=%async_computation.2 | async-start | bytes 1048576 | tf_op jit(solution)/shard_map/all_to_all | solution.py:74
  155.9 15.3 %collective-permute-start.3 = (f32[32,7,384]{2,0,1:T(8,128)S(1)}, f32[32,7,384]{2,0,1:T(8,128)S(1)}, u32[]{:S(2)}, u32[]{:S(2)}) collective-permute-start(f32[32,7,384]{2,0,1:T(8,128)S(1)} %dynamic-slice_bitcast_fusion.2), channel_id=1, source_target_pairs={{0,1},{1,0},{2,3},{3,2},{4,5},{5,4},{6,7},{7,6},{8,9},{9,8},{10,11... | collective-permute-start | bytes 1032200 | tf_op jit(solution)/shard_map/ppermute | solution.py:72
Sparse Core Ops, SparseCore 0:
  9.1 58.7 all-gather.7
  69.7 33.7 all-gather.5
  105.4 29.0 all-gather.3

commit v10 on v9

--- a/solution.py
+++ b/solution.py
@@ -4,7 +4,7 @@
 from jax import lax
 from jax.sharding import Mesh, PartitionSpec as P
 
-CHUNK_PARTS = (9, 4, 3)
+CHUNK_PARTS = (10, 3, 3)
 
 
 def lookup(energy, idx):

time: 203 us -> 210 us (1.034)
  waiting for transfers between devices: 97.3 us -> 103 us
  starting transfers between devices: 33 us -> 35.7 us
  local copies, waits for them, and re-layouts: 19.8 us -> 17.5 us
    all_to_all x2, waiting for transfers between devices: 2.2 us -> 12.3 us  [on_device(): outs.append(lax.all_to_all(payload, 'pair', 0, 0, tiled=True))]
    ppermute x3, waiting for transfers between devices: 52.5 us -> 48.2 us  [on_device(): works.append(keep + lax.ppermute(send, 'gx', swap))]
    all_to_all x2, starting transfers between devices: 10.4 us -> 12.7 us  [on_device(): outs.append(lax.all_to_all(payload, 'pair', 0, 0, tiled=True))]
    slice x3 -> x2, local copies, waits for them, and re-layouts: 6.1 us -> 4.65 us  [on_device(): piece = lax.all_gather(integrals[:, lo:hi], 'gy', axis=0, tiled=True)]
  transfers between devices with their start and end apart: 10 -> 10, of which waited for: 5 -> 5; matrix products, arithmetic and copies ran while one was open for 15% -> 13% of each run, Pallas kernels for 0% -> 0%
where the time goes in v10:
time: 210 us; the launch traced here: 209 us
  waiting for transfers between devices  103 us (49%)
  starting transfers between devices  35.7 us (17%)
  blocking collectives  21.5 us (10%)
  local copies, waits for them, and re-layouts  17.5 us (8%)
  matrix products  13.7 us (7%)
  between operations  13.4 us (6%)
  other arithmetic  4.28 us (2%)
    ppermute x3, waiting for transfers between devices, on_device(): works.append(keep + lax.ppermute(send, 'gx', swap))  48.2 us
    all_to_all x1, waiting for transfers between devices, on_device(): t_all = lax.all_to_all(spread, 'pair', 0, 0, tiled=True)  42.4 us
    all_to_all x1, blocking collectives, on_device(): outs.append(lax.all_to_all(payload, 'pair', 0, 0, tiled=True))  21.5 us
    dot_general x3, matrix products, on_device(): jnp.dot(lhs, piece, precision=lax.Precision.HIGH, preferred_element_type=...  13.7 us
    all_to_all x2, starting transfers between devices, on_device(): outs.append(lax.all_to_all(payload, 'pair', 0, 0, tiled=True))  12.7 us
    all_to_all x2, waiting for transfers between devices, on_device(): outs.append(lax.all_to_all(payload, 'pair', 0, 0, tiled=True))  12.3 us
    all_to_all x1, starting transfers between devices, on_device(): t_all = lax.all_to_all(spread, 'pair', 0, 0, tiled=True)  11.6 us
    ppermute x3, starting transfers between devices, on_device(): works.append(keep + lax.ppermute(send, 'gx', swap))  7.72 us
  transfers between devices with their start and end apart: 10, of which 5 were waited for; matrix products, arithmetic and copies ran while one was open for 13% of the time, Pallas kernels for 0%

profile of v10, /device:TPU:1, one launch (start us, length us, event | category | flops | bytes accessed | tf_op | source)
XLA Modules:
  0.0 208.9 jit_solution(5923572952117857450)
XLA Ops:
  6.5 2.5 %slice.34 = f32[256,1280]{1,0:T(8,128)} slice(f32[256,2048]{1,0:T(8,128)} %param.12), slice={[0:256], [0:1280]} | slice | bytes 2621440 | tf_op jit(solution)/shard_map/slice | solution.py:63
  9.2 0.6 gather_fusion.2
  9.9 0.6 gather_fusion.3
  10.5 3.6 %collective-permute-start = (f32[7,1024]{1,0:T(8,128)S(1)}, f32[7,1024]{1,0:T(8,128)S(1)}, u32[]{:S(2)}, u32[]{:S(2)}) collective-permute-start(f32[7,1024]{1,0:T(8,128)S(1)} %select_bitcast_fusion), channel_id=1, source_target_pairs={{0,1},{1,0},{2,3},{3,2},{4,5},{5,4},{6,7},{7,6},{8,9},{9,8},{10,11... | collective-permute-start | bytes 86024 | tf_op jit(solution)/shard_map/ppermute | solution.py:46
  14.1 0.6 gather_fusion
  14.8 0.6 gather_fusion.1
  15.5 1.7 broadcast_in_dim.45
  17.2 11.6 %all-to-all-start = ((f32[32,2,7,1024]{3,1,2,0:T(2,128)}), f32[32,2,7,1024]{3,1,2,0:T(2,128)S(1)}, u32[]{:S(2)}, u32[]{:S(2)}) async-start(f32[32,2,7,1024]{3,1,2,0:T(2,128)} %broadcast_in_dim.45), calls=%async_computation | async-start | bytes 3670016 | tf_op jit(solution)/shard_map/all_to_all | solution.py:49
  28.8 2.1 %fusion.11 = (f32[256,384]{1,0:T(8,128)}, f32[256,384]{1,0:T(8,128)}) fusion(f32[256,2048]{1,0:T(8,128)} %param.12), kind=kLoop, calls=%fused_computation.53 | loop fusion | bytes 1572864 | tf_op jit(solution)/shard_map/slice | solution.py:63
  31.0 42.4 %all-to-all-done = f32[32,2,7,1024]{3,1,2,0:T(2,128)S(1)} async-done(((f32[32,2,7,1024]{3,1,2,0:T(2,128)}), f32[32,2,7,1024]{3,1,2,0:T(2,128)S(1)}, u32[]{:S(2)}, u32[]{:S(2)}) %all-to-all-start) | async-done | bytes 1835040 | tf_op jit(solution)/shard_map/all_to_all | solution.py:49
  73.4 7.0 %fusion = f32[32,2,7,1280]{3,0,2,1:T(8,128)S(1)} fusion(f32[1024,1280]{1,0:T(8,128)} %all-gather.8.cloned.1.call-done, f32[32,2,7,1024]{3,1,2,0:T(2,128)S(1)} %all-to-all-done), kind=kOutput, calls=%fused_computation.4 | convolution fusion | flops 3523215360 | bytes 9371648 | tf_op jit(solution)/shard_map/dot_general | solution.py:68
  80.4 1.4 copy-done.1
  81.9 2.5 %collective-permute-start.1 = (f32[32,7,1280]{2,0,1:T(8,128)S(1)}, f32[32,7,1280]{2,0,1:T(8,128)}, u32[]{:S(2)}, u32[]{:S(2)}) collective-permute-start(f32[32,7,1280]{2,0,1:T(8,128)S(1)} %dynamic-slice_bitcast_fusion), channel_id=1, source_target_pairs={{0,1},{1,0},{2,3},{3,2},{4,5},{5,4},{6,7},{7,6},{8,9},{9,8},{10,11... | collective-permute-start | bytes 3440648 | tf_op jit(solution)/shard_map/ppermute | solution.py:72
  84.8 0.9 constant_dynamic-slice_fusion
  85.7 1.6 select_reduce_fusion
  87.3 22.6 %collective-permute-done.1 = f32[32,7,1280]{2,0,1:T(8,128)} collective-permute-done((f32[32,7,1280]{2,0,1:T(8,128)S(1)}, f32[32,7,1280]{2,0,1:T(8,128)}, u32[]{:S(2)}, u32[]{:S(2)}) %collective-permute-start.1) | collective-permute-done | bytes 1146912 | tf_op jit(solution)/shard_map/ppermute | solution.py:72
  109.9 1.8 subtract_divide_fusion
  111.8 1.7 copy.48
  113.5 8.4 %all-to-all-start.1 = ((f32[32,7,1280]{2,1,0:T(8,128)}), f32[32,7,1280]{2,1,0:T(8,128)S(1)}, u32[]{:S(2)}, u32[]{:S(2)}) async-start(f32[32,7,1280]{2,1,0:T(8,128)} %copy.48), calls=%async_computation.1 | async-start | bytes 2621440 | tf_op jit(solution)/shard_map/all_to_all | solution.py:74
  121.9 3.4 %fusion.5 = f32[32,2,7,384]{3,0,2,1:T(8,128)S(1)} fusion(f32[32,2,7,1024]{3,1,2,0:T(2,128)S(1)} %all-to-all-done, f32[1024,384]{1,0:T(8,128)} %all-gather.6.cloned.1.call-done), kind=kOutput, calls=%fused_computation.14 | convolution fusion | flops 1056964608 | bytes 4096000 | tf_op jit(solution)/shard_map/dot_general | solution.py:68
  125.3 2.7 %collective-permute-start.2 = (f32[32,7,384]{2,0,1:T(8,128)S(1)}, f32[32,7,384]{2,0,1:T(8,128)S(1)}, u32[]{:S(2)}, u32[]{:S(2)}) collective-permute-start(f32[32,7,384]{2,0,1:T(8,128)S(1)} %dynamic-slice_bitcast_fusion.2), channel_id=1, source_target_pairs={{0,1},{1,0},{2,3},{3,2},{4,5},{5,4},{6,7},{7,6},{8,9},{9,8},{10,11... | collective-permute-start | bytes 1032200 | tf_op jit(solution)/shard_map/ppermute | solution.py:72
  128.0 14.2 %collective-permute-done.2 = f32[32,7,384]{2,0,1:T(8,128)S(1)} collective-permute-done((f32[32,7,384]{2,0,1:T(8,128)S(1)}, f32[32,7,384]{2,0,1:T(8,128)S(1)}, u32[]{:S(2)}, u32[]{:S(2)}) %collective-permute-start.2) | collective-permute-done | bytes 344096 | tf_op jit(solution)/shard_map/ppermute | solution.py:72
  142.4 1.0 copy.50
  143.3 12.3 %all-to-all-done.1 = f32[32,7,1280]{2,1,0:T(8,128)S(1)} async-done(((f32[32,7,1280]{2,1,0:T(8,128)}), f32[32,7,1280]{2,1,0:T(8,128)S(1)}, u32[]{:S(2)}, u32[]{:S(2)}) %all-to-all-start.1) | async-done | bytes 1146912 | tf_op jit(solution)/shard_map/all_to_all | solution.py:74
  155.6 4.3 %all-to-all-start.2 = ((f32[32,7,384]{2,1,0:T(8,128)}), f32[32,7,384]{2,1,0:T(8,128)S(1)}, u32[]{:S(2)}, u32[]{:S(2)}) async-start(f32[32,7,384]{2,1,0:T(8,128)} %copy.50), calls=%async_computation.2 | async-start | bytes 786432 | tf_op jit(solution)/shard_map/all_to_all | solution.py:74
  159.9 3.4 %fusion.2 = f32[32,2,7,384]{3,0,2,1:T(8,128)S(1)} fusion(f32[32,2,7,1024]{3,1,2,0:T(2,128)S(1)} %all-to-all-done, f32[1024,384]{1,0:T(8,128)} %all-gather.4.cloned.1.call-done), kind=kOutput, calls=%fused_computation.11 | convolution fusion | flops 1056964608 | bytes 4096000 | tf_op jit(solution)/shard_map/dot_general | solution.py:68
  163.3 2.5 %collective-permute-start.3 = (f32[32,7,384]{2,0,1:T(8,128)S(1)}, f32[32,7,384]{2,0,1:T(8,128)S(1)}, u32[]{:S(2)}, u32[]{:S(2)}) collective-permute-start(f32[32,7,384]{2,0,1:T(8,128)S(1)} %dynamic-slice_bitcast_fusion.1), channel_id=1, source_target_pairs={{0,1},{1,0},{2,3},{3,2},{4,5},{5,4},{6,7},{7,6},{8,9},{9,8},{10,11... | collective-permute-start | bytes 1032200 | tf_op jit(solution)/shard_map/ppermute | solution.py:72
  165.8 11.3 %collective-permute-done.3 = f32[32,7,384]{2,0,1:T(8,128)S(1)} collective-permute-done((f32[32,7,384]{2,0,1:T(8,128)S(1)}, f32[32,7,384]{2,0,1:T(8,128)S(1)}, u32[]{:S(2)}, u32[]{:S(2)}) %collective-permute-start.3) | collective-permute-done | bytes 344096 | tf_op jit(solution)/shard_map/ppermute | solution.py:72
  177.3 0.2 copy.52
  177.5 21.5 %all_to_all.20 = f32[32,7,384]{2,1,0:T(8,128)S(1)} all-to-all(f32[32,7,384]{2,1,0:T(8,128)S(1)} %copy.52), channel_id=1, replica_groups=mesh['pair'=32,'gy'=4,'gx'=2] {'pair'}, dimensions={0} | all-to-all | bytes 688128 | tf_op jit(solution)/shard_map/all_to_all | solution.py:74
  199.0 0.3 pad_maximum_fusion
  199.3 3.1 %copy.53 = f32[1,7,65536]{2,0,1:T(1,128)} copy(f32[1,7,65536]{2,1,0:T(8,128)S(1)} %bitcast.49) | data formatting | bytes 3670016 | tf_op jit(solution)/shard_map/reshape | solution.py:76
  (46 shorter events, 1.2 us)
Async XLA Ops:
  6.5 2.6 %copy-start = (s32[16]{0:T(128)S(1)}, s32[16]{0:T(128)}, u32[]{:S(2)}) copy-start(s32[16]{0:T(128)} %param.13) | copy-start | bytes 196
  6.5 2.6 %copy-start.2 = (f32[1,7,2048]{2,0,1:T(1,128)S(1)}, f32[1,7,2048]{2,0,1:T(1,128)}, u32[]{:S(2)}) copy-start(f32[1,7,2048]{2,0,1:T(1,128)} %param.11) | copy-start | bytes 172036
  6.5 66.9 %all-gather.8.cloned.1.call-start = ((), (), s32[]{:S(2)}) async-start(), calls=%async_computation.6 | async-start | bytes 6553600 | tf_op jit(solution)/shard_map/all_gather | solution.py:63
  10.5 4.9 %collective-permute-start = (f32[7,1024]{1,0:T(8,128)S(1)}, f32[7,1024]{1,0:T(8,128)S(1)}, u32[]{:S(2)}, u32[]{:S(2)}) collective-permute-start(f32[7,1024]{1,0:T(8,128)S(1)} %select_bitcast_fusion), channel_id=1, source_target_pairs={{0,1},{1,0},{2,3},{3,2},{4,5},{5,4},{6,7},{7,6},{8,9},{9,8},{10,11... | collective-permute-start | bytes 86024 | tf_op jit(solution)/shard_map/ppermute | solution.py:46
  17.2 56.2 %all-to-all-start = ((f32[32,2,7,1024]{3,1,2,0:T(2,128)}), f32[32,2,7,1024]{3,1,2,0:T(2,128)S(1)}, u32[]{:S(2)}, u32[]{:S(2)}) async-start(f32[32,2,7,1024]{3,1,2,0:T(2,128)} %broadcast_in_dim.45), calls=%async_computation | async-start | bytes 3670016 | tf_op jit(solution)/shard_map/all_to_all | solution.py:49
  28.8 93.1 %all-gather.6.cloned.1.call-start = ((), (), s32[]{:S(2)}) async-start(), calls=%async_computation.5 | async-start | bytes 1966080 | tf_op jit(solution)/shard_map/all_gather | solution.py:63
  31.0 111.4 %all-gather.4.cloned.1.call-start = ((), (), s32[]{:S(2)}) async-start(), calls=%async_computation.4 | async-start | bytes 1966080 | tf_op jit(solution)/shard_map/all_gather | solution.py:63
  80.4 1.4 copy-start.1
  81.8 2.7 %copy-start.4 = (s32[1,2,224]{2,1,0:T(2,128)S(1)}, s32[1,2,224]{2,1,0:T(2,128)}, u32[]{:S(2)}) copy-start(s32[1,2,224]{2,1,0:T(2,128)} %param.14) | copy-start | bytes 5380
  81.8 2.7 %copy-start.5 = (f32[64]{0:T(128)S(1)}, f32[64]{0:T(128)}, u32[]{:S(2)}) copy-start(f32[64]{0:T(128)} %param.16) | copy-start | bytes 772
  81.8 3.9 %copy-start.3 = (f32[512]{0:T(512)S(1)}, f32[512]{0:T(512)}, u32[]{:S(2)}) copy-start(f32[512]{0:T(512)} %param.17) | copy-start | bytes 6148
  81.9 28.0 %collective-permute-start.1 = (f32[32,7,1280]{2,0,1:T(8,128)S(1)}, f32[32,7,1280]{2,0,1:T(8,128)}, u32[]{:S(2)}, u32[]{:S(2)}) collective-permute-start(f32[32,7,1280]{2,0,1:T(8,128)S(1)} %dynamic-slice_bitcast_fusion), channel_id=1, source_target_pairs={{0,1},{1,0},{2,3},{3,2},{4,5},{5,4},{6,7},{7,6},{8,9},{9,8},{10,11... | collective-permute-start | bytes 3440648 | tf_op jit(solution)/shard_map/ppermute | solution.py:72
  113.5 42.1 %all-to-all-start.1 = ((f32[32,7,1280]{2,1,0:T(8,128)}), f32[32,7,1280]{2,1,0:T(8,128)S(1)}, u32[]{:S(2)}, u32[]{:S(2)}) async-start(f32[32,7,1280]{2,1,0:T(8,128)} %copy.48), calls=%async_computation.1 | async-start | bytes 2621440 | tf_op jit(solution)/shard_map/all_to_all | solution.py:74
  125.3 16.9 %collective-permute-start.2 = (f32[32,7,384]{2,0,1:T(8,128)S(1)}, f32[32,7,384]{2,0,1:T(8,128)S(1)}, u32[]{:S(2)}, u32[]{:S(2)}) collective-permute-start(f32[32,7,384]{2,0,1:T(8,128)S(1)} %dynamic-slice_bitcast_fusion.2), channel_id=1, source_target_pairs={{0,1},{1,0},{2,3},{3,2},{4,5},{5,4},{6,7},{7,6},{8,9},{9,8},{10,11... | collective-permute-start | bytes 1032200 | tf_op jit(solution)/shard_map/ppermute | solution.py:72
  155.6 21.9 %all-to-all-start.2 = ((f32[32,7,384]{2,1,0:T(8,128)}), f32[32,7,384]{2,1,0:T(8,128)S(1)}, u32[]{:S(2)}, u32[]{:S(2)}) async-start(f32[32,7,384]{2,1,0:T(8,128)} %copy.50), calls=%async_computation.2 | async-start | bytes 786432 | tf_op jit(solution)/shard_map/all_to_all | solution.py:74
  163.3 13.8 %collective-permute-start.3 = (f32[32,7,384]{2,0,1:T(8,128)S(1)}, f32[32,7,384]{2,0,1:T(8,128)S(1)}, u32[]{:S(2)}, u32[]{:S(2)}) collective-permute-start(f32[32,7,384]{2,0,1:T(8,128)S(1)} %dynamic-slice_bitcast_fusion.1), channel_id=1, source_target_pairs={{0,1},{1,0},{2,3},{3,2},{4,5},{5,4},{6,7},{7,6},{8,9},{9,8},{10,11... | collective-permute-start | bytes 1032200 | tf_op jit(solution)/shard_map/ppermute | solution.py:72
Sparse Core Ops, SparseCore 0:
  9.2 63.1 all-gather.7
  74.2 29.5 all-gather.5
  105.5 29.0 all-gather.3

commit v11 on v10

--- a/solution.py
+++ b/solution.py
@@ -4,7 +4,7 @@
 from jax import lax
 from jax.sharding import Mesh, PartitionSpec as P
 
-CHUNK_PARTS = (10, 3, 3)
+CHUNK_PARTS = (9, 5, 2)
 
 
 def lookup(energy, idx):

time: 210 us -> 204 us (0.971)
  blocking collectives: 21.5 us -> 16.1 us
  waiting for transfers between devices: 103 us -> 99.3 us
  local copies, waits for them, and re-layouts: 17.5 us -> 20 us
    all_to_all x2, waiting for transfers between devices: 12.3 us -> 3.47 us  [on_device(): outs.append(lax.all_to_all(payload, 'pair', 0, 0, tiled=True))]
    all_to_all x1, blocking collectives: 21.5 us -> 16.1 us  [on_device(): outs.append(lax.all_to_all(payload, 'pair', 0, 0, tiled=True))]
    ppermute x3, waiting for transfers between devices: 48.2 us -> 53.3 us  [on_device(): works.append(keep + lax.ppermute(send, 'gx', swap))]
    slice x2 -> x3, local copies, waits for them, and re-layouts: 4.65 us -> 6.22 us  [on_device(): piece = lax.all_gather(integrals[:, lo:hi], 'gy', axis=0, tiled=True)]
  transfers between devices with their start and end apart: 10 -> 10, of which waited for: 5 -> 5; matrix products, arithmetic and copies ran while one was open for 13% -> 15% of each run, Pallas kernels for 0% -> 0%
where the time goes in v11:
time: 204 us
  waiting for transfers between devices  99.3 us (49%)
  starting transfers between devices  35.7 us (18%)
  local copies, waits for them, and re-layouts  20 us (10%)
  blocking collectives  16.1 us (8%)
  matrix products  14.2 us (7%)
  between operations  13.4 us (7%)
  other arithmetic  5 us (2%)
    ppermute x3, waiting for transfers between devices, on_device(): works.append(keep + lax.ppermute(send, 'gx', swap))  53.3 us
    all_to_all x1, waiting for transfers between devices, on_device(): t_all = lax.all_to_all(spread, 'pair', 0, 0, tiled=True)  42.5 us
    all_to_all x1, blocking collectives, on_device(): outs.append(lax.all_to_all(payload, 'pair', 0, 0, tiled=True))  16.1 us
    dot_general x3, matrix products, on_device(): jnp.dot(lhs, piece, precision=lax.Precision.HIGH, preferred_element_type=...  14.2 us
    all_to_all x2, starting transfers between devices, on_device(): outs.append(lax.all_to_all(payload, 'pair', 0, 0, tiled=True))  13.1 us
    all_to_all x1, starting transfers between devices, on_device(): t_all = lax.all_to_all(spread, 'pair', 0, 0, tiled=True)  11.6 us
    ppermute x3, starting transfers between devices, on_device(): works.append(keep + lax.ppermute(send, 'gx', swap))  7.19 us
    slice x3, local copies, waits for them, and re-layouts, on_device(): piece = lax.all_gather(integrals[:, lo:hi], 'gy', axis=0, tiled=True)  6.22 us
  transfers between devices with their start and end apart: 10, of which 5 were waited for; matrix products, arithmetic and copies ran while one was open for 15% of the time, Pallas kernels for 0%

profile of v11, /device:TPU:1, one launch (start us, length us, event | category | flops | bytes accessed | tf_op | source)
XLA Modules:
  0.0 203.7 jit_solution(48155878922542649)
XLA Ops:
  6.5 2.5 %slice.34 = f32[256,1152]{1,0:T(8,128)} slice(f32[256,2048]{1,0:T(8,128)} %param.12), slice={[0:256], [0:1152]} | slice | bytes 2359296 | tf_op jit(solution)/shard_map/slice | solution.py:63
  9.2 0.6 gather_fusion.2
  9.8 0.6 gather_fusion.3
  10.5 3.6 %collective-permute-start = (f32[7,1024]{1,0:T(8,128)S(1)}, f32[7,1024]{1,0:T(8,128)S(1)}, u32[]{:S(2)}, u32[]{:S(2)}) collective-permute-start(f32[7,1024]{1,0:T(8,128)S(1)} %select_bitcast_fusion), channel_id=1, source_target_pairs={{0,1},{1,0},{2,3},{3,2},{4,5},{5,4},{6,7},{7,6},{8,9},{9,8},{10,11... | collective-permute-start | bytes 86024 | tf_op jit(solution)/shard_map/ppermute | solution.py:46
  14.1 0.6 gather_fusion
  15.5 1.7 broadcast_in_dim.45
  17.2 11.6 %all-to-all-start = ((f32[32,2,7,1024]{3,1,2,0:T(2,128)}), f32[32,2,7,1024]{3,1,2,0:T(2,128)S(1)}, u32[]{:S(2)}, u32[]{:S(2)}) async-start(f32[32,2,7,1024]{3,1,2,0:T(2,128)} %broadcast_in_dim.45), calls=%async_computation | async-start | bytes 3670016 | tf_op jit(solution)/shard_map/all_to_all | solution.py:49
  28.8 2.1 %slice.33 = f32[256,640]{1,0:T(8,128)} slice(f32[256,2048]{1,0:T(8,128)} %param.12), slice={[0:256], [1152:1792]} | slice | bytes 1310720 | tf_op jit(solution)/shard_map/slice | solution.py:63
  30.9 42.5 %all-to-all-done = f32[32,2,7,1024]{3,1,2,0:T(2,128)S(1)} async-done(((f32[32,2,7,1024]{3,1,2,0:T(2,128)}), f32[32,2,7,1024]{3,1,2,0:T(2,128)S(1)}, u32[]{:S(2)}, u32[]{:S(2)}) %all-to-all-start) | async-done | bytes 1835040 | tf_op jit(solution)/shard_map/all_to_all | solution.py:49
  73.4 6.9 %fusion = f32[32,2,7,1152]{3,0,2,1:T(8,128)S(1)} fusion(f32[1024,1152]{1,0:T(8,128)} %all-gather.8.cloned.1.call-done, f32[32,2,7,1024]{3,1,2,0:T(2,128)S(1)} %all-to-all-done), kind=kOutput, calls=%fused_computation.4 | convolution fusion | flops 3170893824 | bytes 8617984 | tf_op jit(solution)/shard_map/dot_general | solution.py:68
  80.3 1.3 copy-done.1
  81.6 1.0 dynamic-slice_bitcast_fusion
  82.6 2.5 %collective-permute-start.1 = (f32[32,7,1152]{2,0,1:T(8,128)}, f32[32,7,1152]{2,0,1:T(8,128)S(1)}, u32[]{:S(2)}, u32[]{:S(2)}) collective-permute-start(f32[32,7,1152]{2,0,1:T(8,128)} %dynamic-slice_bitcast_fusion), channel_id=1, source_target_pairs={{0,1},{1,0},{2,3},{3,2},{4,5},{5,4},{6,7},{7,6},{8,9},{9,8},{10,11... | collective-permute-start | bytes 3096584 | tf_op jit(solution)/shard_map/ppermute | solution.py:72
  85.4 0.9 constant_dynamic-slice_fusion
  86.3 1.6 select_reduce_fusion
  87.9 20.3 %collective-permute-done.1 = f32[32,7,1152]{2,0,1:T(8,128)S(1)} collective-permute-done((f32[32,7,1152]{2,0,1:T(8,128)}, f32[32,7,1152]{2,0,1:T(8,128)S(1)}, u32[]{:S(2)}, u32[]{:S(2)}) %collective-permute-start.1) | collective-permute-done | bytes 1032224 | tf_op jit(solution)/shard_map/ppermute | solution.py:72
  108.2 1.5 subtract_divide_fusion
  109.7 1.6 copy.52
  111.3 5.5 %all-to-all-start.1 = ((f32[32,7,1152]{2,1,0:T(8,128)}), f32[32,7,1152]{2,1,0:T(8,128)S(1)}, u32[]{:S(2)}, u32[]{:S(2)}) async-start(f32[32,7,1152]{2,1,0:T(8,128)} %copy.52), calls=%async_computation.1 | async-start | bytes 2359296 | tf_op jit(solution)/shard_map/all_to_all | solution.py:74
  117.0 1.7 slice.32
  118.7 4.7 %fusion.2 = f32[32,2,7,640]{3,0,2,1:T(8,128)S(1)} fusion(f32[1024,640]{1,0:T(8,128)} %all-gather.6.cloned.1.call-done, f32[32,2,7,1024]{3,1,2,0:T(2,128)S(1)} %all-to-all-done), kind=kOutput, calls=%fused_computation.10 | convolution fusion | flops 1761607680 | bytes 5603328 | tf_op jit(solution)/shard_map/dot_general | solution.py:68
  123.5 2.5 %collective-permute-start.2 = (f32[32,7,640]{2,0,1:T(8,128)S(1)}, f32[32,7,640]{2,0,1:T(8,128)S(1)}, u32[]{:S(2)}, u32[]{:S(2)}) collective-permute-start(f32[32,7,640]{2,0,1:T(8,128)S(1)} %dynamic-slice_bitcast_fusion.1), channel_id=1, source_target_pairs={{0,1},{1,0},{2,3},{3,2},{4,5},{5,4},{6,7},{7,6},{8,9},{9,8},{10,11... | collective-permute-start | bytes 1720328 | tf_op jit(solution)/shard_map/ppermute | solution.py:72
  126.1 22.0 %collective-permute-done.2 = f32[32,7,640]{2,0,1:T(8,128)S(1)} collective-permute-done((f32[32,7,640]{2,0,1:T(8,128)S(1)}, f32[32,7,640]{2,0,1:T(8,128)S(1)}, u32[]{:S(2)}, u32[]{:S(2)}) %collective-permute-start.2) | collective-permute-done | bytes 573472 | tf_op jit(solution)/shard_map/ppermute | solution.py:72
  148.2 1.2 copy.54
  149.4 7.6 %all-to-all-start.2 = ((f32[32,7,640]{2,1,0:T(8,128)}), f32[32,7,640]{2,1,0:T(8,128)}, u32[]{:S(2)}, u32[]{:S(2)}) async-start(f32[32,7,640]{2,1,0:T(8,128)} %copy.54), calls=%async_computation.2 | async-start | bytes 1310720 | tf_op jit(solution)/shard_map/all_to_all | solution.py:74
  157.0 2.6 %fusion.4 = f32[32,2,7,256]{3,0,2,1:T(8,128)S(1)} fusion(f32[32,2,7,1024]{3,1,2,0:T(2,128)S(1)} %all-to-all-done, f32[1024,256]{1,0:T(8,128)} %all-gather.4.cloned.1.call-done), kind=kOutput, calls=%fused_computation.13 | convolution fusion | flops 704643072 | bytes 3342336 | tf_op jit(solution)/shard_map/dot_general | solution.py:68
  159.7 2.2 %collective-permute-start.3 = (f32[32,7,256]{2,0,1:T(8,128)S(1)}, f32[32,7,256]{2,0,1:T(8,128)S(1)}, u32[]{:S(2)}, u32[]{:S(2)}) collective-permute-start(f32[32,7,256]{2,0,1:T(8,128)S(1)} %dynamic-slice_bitcast_fusion.2), channel_id=1, source_target_pairs={{0,1},{1,0},{2,3},{3,2},{4,5},{5,4},{6,7},{7,6},{8,9},{9,8},{10,11... | collective-permute-start | bytes 688136 | tf_op jit(solution)/shard_map/ppermute | solution.py:72
  161.9 11.0 %collective-permute-done.3 = f32[32,7,256]{2,0,1:T(8,128)S(1)} collective-permute-done((f32[32,7,256]{2,0,1:T(8,128)S(1)}, f32[32,7,256]{2,0,1:T(8,128)S(1)}, u32[]{:S(2)}, u32[]{:S(2)}) %collective-permute-start.3) | collective-permute-done | bytes 229408 | tf_op jit(solution)/shard_map/ppermute | solution.py:72
  173.1 3.5 %all-to-all-done.2 = f32[32,7,640]{2,1,0:T(8,128)} async-done(((f32[32,7,640]{2,1,0:T(8,128)}), f32[32,7,640]{2,1,0:T(8,128)}, u32[]{:S(2)}, u32[]{:S(2)}) %all-to-all-start.2) | async-done | bytes 573472 | tf_op jit(solution)/shard_map/all_to_all | solution.py:74
  176.6 16.1 %all_to_all.20 = f32[32,7,256]{2,1,0:T(8,128)S(1)} all-to-all(f32[32,7,256]{2,1,0:T(8,128)S(1)} %copy.57), channel_id=1, replica_groups=mesh['pair'=32,'gy'=4,'gx'=2] {'pair'}, dimensions={0} | all-to-all | bytes 458752 | tf_op jit(solution)/shard_map/all_to_all | solution.py:74
  192.7 1.4 pad_maximum_fusion
  194.1 3.1 %copy.58 = f32[1,7,65536]{2,0,1:T(1,128)} copy(f32[1,7,65536]{2,1,0:T(8,128)S(1)} %bitcast.49) | data formatting | bytes 3670016 | tf_op jit(solution)/shard_map/reshape | solution.py:76
  (48 shorter events, 2.0 us)
Async XLA Ops:
  6.5 2.6 %copy-start = (s32[16]{0:T(128)S(1)}, s32[16]{0:T(128)}, u32[]{:S(2)}) copy-start(s32[16]{0:T(128)} %param.13) | copy-start | bytes 196
  6.5 2.5 %copy-start.2 = (f32[1,7,2048]{2,0,1:T(1,128)S(1)}, f32[1,7,2048]{2,0,1:T(1,128)}, u32[]{:S(2)}) copy-start(f32[1,7,2048]{2,0,1:T(1,128)} %param.11) | copy-start | bytes 172036
  6.5 66.8 %all-gather.8.cloned.1.call-start = ((), (), s32[]{:S(2)}) async-start(), calls=%async_computation.6 | async-start | bytes 5898240 | tf_op jit(solution)/shard_map/all_gather | solution.py:63
  10.5 4.9 %collective-permute-start = (f32[7,1024]{1,0:T(8,128)S(1)}, f32[7,1024]{1,0:T(8,128)S(1)}, u32[]{:S(2)}, u32[]{:S(2)}) collective-permute-start(f32[7,1024]{1,0:T(8,128)S(1)} %select_bitcast_fusion), channel_id=1, source_target_pairs={{0,1},{1,0},{2,3},{3,2},{4,5},{5,4},{6,7},{7,6},{8,9},{9,8},{10,11... | collective-permute-start | bytes 86024 | tf_op jit(solution)/shard_map/ppermute | solution.py:46
  17.2 56.2 %all-to-all-start = ((f32[32,2,7,1024]{3,1,2,0:T(2,128)}), f32[32,2,7,1024]{3,1,2,0:T(2,128)S(1)}, u32[]{:S(2)}, u32[]{:S(2)}) async-start(f32[32,2,7,1024]{3,1,2,0:T(2,128)} %broadcast_in_dim.45), calls=%async_computation | async-start | bytes 3670016 | tf_op jit(solution)/shard_map/all_to_all | solution.py:49
  28.8 90.0 %all-gather.6.cloned.1.call-start = ((), (), s32[]{:S(2)}) async-start(), calls=%async_computation.5 | async-start | bytes 3276800 | tf_op jit(solution)/shard_map/all_gather | solution.py:63
  80.3 1.3 copy-start.1
  81.6 3.5 %copy-start.4 = (s32[1,2,224]{2,1,0:T(2,128)S(1)}, s32[1,2,224]{2,1,0:T(2,128)}, u32[]{:S(2)}) copy-start(s32[1,2,224]{2,1,0:T(2,128)} %param.14) | copy-start | bytes 5380
  81.6 3.5 %copy-start.5 = (f32[64]{0:T(128)S(1)}, f32[64]{0:T(128)}, u32[]{:S(2)}) copy-start(f32[64]{0:T(128)} %param.16) | copy-start | bytes 772
  81.6 4.7 %copy-start.3 = (f32[512]{0:T(512)S(1)}, f32[512]{0:T(512)}, u32[]{:S(2)}) copy-start(f32[512]{0:T(512)} %param.17) | copy-start | bytes 6148
  82.6 25.6 %collective-permute-start.1 = (f32[32,7,1152]{2,0,1:T(8,128)}, f32[32,7,1152]{2,0,1:T(8,128)S(1)}, u32[]{:S(2)}, u32[]{:S(2)}) collective-permute-start(f32[32,7,1152]{2,0,1:T(8,128)} %dynamic-slice_bitcast_fusion), channel_id=1, source_target_pairs={{0,1},{1,0},{2,3},{3,2},{4,5},{5,4},{6,7},{7,6},{8,9},{9,8},{10,11... | collective-permute-start | bytes 3096584 | tf_op jit(solution)/shard_map/ppermute | solution.py:72
  111.3 38.1 %all-to-all-start.1 = ((f32[32,7,1152]{2,1,0:T(8,128)}), f32[32,7,1152]{2,1,0:T(8,128)S(1)}, u32[]{:S(2)}, u32[]{:S(2)}) async-start(f32[32,7,1152]{2,1,0:T(8,128)} %copy.52), calls=%async_computation.1 | async-start | bytes 2359296 | tf_op jit(solution)/shard_map/all_to_all | solution.py:74
  116.8 40.2 %all-gather.4.cloned.1.call-start = ((), (), s32[]{:S(2)}) async-start(), calls=%async_computation.4 | async-start | bytes 1310720 | tf_op jit(solution)/shard_map/all_gather | solution.py:63
  123.5 24.5 %collective-permute-start.2 = (f32[32,7,640]{2,0,1:T(8,128)S(1)}, f32[32,7,640]{2,0,1:T(8,128)S(1)}, u32[]{:S(2)}, u32[]{:S(2)}) collective-permute-start(f32[32,7,640]{2,0,1:T(8,128)S(1)} %dynamic-slice_bitcast_fusion.1), channel_id=1, source_target_pairs={{0,1},{1,0},{2,3},{3,2},{4,5},{5,4},{6,7},{7,6},{8,9},{9,8},{10,11... | collective-permute-start | bytes 1720328 | tf_op jit(solution)/shard_map/ppermute | solution.py:72
  149.4 27.2 %all-to-all-start.2 = ((f32[32,7,640]{2,1,0:T(8,128)}), f32[32,7,640]{2,1,0:T(8,128)}, u32[]{:S(2)}, u32[]{:S(2)}) async-start(f32[32,7,640]{2,1,0:T(8,128)} %copy.54), calls=%async_computation.2 | async-start | bytes 1310720 | tf_op jit(solution)/shard_map/all_to_all | solution.py:74
  159.7 13.2 %collective-permute-start.3 = (f32[32,7,256]{2,0,1:T(8,128)S(1)}, f32[32,7,256]{2,0,1:T(8,128)S(1)}, u32[]{:S(2)}, u32[]{:S(2)}) collective-permute-start(f32[32,7,256]{2,0,1:T(8,128)S(1)} %dynamic-slice_bitcast_fusion.2), channel_id=1, source_target_pairs={{0,1},{1,0},{2,3},{3,2},{4,5},{5,4},{6,7},{7,6},{8,9},{9,8},{10,11... | collective-permute-start | bytes 688136 | tf_op jit(solution)/shard_map/ppermute | solution.py:72
Sparse Core Ops, SparseCore 0:
  9.2 58.7 all-gather.7
  69.8 38.1 all-gather.5
  119.4 25.5 all-gather.3

commit v12 on v9

--- a/solution.py
+++ b/solution.py
@@ -40,13 +40,10 @@
     def select(x):
         return jnp.take(tau, half_blocks(x), axis=1).reshape(rows_l, -1)
 
-    mine = select(gx)
-    other = select(1 - gx)
+    halves = jnp.stack([select(x) for x in range(nx)])
+    spread = jnp.broadcast_to(halves[None], (npair,) + halves.shape).reshape((npair * nx,) + halves.shape[1:])
+    t_all = lax.all_to_all(spread, ("pair", "gx"), 0, 0, tiled=True)
     swap = [(0, 1), (1, 0)]
-    got = lax.ppermute(other, "gx", swap)
-    both = jnp.where(gx == 0, jnp.stack([mine, got]), jnp.stack([got, mine]))
-    spread = jnp.broadcast_to(both[None], (npair,) + both.shape)
-    t_all = lax.all_to_all(spread, "pair", 0, 0, tiled=True)
     lhs = t_all.reshape(npair * nx * rows_l, -1)
 
     occ_sum = pair_energies(occ_energy, occ_pairs[0]).reshape(npair, rows_l)

time: 203 us -> 211 us (1.039)
  starting transfers between devices: 33 us -> 35.3 us
    all_to_all x2, starting transfers between devices: 10.4 us -> 15.4 us  [on_device(): outs.append(lax.all_to_all(payload, 'pair', 0, 0, tiled=True))]
    all_to_all x1, waiting for transfers between devices: 42.6 us -> 47.5 us  [on_device(): t_all = lax.all_to_all(spread, ('pair', 'gx'), 0, 0, tiled=True)]
    ppermute x1 -> x0, starting transfers between devices: 3.62 us -> none  [on_device(): got = lax.ppermute(other, 'gx', swap)]
    all_to_all x2, waiting for transfers between devices: 2.2 us -> 0.01 us  [on_device(): outs.append(lax.all_to_all(payload, 'pair', 0, 0, tiled=True))]
  transfers between devices with their start and end apart: 10 -> 9, of which waited for: 5 -> 4; matrix products, arithmetic and copies ran while one was open for 15% -> 16% of each run, Pallas kernels for 0% -> 0%
where the time goes in v12:
time: 211 us; the launch traced here: 210 us
  waiting for transfers between devices  98.2 us (47%)
  starting transfers between devices  35.3 us (17%)
  blocking collectives  21.6 us (10%)
  local copies, waits for them, and re-layouts  20.7 us (10%)
  matrix products  15.3 us (7%)
  between operations  13.4 us (6%)
  other arithmetic  5.73 us (3%)
    ppermute x3, waiting for transfers between devices, on_device(): works.append(keep + lax.ppermute(send, 'gx', swap))  50.6 us
    all_to_all x1, waiting for transfers between devices, on_device(): t_all = lax.all_to_all(spread, ('pair', 'gx'), 0, 0, tiled=True)  47.5 us
    all_to_all x1, blocking collectives, on_device(): outs.append(lax.all_to_all(payload, 'pair', 0, 0, tiled=True))  21.6 us
    all_to_all x2, starting transfers between devices, on_device(): outs.append(lax.all_to_all(payload, 'pair', 0, 0, tiled=True))  15.4 us
    dot_general x3, matrix products, on_device(): jnp.dot(lhs, piece, precision=lax.Precision.HIGH, preferred_element_type=...  15.3 us
    all_to_all x1, starting transfers between devices, on_device(): t_all = lax.all_to_all(spread, ('pair', 'gx'), 0, 0, tiled=True)  13 us
    ppermute x3, starting transfers between devices, on_device(): works.append(keep + lax.ppermute(send, 'gx', swap))  6.83 us
    slice x3, local copies, waits for them, and re-layouts, on_device(): piece = lax.all_gather(integrals[:, lo:hi], 'gy', axis=0, tiled=True)  6.09 us
  transfers between devices with their start and end apart: 9, of which 4 were waited for; matrix products, arithmetic and copies ran while one was open for 16% of the time, Pallas kernels for 0%

profile of v12, /device:TPU:1, one launch (start us, length us, event | category | flops | bytes accessed | tf_op | source)
XLA Modules:
  0.0 210.2 jit_solution(4733313852502052399)
XLA Ops:
  6.5 2.4 %slice.34 = f32[256,1152]{1,0:T(8,128)} slice(f32[256,2048]{1,0:T(8,128)} %param.12), slice={[0:256], [0:1152]} | slice | bytes 2359296 | tf_op jit(solution)/shard_map/slice | solution.py:60
  9.0 0.6 gather_fusion.2
  9.7 0.6 gather_fusion
  10.4 0.6 gather_fusion.3
  11.0 0.6 gather_fusion.1
  11.7 1.6 broadcast_in_dim.45
  13.3 13.0 %all-to-all-start = ((f32[64,7,1024]{2,1,0:T(8,128)}), f32[64,7,1024]{2,1,0:T(8,128)S(1)}, u32[]{:S(2)}, u32[]{:S(2)}) async-start(f32[64,7,1024]{2,1,0:T(8,128)} %bitcast.53), calls=%async_computation | async-start | bytes 4194304 | tf_op jit(solution)/shard_map/all_to_all | solution.py:45
  26.4 1.9 slice.33
  28.4 47.5 %all-to-all-done = f32[64,7,1024]{2,1,0:T(8,128)S(1)} async-done(((f32[64,7,1024]{2,1,0:T(8,128)}), f32[64,7,1024]{2,1,0:T(8,128)S(1)}, u32[]{:S(2)}, u32[]{:S(2)}) %all-to-all-start) | async-done | bytes 1835040 | tf_op jit(solution)/shard_map/all_to_all | solution.py:45
  75.9 7.3 %fusion = f32[32,2,7,1152]{3,0,2,1:T(8,128)S(1)} fusion(f32[1024,1152]{1,0:T(8,128)} %all-gather.8.cloned.1.call-done, f32[32,2,7,1024]{3,2,1,0:T(8,128)S(1)} %bitcast.50), kind=kOutput, calls=%fused_computation.4 | convolution fusion | flops 3170893824 | bytes 8617984 | tf_op jit(solution)/shard_map/dot_general | solution.py:65
  83.2 1.3 copy-done.1
  84.6 1.0 dynamic-slice_bitcast_fusion
  85.6 2.4 %collective-permute-start = (f32[32,7,1152]{2,0,1:T(8,128)}, f32[32,7,1152]{2,0,1:T(8,128)S(1)}, u32[]{:S(2)}, u32[]{:S(2)}) collective-permute-start(f32[32,7,1152]{2,0,1:T(8,128)} %dynamic-slice_bitcast_fusion), channel_id=1, source_target_pairs={{0,1},{1,0},{2,3},{3,2},{4,5},{5,4},{6,7},{7,6},{8,9},{9,8},{10,11... | collective-permute-start | bytes 3096584 | tf_op jit(solution)/shard_map/ppermute | solution.py:69
  88.0 1.8 slice.32
  90.1 0.9 constant_dynamic-slice_fusion
  91.0 1.6 select_reduce_fusion
  92.6 16.9 %collective-permute-done = f32[32,7,1152]{2,0,1:T(8,128)S(1)} collective-permute-done((f32[32,7,1152]{2,0,1:T(8,128)}, f32[32,7,1152]{2,0,1:T(8,128)S(1)}, u32[]{:S(2)}, u32[]{:S(2)}) %collective-permute-start) | collective-permute-done | bytes 1032224 | tf_op jit(solution)/shard_map/ppermute | solution.py:69
  109.5 1.5 subtract_divide_fusion
  110.9 1.6 copy.49
  112.6 8.7 %all-to-all-start.1 = ((f32[32,7,1152]{2,1,0:T(8,128)}), f32[32,7,1152]{2,1,0:T(8,128)S(1)}, u32[]{:S(2)}, u32[]{:S(2)}) async-start(f32[32,7,1152]{2,1,0:T(8,128)} %copy.49), calls=%async_computation.1 | async-start | bytes 2359296 | tf_op jit(solution)/shard_map/all_to_all | solution.py:71
  121.3 4.1 %fusion.2 = f32[32,2,7,512]{3,0,2,1:T(8,128)S(1)} fusion(f32[1024,512]{1,0:T(8,128)} %all-gather.6.cloned.1.call-done, f32[32,2,7,1024]{3,2,1,0:T(8,128)S(1)} %bitcast.51), kind=kOutput, calls=%fused_computation.11 | convolution fusion | flops 1409286144 | bytes 4849664 | tf_op jit(solution)/shard_map/dot_general | solution.py:65
  125.5 2.3 %collective-permute-start.1 = (f32[32,7,512]{2,0,1:T(8,128)S(1)}, f32[32,7,512]{2,0,1:T(8,128)S(1)}, u32[]{:S(2)}, u32[]{:S(2)}) collective-permute-start(f32[32,7,512]{2,0,1:T(8,128)S(1)} %dynamic-slice_bitcast_fusion.1), channel_id=1, source_target_pairs={{0,1},{1,0},{2,3},{3,2},{4,5},{5,4},{6,7},{7,6},{8,9},{9,8},{10,11... | collective-permute-start | bytes 1376264 | tf_op jit(solution)/shard_map/ppermute | solution.py:69
  127.8 21.3 %collective-permute-done.1 = f32[32,7,512]{2,0,1:T(8,128)S(1)} collective-permute-done((f32[32,7,512]{2,0,1:T(8,128)S(1)}, f32[32,7,512]{2,0,1:T(8,128)S(1)}, u32[]{:S(2)}, u32[]{:S(2)}) %collective-permute-start.1) | collective-permute-done | bytes 458784 | tf_op jit(solution)/shard_map/ppermute | solution.py:69
  149.1 0.9 subtract_divide_fusion.1
  150.0 2.1 copy.51
  152.1 6.7 %all-to-all-start.2 = ((f32[32,7,512]{2,1,0:T(8,128)}), f32[32,7,512]{2,1,0:T(8,128)}, u32[]{:S(2)}, u32[]{:S(2)}) async-start(f32[32,7,512]{2,1,0:T(8,128)} %copy.51), calls=%async_computation.2 | async-start | bytes 1048576 | tf_op jit(solution)/shard_map/all_to_all | solution.py:71
  158.9 3.8 %fusion.4 = f32[32,2,7,384]{3,0,2,1:T(8,128)S(1)} fusion(f32[1024,384]{1,0:T(8,128)} %all-gather.4.cloned.1.call-done, f32[32,2,7,1024]{3,2,1,0:T(8,128)S(1)} %bitcast.52), kind=kOutput, calls=%fused_computation.13 | convolution fusion | flops 1056964608 | bytes 4096000 | tf_op jit(solution)/shard_map/dot_general | solution.py:65
  162.7 2.2 %collective-permute-start.2 = (f32[32,7,384]{2,0,1:T(8,128)S(1)}, f32[32,7,384]{2,0,1:T(8,128)S(1)}, u32[]{:S(2)}, u32[]{:S(2)}) collective-permute-start(f32[32,7,384]{2,0,1:T(8,128)S(1)} %dynamic-slice_bitcast_fusion.2), channel_id=1, source_target_pairs={{0,1},{1,0},{2,3},{3,2},{4,5},{5,4},{6,7},{7,6},{8,9},{9,8},{10,11... | collective-permute-start | bytes 1032200 | tf_op jit(solution)/shard_map/ppermute | solution.py:69
  164.9 12.3 %collective-permute-done.2 = f32[32,7,384]{2,0,1:T(8,128)S(1)} collective-permute-done((f32[32,7,384]{2,0,1:T(8,128)S(1)}, f32[32,7,384]{2,0,1:T(8,128)S(1)}, u32[]{:S(2)}, u32[]{:S(2)}) %collective-permute-start.2) | collective-permute-done | bytes 344096 | tf_op jit(solution)/shard_map/ppermute | solution.py:69
  177.6 21.6 %all_to_all.20 = f32[32,7,384]{2,1,0:T(8,128)S(1)} all-to-all(f32[32,7,384]{2,1,0:T(8,128)S(1)} %copy.54), channel_id=1, replica_groups=mesh['pair'=32,'gy'=4,'gx'=2] {'pair'}, dimensions={0} | all-to-all | bytes 688128 | tf_op jit(solution)/shard_map/all_to_all | solution.py:71
  199.2 1.3 pad_maximum_fusion
  200.5 3.1 %copy.55 = f32[1,7,65536]{2,0,1:T(1,128)} copy(f32[1,7,65536]{2,1,0:T(8,128)S(1)} %bitcast.54) | data formatting | bytes 3670016 | tf_op jit(solution)/shard_map/reshape | solution.py:73
  (45 shorter events, 1.1 us)
Async XLA Ops:
  6.5 2.5 %copy-start = (s32[16]{0:T(128)S(1)}, s32[16]{0:T(128)}, u32[]{:S(2)}) copy-start(s32[16]{0:T(128)} %param.13) | copy-start | bytes 196
  6.5 2.4 %copy-start.2 = (f32[1,7,2048]{2,0,1:T(1,128)S(1)}, f32[1,7,2048]{2,0,1:T(1,128)}, u32[]{:S(2)}) copy-start(f32[1,7,2048]{2,0,1:T(1,128)} %param.11) | copy-start | bytes 172036
  6.5 69.4 %all-gather.8.cloned.1.call-start = ((), (), s32[]{:S(2)}) async-start(), calls=%async_computation.6 | async-start | bytes 5898240 | tf_op jit(solution)/shard_map/all_gather | solution.py:60
  13.3 62.6 %all-to-all-start = ((f32[64,7,1024]{2,1,0:T(8,128)}), f32[64,7,1024]{2,1,0:T(8,128)S(1)}, u32[]{:S(2)}, u32[]{:S(2)}) async-start(f32[64,7,1024]{2,1,0:T(8,128)} %bitcast.53), calls=%async_computation | async-start | bytes 4194304 | tf_op jit(solution)/shard_map/all_to_all | solution.py:45
  26.3 95.0 %all-gather.6.cloned.1.call-start = ((), (), s32[]{:S(2)}) async-start(), calls=%async_computation.5 | async-start | bytes 2621440 | tf_op jit(solution)/shard_map/all_gather | solution.py:60
  28.3 121.7 %all-gather.4.cloned.1.call-start = ((), (), s32[]{:S(2)}) async-start(), calls=%async_computation.4 | async-start | bytes 1966080 | tf_op jit(solution)/shard_map/all_gather | solution.py:60
  83.2 1.3 copy-start.1
  84.6 5.2 %copy-start.4 = (s32[1,2,224]{2,1,0:T(2,128)S(1)}, s32[1,2,224]{2,1,0:T(2,128)}, u32[]{:S(2)}) copy-start(s32[1,2,224]{2,1,0:T(2,128)} %param.14) | copy-start | bytes 5380
  84.6 5.2 %copy-start.5 = (f32[64]{0:T(128)S(1)}, f32[64]{0:T(128)}, u32[]{:S(2)}) copy-start(f32[64]{0:T(128)} %param.16) | copy-start | bytes 772
  84.6 6.4 %copy-start.3 = (f32[512]{0:T(512)S(1)}, f32[512]{0:T(512)}, u32[]{:S(2)}) copy-start(f32[512]{0:T(512)} %param.17) | copy-start | bytes 6148
  85.6 23.9 %collective-permute-start = (f32[32,7,1152]{2,0,1:T(8,128)}, f32[32,7,1152]{2,0,1:T(8,128)S(1)}, u32[]{:S(2)}, u32[]{:S(2)}) collective-permute-start(f32[32,7,1152]{2,0,1:T(8,128)} %dynamic-slice_bitcast_fusion), channel_id=1, source_target_pairs={{0,1},{1,0},{2,3},{3,2},{4,5},{5,4},{6,7},{7,6},{8,9},{9,8},{10,11... | collective-permute-start | bytes 3096584 | tf_op jit(solution)/shard_map/ppermute | solution.py:69
  112.6 39.6 %all-to-all-start.1 = ((f32[32,7,1152]{2,1,0:T(8,128)}), f32[32,7,1152]{2,1,0:T(8,128)S(1)}, u32[]{:S(2)}, u32[]{:S(2)}) async-start(f32[32,7,1152]{2,1,0:T(8,128)} %copy.49), calls=%async_computation.1 | async-start | bytes 2359296 | tf_op jit(solution)/shard_map/all_to_all | solution.py:71
  125.5 23.6 %collective-permute-start.1 = (f32[32,7,512]{2,0,1:T(8,128)S(1)}, f32[32,7,512]{2,0,1:T(8,128)S(1)}, u32[]{:S(2)}, u32[]{:S(2)}) collective-permute-start(f32[32,7,512]{2,0,1:T(8,128)S(1)} %dynamic-slice_bitcast_fusion.1), channel_id=1, source_target_pairs={{0,1},{1,0},{2,3},{3,2},{4,5},{5,4},{6,7},{7,6},{8,9},{9,8},{10,11... | collective-permute-start | bytes 1376264 | tf_op jit(solution)/shard_map/ppermute | solution.py:69
  152.1 25.4 %all-to-all-start.2 = ((f32[32,7,512]{2,1,0:T(8,128)}), f32[32,7,512]{2,1,0:T(8,128)}, u32[]{:S(2)}, u32[]{:S(2)}) async-start(f32[32,7,512]{2,1,0:T(8,128)} %copy.51), calls=%async_computation.2 | async-start | bytes 1048576 | tf_op jit(solution)/shard_map/all_to_all | solution.py:71
  162.7 14.5 %collective-permute-start.2 = (f32[32,7,384]{2,0,1:T(8,128)S(1)}, f32[32,7,384]{2,0,1:T(8,128)S(1)}, u32[]{:S(2)}, u32[]{:S(2)}) collective-permute-start(f32[32,7,384]{2,0,1:T(8,128)S(1)} %dynamic-slice_bitcast_fusion.2), channel_id=1, source_target_pairs={{0,1},{1,0},{2,3},{3,2},{4,5},{5,4},{6,7},{7,6},{8,9},{9,8},{10,11... | collective-permute-start | bytes 1032200 | tf_op jit(solution)/shard_map/ppermute | solution.py:69
Sparse Core Ops, SparseCore 0:
  9.1 58.7 all-gather.7
  69.7 33.7 all-gather.5
  105.4 29.0 all-gather.3

commit v13 on v9

--- a/solution.py
+++ b/solution.py
@@ -61,7 +61,7 @@
         lo, hi = int(bounds[c]), int(bounds[c + 1])
         w = hi - lo
         piece = lax.all_gather(integrals[:, lo:hi], "gy", axis=0, tiled=True)
-        if c >= 1:
+        if c >= 2:
             piece, works[c - 1] = lax.optimization_barrier((piece, works[c - 1]))
         if c >= 2:
             piece, outs[c - 2] = lax.optimization_barrier((piece, outs[c - 2]))

time: 203 us -> 203 us (level)
  no operation moved by 1% of the time
where the time goes in v13:
time: 203 us; the launch traced here: 202 us
  waiting for transfers between devices  97.3 us (48%)
  starting transfers between devices  33 us (16%)
  blocking collectives  20.8 us (10%)
  local copies, waits for them, and re-layouts  19.8 us (10%)
  matrix products  14 us (7%)
  between operations  13.4 us (7%)
  other arithmetic  3.89 us (2%)
    ppermute x3, waiting for transfers between devices, on_device(): works.append(keep + lax.ppermute(send, 'gx', swap))  52.5 us
    all_to_all x1, waiting for transfers between devices, on_device(): t_all = lax.all_to_all(spread, 'pair', 0, 0, tiled=True)  42.6 us
    all_to_all x1, blocking collectives, on_device(): outs.append(lax.all_to_all(payload, 'pair', 0, 0, tiled=True))  20.8 us
    dot_general x3, matrix products, on_device(): jnp.dot(lhs, piece, precision=lax.Precision.HIGH, preferred_element_type=...  14 us
    all_to_all x1, starting transfers between devices, on_device(): t_all = lax.all_to_all(spread, 'pair', 0, 0, tiled=True)  11.6 us
    all_to_all x2, starting transfers between devices, on_device(): outs.append(lax.all_to_all(payload, 'pair', 0, 0, tiled=True))  10.4 us
    ppermute x3, starting transfers between devices, on_device(): works.append(keep + lax.ppermute(send, 'gx', swap))  7.32 us
    slice x3, local copies, waits for them, and re-layouts, on_device(): piece = lax.all_gather(integrals[:, lo:hi], 'gy', axis=0, tiled=True)  6.1 us
  transfers between devices with their start and end apart: 10, of which 5 were waited for; matrix products, arithmetic and copies ran while one was open for 15% of the time, Pallas kernels for 0%

profile of v13, /device:TPU:1, one launch (start us, length us, event | category | flops | bytes accessed | tf_op | source)
XLA Modules:
  0.0 202.3 jit_solution(14329600702897123212)
XLA Ops:
  6.5 2.4 %slice.34 = f32[256,1152]{1,0:T(8,128)} slice(f32[256,2048]{1,0:T(8,128)} %param.12), slice={[0:256], [0:1152]} | slice | bytes 2359296 | tf_op jit(solution)/shard_map/slice | solution.py:63
  9.1 0.6 gather_fusion.2
  9.7 0.6 gather_fusion.3
  10.4 3.6 %collective-permute-start = (f32[7,1024]{1,0:T(8,128)S(1)}, f32[7,1024]{1,0:T(8,128)S(1)}, u32[]{:S(2)}, u32[]{:S(2)}) collective-permute-start(f32[7,1024]{1,0:T(8,128)S(1)} %select_bitcast_fusion), channel_id=1, source_target_pairs={{0,1},{1,0},{2,3},{3,2},{4,5},{5,4},{6,7},{7,6},{8,9},{9,8},{10,11... | collective-permute-start | bytes 86024 | tf_op jit(solution)/shard_map/ppermute | solution.py:46
  14.0 0.6 gather_fusion
  14.7 0.6 gather_fusion.1
  15.4 1.7 broadcast_in_dim.45
  17.1 11.6 %all-to-all-start = ((f32[32,2,7,1024]{3,1,2,0:T(2,128)}), f32[32,2,7,1024]{3,1,2,0:T(2,128)S(1)}, u32[]{:S(2)}, u32[]{:S(2)}) async-start(f32[32,2,7,1024]{3,1,2,0:T(2,128)} %broadcast_in_dim.45), calls=%async_computation | async-start | bytes 3670016 | tf_op jit(solution)/shard_map/all_to_all | solution.py:49
  28.7 1.9 slice.33
  30.7 42.6 %all-to-all-done = f32[32,2,7,1024]{3,1,2,0:T(2,128)S(1)} async-done(((f32[32,2,7,1024]{3,1,2,0:T(2,128)}), f32[32,2,7,1024]{3,1,2,0:T(2,128)S(1)}, u32[]{:S(2)}, u32[]{:S(2)}) %all-to-all-start) | async-done | bytes 1835040 | tf_op jit(solution)/shard_map/all_to_all | solution.py:49
  73.3 6.9 %fusion = f32[32,2,7,1152]{3,0,2,1:T(8,128)S(1)} fusion(f32[1024,1152]{1,0:T(8,128)} %all-gather.8.cloned.1.call-done, f32[32,2,7,1024]{3,1,2,0:T(2,128)S(1)} %all-to-all-done), kind=kOutput, calls=%fused_computation.4 | convolution fusion | flops 3170893824 | bytes 8617984 | tf_op jit(solution)/shard_map/dot_general | solution.py:68
  80.2 1.3 copy-done.1
  81.5 1.0 dynamic-slice_bitcast_fusion
  82.5 2.5 %collective-permute-start.2 = (f32[32,7,1152]{2,0,1:T(8,128)}, f32[32,7,1152]{2,0,1:T(8,128)S(1)}, u32[]{:S(2)}, u32[]{:S(2)}) collective-permute-start(f32[32,7,1152]{2,0,1:T(8,128)} %dynamic-slice_bitcast_fusion), channel_id=1, source_target_pairs={{0,1},{1,0},{2,3},{3,2},{4,5},{5,4},{6,7},{7,6},{8,9},{9,8},{10,11... | collective-permute-start | bytes 3096584 | tf_op jit(solution)/shard_map/ppermute | solution.py:72
  85.0 1.8 slice.32
  87.1 0.9 constant_dynamic-slice_fusion
  88.0 1.6 select_reduce_fusion
  89.6 18.5 %collective-permute-done.2 = f32[32,7,1152]{2,0,1:T(8,128)S(1)} collective-permute-done((f32[32,7,1152]{2,0,1:T(8,128)}, f32[32,7,1152]{2,0,1:T(8,128)S(1)}, u32[]{:S(2)}, u32[]{:S(2)}) %collective-permute-start.2) | collective-permute-done | bytes 1032224 | tf_op jit(solution)/shard_map/ppermute | solution.py:72
  108.1 1.5 fusion.9
  109.6 1.6 copy.52
  111.2 5.5 %all-to-all-start.1 = ((f32[32,7,1152]{2,1,0:T(8,128)}), f32[32,7,1152]{2,1,0:T(8,128)S(1)}, u32[]{:S(2)}, u32[]{:S(2)}) async-start(f32[32,7,1152]{2,1,0:T(8,128)} %copy.52), calls=%async_computation.1 | async-start | bytes 2359296 | tf_op jit(solution)/shard_map/all_to_all | solution.py:74
  116.7 3.8 %fusion.2 = f32[32,2,7,512]{3,0,2,1:T(8,128)S(1)} fusion(f32[1024,512]{1,0:T(8,128)} %all-gather.6.cloned.1.call-done, f32[32,2,7,1024]{3,1,2,0:T(2,128)S(1)} %all-to-all-done), kind=kOutput, calls=%fused_computation.11 | convolution fusion | flops 1409286144 | bytes 4849664 | tf_op jit(solution)/shard_map/dot_general | solution.py:68
  120.6 2.7 %collective-permute-start.1 = (f32[32,7,512]{2,0,1:T(8,128)S(1)}, f32[32,7,512]{2,0,1:T(8,128)S(1)}, u32[]{:S(2)}, u32[]{:S(2)}) collective-permute-start(f32[32,7,512]{2,0,1:T(8,128)S(1)} %dynamic-slice_bitcast_fusion.1), channel_id=1, source_target_pairs={{0,1},{1,0},{2,3},{3,2},{4,5},{5,4},{6,7},{7,6},{8,9},{9,8},{10,11... | collective-permute-start | bytes 1376264 | tf_op jit(solution)/shard_map/ppermute | solution.py:72
  123.3 20.8 %collective-permute-done.1 = f32[32,7,512]{2,0,1:T(8,128)S(1)} collective-permute-done((f32[32,7,512]{2,0,1:T(8,128)S(1)}, f32[32,7,512]{2,0,1:T(8,128)S(1)}, u32[]{:S(2)}, u32[]{:S(2)}) %collective-permute-start.1) | collective-permute-done | bytes 458784 | tf_op jit(solution)/shard_map/ppermute | solution.py:72
  144.3 1.1 copy.54
  145.3 2.2 %all-to-all-done.1 = f32[32,7,1152]{2,1,0:T(8,128)S(1)} async-done(((f32[32,7,1152]{2,1,0:T(8,128)}), f32[32,7,1152]{2,1,0:T(8,128)S(1)}, u32[]{:S(2)}, u32[]{:S(2)}) %all-to-all-start.1) | async-done | bytes 1032224 | tf_op jit(solution)/shard_map/all_to_all | solution.py:74
  147.5 4.9 %all-to-all-start.2 = ((f32[32,7,512]{2,1,0:T(8,128)}), f32[32,7,512]{2,1,0:T(8,128)S(1)}, u32[]{:S(2)}, u32[]{:S(2)}) async-start(f32[32,7,512]{2,1,0:T(8,128)} %copy.54), calls=%async_computation.2 | async-start | bytes 1048576 | tf_op jit(solution)/shard_map/all_to_all | solution.py:74
  152.5 3.4 %fusion.4 = f32[32,2,7,384]{3,0,2,1:T(8,128)S(1)} fusion(f32[32,2,7,1024]{3,1,2,0:T(2,128)S(1)} %all-to-all-done, f32[1024,384]{1,0:T(8,128)} %all-gather.4.cloned.1.call-done), kind=kOutput, calls=%fused_computation.13 | convolution fusion | flops 1056964608 | bytes 4096000 | tf_op jit(solution)/shard_map/dot_general | solution.py:68
  155.9 2.2 %collective-permute-start.3 = (f32[32,7,384]{2,0,1:T(8,128)S(1)}, f32[32,7,384]{2,0,1:T(8,128)S(1)}, u32[]{:S(2)}, u32[]{:S(2)}) collective-permute-start(f32[32,7,384]{2,0,1:T(8,128)S(1)} %dynamic-slice_bitcast_fusion.2), channel_id=1, source_target_pairs={{0,1},{1,0},{2,3},{3,2},{4,5},{5,4},{6,7},{7,6},{8,9},{9,8},{10,11... | collective-permute-start | bytes 1032200 | tf_op jit(solution)/shard_map/ppermute | solution.py:72
  158.1 13.1 %collective-permute-done.3 = f32[32,7,384]{2,0,1:T(8,128)S(1)} collective-permute-done((f32[32,7,384]{2,0,1:T(8,128)S(1)}, f32[32,7,384]{2,0,1:T(8,128)S(1)}, u32[]{:S(2)}, u32[]{:S(2)}) %collective-permute-start.3) | collective-permute-done | bytes 344096 | tf_op jit(solution)/shard_map/ppermute | solution.py:72
  171.6 20.8 %all_to_all.20 = f32[32,7,384]{2,1,0:T(8,128)S(1)} all-to-all(f32[32,7,384]{2,1,0:T(8,128)S(1)} %copy.57), channel_id=1, replica_groups=mesh['pair'=32,'gy'=4,'gx'=2] {'pair'}, dimensions={0} | all-to-all | bytes 688128 | tf_op jit(solution)/shard_map/all_to_all | solution.py:74
  192.6 3.1 %copy.58 = f32[1,7,65536]{2,0,1:T(1,128)} copy(f32[1,7,65536]{2,1,0:T(8,128)S(1)} %bitcast.50) | data formatting | bytes 3670016 | tf_op jit(solution)/shard_map/reshape | solution.py:76
  (48 shorter events, 1.6 us)
Async XLA Ops:
  6.5 2.5 %copy-start = (s32[16]{0:T(128)S(1)}, s32[16]{0:T(128)}, u32[]{:S(2)}) copy-start(s32[16]{0:T(128)} %param.13) | copy-start | bytes 196
  6.5 2.4 %copy-start.2 = (f32[1,7,2048]{2,0,1:T(1,128)S(1)}, f32[1,7,2048]{2,0,1:T(1,128)}, u32[]{:S(2)}) copy-start(f32[1,7,2048]{2,0,1:T(1,128)} %param.11) | copy-start | bytes 172036
  6.5 66.8 %all-gather.8.cloned.1.call-start = ((), (), s32[]{:S(2)}) async-start(), calls=%async_computation.6 | async-start | bytes 5898240 | tf_op jit(solution)/shard_map/all_gather | solution.py:63
  10.4 4.9 %collective-permute-start = (f32[7,1024]{1,0:T(8,128)S(1)}, f32[7,1024]{1,0:T(8,128)S(1)}, u32[]{:S(2)}, u32[]{:S(2)}) collective-permute-start(f32[7,1024]{1,0:T(8,128)S(1)} %select_bitcast_fusion), channel_id=1, source_target_pairs={{0,1},{1,0},{2,3},{3,2},{4,5},{5,4},{6,7},{7,6},{8,9},{9,8},{10,11... | collective-permute-start | bytes 86024 | tf_op jit(solution)/shard_map/ppermute | solution.py:46
  17.1 56.2 %all-to-all-start = ((f32[32,2,7,1024]{3,1,2,0:T(2,128)}), f32[32,2,7,1024]{3,1,2,0:T(2,128)S(1)}, u32[]{:S(2)}, u32[]{:S(2)}) async-start(f32[32,2,7,1024]{3,1,2,0:T(2,128)} %broadcast_in_dim.45), calls=%async_computation | async-start | bytes 3670016 | tf_op jit(solution)/shard_map/all_to_all | solution.py:49
  28.7 88.0 %all-gather.6.cloned.1.call-start = ((), (), s32[]{:S(2)}) async-start(), calls=%async_computation.5 | async-start | bytes 2621440 | tf_op jit(solution)/shard_map/all_gather | solution.py:63
  30.7 113.6 %all-gather.4.cloned.1.call-start = ((), (), s32[]{:S(2)}) async-start(), calls=%async_computation.4 | async-start | bytes 1966080 | tf_op jit(solution)/shard_map/all_gather | solution.py:63
  80.2 1.3 copy-start.1
  81.5 5.3 %copy-start.4 = (s32[1,2,224]{2,1,0:T(2,128)S(1)}, s32[1,2,224]{2,1,0:T(2,128)}, u32[]{:S(2)}) copy-start(s32[1,2,224]{2,1,0:T(2,128)} %param.14) | copy-start | bytes 5380
  81.5 5.3 %copy-start.5 = (f32[64]{0:T(128)S(1)}, f32[64]{0:T(128)}, u32[]{:S(2)}) copy-start(f32[64]{0:T(128)} %param.16) | copy-start | bytes 772
  81.5 6.5 %copy-start.3 = (f32[512]{0:T(512)S(1)}, f32[512]{0:T(512)}, u32[]{:S(2)}) copy-start(f32[512]{0:T(512)} %param.17) | copy-start | bytes 6148
  82.5 25.6 %collective-permute-start.2 = (f32[32,7,1152]{2,0,1:T(8,128)}, f32[32,7,1152]{2,0,1:T(8,128)S(1)}, u32[]{:S(2)}, u32[]{:S(2)}) collective-permute-start(f32[32,7,1152]{2,0,1:T(8,128)} %dynamic-slice_bitcast_fusion), channel_id=1, source_target_pairs={{0,1},{1,0},{2,3},{3,2},{4,5},{5,4},{6,7},{7,6},{8,9},{9,8},{10,11... | collective-permute-start | bytes 3096584 | tf_op jit(solution)/shard_map/ppermute | solution.py:72
  111.2 36.4 %all-to-all-start.1 = ((f32[32,7,1152]{2,1,0:T(8,128)}), f32[32,7,1152]{2,1,0:T(8,128)S(1)}, u32[]{:S(2)}, u32[]{:S(2)}) async-start(f32[32,7,1152]{2,1,0:T(8,128)} %copy.52), calls=%async_computation.1 | async-start | bytes 2359296 | tf_op jit(solution)/shard_map/all_to_all | solution.py:74
  120.6 23.5 %collective-permute-start.1 = (f32[32,7,512]{2,0,1:T(8,128)S(1)}, f32[32,7,512]{2,0,1:T(8,128)S(1)}, u32[]{:S(2)}, u32[]{:S(2)}) collective-permute-start(f32[32,7,512]{2,0,1:T(8,128)S(1)} %dynamic-slice_bitcast_fusion.1), channel_id=1, source_target_pairs={{0,1},{1,0},{2,3},{3,2},{4,5},{5,4},{6,7},{7,6},{8,9},{9,8},{10,11... | collective-permute-start | bytes 1376264 | tf_op jit(solution)/shard_map/ppermute | solution.py:72
  147.5 24.0 %all-to-all-start.2 = ((f32[32,7,512]{2,1,0:T(8,128)}), f32[32,7,512]{2,1,0:T(8,128)S(1)}, u32[]{:S(2)}, u32[]{:S(2)}) async-start(f32[32,7,512]{2,1,0:T(8,128)} %copy.54), calls=%async_computation.2 | async-start | bytes 1048576 | tf_op jit(solution)/shard_map/all_to_all | solution.py:74
  155.9 15.3 %collective-permute-start.3 = (f32[32,7,384]{2,0,1:T(8,128)S(1)}, f32[32,7,384]{2,0,1:T(8,128)S(1)}, u32[]{:S(2)}, u32[]{:S(2)}) collective-permute-start(f32[32,7,384]{2,0,1:T(8,128)S(1)} %dynamic-slice_bitcast_fusion.2), channel_id=1, source_target_pairs={{0,1},{1,0},{2,3},{3,2},{4,5},{5,4},{6,7},{7,6},{8,9},{9,8},{10,11... | collective-permute-start | bytes 1032200 | tf_op jit(solution)/shard_map/ppermute | solution.py:72
Sparse Core Ops, SparseCore 0:
  9.1 58.7 all-gather.7
  69.7 33.7 all-gather.5
  105.4 29.0 all-gather.3
